TPU v7x, 256 devices: a whole 4x4x8 slice. The times are simulated.
256 devices in a mesh: ctx: 64 (over z, y, x_lo), tp: 4 (over x_hi, core).
Axes of the slice: x: 4 (x_hi: 2, x_lo: 2; x = x_hi * 2 + x_lo), y: 4, z: 8, core: 2. Of those that a mesh axis runs over, the one named last changes fastest.
Arguments:
- hidden_in: bfloat16 [8192, 4096], P('ctx', 'tp'), may hold values from -6 to 6
- w_query: bfloat16 [4096, 2048], P(None, 'tp'), may hold values from -8 to 8, as said below
- w_key: bfloat16 [4096, 2048], P(None, 'tp'), may hold values from -8 to 8, as said below
- w_value: bfloat16 [4096, 2048], P(None, 'tp'), may hold values from -0.09375 to 0.09375
- query_gain: float32 [2048], P('tp'), may hold values from 0.1 to 1.9
- key_gain: float32 [2048], P('tp'), may hold values from 0.1 to 1.9
- prompt_lengths: int32 [4], replicated, may hold values from 1 to 4096, 8192 in all
Outputs:
- attn_out: bfloat16 [8192, 2048], P('ctx', 'tp')
- key_cache: bfloat16 [8192, 2048], P('ctx', 'tp')
- value_cache: bfloat16 [8192, 2048], P('ctx', 'tp')
Inputs may be any that keep to these rules, and one draw needn't show every extreme that they name: `prompt_lengths`: lengths of the 4 prompts in order; they sum to 8192 and the longest holds exactly half of 8192. `w_query`: a projection matrix of 4096 rows. `w_key`: a projection matrix of 4096 rows.
All inputs are finite; a program needn't handle non-finite values.
Results may differ from a plain program's by a relative error of at most 0.0075.
Values may be sent and summed in bfloat16 or wider, within the bound.
No kernel may reach another device: no remote copies, remote signals or barrier semaphores. Data moves between devices by JAX's collectives and lax.ppermute only.
A program may use at most 128 MiB of HBM per device.

v0:
```python
import functools

import jax
import jax.numpy as jnp
from jax import lax
from jax.experimental import pallas as pl
from jax.experimental.pallas import tpu as pltpu
from jax.sharding import Mesh
from jax.sharding import PartitionSpec as P

HD = 128
KB = 256
CL = ("ylo", "xlo")
CTX = ("z", "yhi", "ylo", "xlo")
TP = ("xhi", "core")


def rotate(matrix, position):
    row_count, columns = matrix.shape
    head_count = columns // HD
    rot_half = HD // 2
    shaped = matrix.reshape(row_count, head_count, HD)
    inverse_freq = 500000.0 ** (-2.0 * jnp.arange(rot_half, dtype=jnp.float32) / HD)
    angles = position.astype(jnp.float32)[:, None] * inverse_freq[None, :]
    cosine = jnp.cos(angles)[:, None, :]
    sine_part = jnp.sin(angles)[:, None, :]
    first_part = shaped[..., :rot_half]
    second_part = shaped[..., rot_half:]
    turned = jnp.concatenate(
        [
            first_part * cosine - second_part * sine_part,
            second_part * cosine + first_part * sine_part,
        ],
        axis=-1,
    )
    return turned.reshape(row_count, columns).astype(jnp.bfloat16)


def request_start(token_ids, prompt_lengths):
    req_ends = jnp.cumsum(prompt_lengths)
    starts = req_ends - prompt_lengths
    request = jnp.sum((token_ids[:, None] >= req_ends[None, :]).astype(jnp.int32), axis=1)
    onehot = request[:, None] == jnp.arange(prompt_lengths.shape[0], dtype=jnp.int32)[None, :]
    return jnp.sum(jnp.where(onehot, starts[None, :], 0), axis=1)


def attn_kernel(info_ref, q_ref, kv_ref, qtok_ref, qlo_ref, o_ref):
    blk = pl.program_id(0)
    lo = info_ref[2 * blk]
    hi = info_ref[2 * blk + 1]
    shift = info_ref[4]
    groups = info_ref[5]
    nblocks = 2 * groups
    q = q_ref[...]
    qtok = qtok_ref[...]
    qlo = qlo_ref[...]
    rows = q.shape[0]
    scale = HD ** (-0.5)

    def body(kb, carry):
        peak, total, acc = carry
        upper = kb >= groups
        group = jnp.where(upper, nblocks - 1 - kb, kb)
        slot = (group - shift + groups) % groups
        start = pl.multiple_of((slot * 2 + upper.astype(jnp.int32)) * KB, KB)
        block = kv_ref[pl.ds(start, KB), :]
        keys = block[:, :HD]
        vals = block[:, HD:]
        scores = (
            lax.dot_general(q, keys, (((1,), (1,)), ((), ())), preferred_element_type=jnp.float32)
            * scale
        )
        ktok = kb * KB + lax.broadcasted_iota(jnp.int32, (1, KB), 1)
        visible = (ktok >= qlo) & (ktok <= qtok)
        masked = jnp.where(visible, scores, -1e30)
        new_peak = jnp.maximum(peak, jnp.max(masked, axis=1, keepdims=True))
        weights = jnp.where(visible, jnp.exp(masked - new_peak), 0.0)
        factor = jnp.exp(peak - new_peak)
        total = total * factor + jnp.sum(weights, axis=1, keepdims=True)
        acc = acc * factor + jnp.dot(
            weights.astype(jnp.bfloat16), vals, preferred_element_type=jnp.float32
        )
        return new_peak, total, acc

    start_state = (
        jnp.full((rows, 1), -1e30, jnp.float32),
        jnp.zeros((rows, 1), jnp.float32),
        jnp.zeros((rows, HD), jnp.float32),
    )
    _, total, acc = lax.fori_loop(lo, hi + 1, body, start_state)
    o_ref[...] = (acc / total).astype(o_ref.dtype)


def attention(info, q, kv, qtok, qlo):
    rows = q.shape[0]
    half = rows // 2
    return pl.pallas_call(
        attn_kernel,
        out_shape=jax.ShapeDtypeStruct((rows, HD), jnp.bfloat16),
        grid_spec=pltpu.PrefetchScalarGridSpec(
            num_scalar_prefetch=1,
            grid=(2,),
            in_specs=[
                pl.BlockSpec((half, HD), lambda i, info: (i, 0)),
                pl.BlockSpec(kv.shape, lambda i, info: (0, 0)),
                pl.BlockSpec((half, 1), lambda i, info: (i, 0)),
                pl.BlockSpec((half, 1), lambda i, info: (i, 0)),
            ],
            out_specs=pl.BlockSpec((half, HD), lambda i, info: (i, 0)),
        ),
    )(info, q, kv, qtok, qlo)


def z_ring(part, n):
    fwd = [part]
    bwd = [part]
    steps = n // 2
    for step in range(1, steps + 1):
        if step < steps:
            fwd.append(lax.ppermute(fwd[-1], "z", [(i, (i + 1) % n) for i in range(n)]))
            bwd.append(lax.ppermute(bwd[-1], "z", [(i, (i - 1) % n) for i in range(n)]))
        else:
            cut = part.shape[0] // 2
            far_a = lax.ppermute(fwd[-1][:cut], "z", [(i, (i + 1) % n) for i in range(n)])
            far_b = lax.ppermute(bwd[-1][cut:], "z", [(i, (i - 1) % n) for i in range(n)])
    ordered = bwd[: steps] + [far_a, far_b] + fwd[1:steps][::-1]
    return jnp.concatenate(ordered, axis=0)


def per_device(hidden_in, w_query, w_key, w_value, query_gain, key_gain, prompt_lengths):
    tok_rows = hidden_in.shape[0]
    half_rows = tok_rows // 2
    local_width = w_query.shape[1]
    head_count = local_width // HD
    nz = lax.axis_size("z")
    nyh = lax.axis_size("yhi")
    ncl = lax.axis_size("ylo") * lax.axis_size("xlo")
    z_idx = lax.axis_index("z")
    cg = z_idx * nyh + lax.axis_index("yhi")
    cl = lax.axis_index("ylo") * lax.axis_size("xlo") + lax.axis_index("xlo")
    groups = nz * nyh
    ctx_count = groups * ncl
    own = cg * ncl + cl

    xh = lax.axis_index("xhi")
    core = lax.axis_index("core")
    swap = [(0, 1), (1, 0)]
    across = lax.ppermute(hidden_in, "xhi", swap)
    pair = jnp.where(xh == 0, jnp.concatenate([hidden_in, across], axis=1), jnp.concatenate([across, hidden_in], axis=1))
    other = lax.ppermute(pair, "core", swap)
    width = hidden_in.shape[1]
    mine_first = jnp.concatenate([pair[:, :width], other[:, :width], pair[:, width:], other[:, width:]], axis=1)
    theirs_first = jnp.concatenate([other[:, :width], pair[:, :width], other[:, width:], pair[:, width:]], axis=1)
    pieces = jnp.where(core == 0, mine_first, theirs_first)
    queries = jnp.dot(pieces, w_query, preferred_element_type=jnp.float32)
    keys_proj = jnp.dot(pieces, w_key, preferred_element_type=jnp.float32)
    values = jnp.dot(pieces, w_value, preferred_element_type=jnp.float32).astype(jnp.bfloat16)
    squares = jnp.stack([jnp.sum(queries * queries, axis=1), jnp.sum(keys_proj * keys_proj, axis=1)])
    squares = squares + lax.ppermute(squares, "xhi", swap)
    squares = squares + lax.ppermute(squares, "core", swap)
    query_sq = squares[0]
    key_sq = squares[1]
    full_width = local_width * lax.axis_size("xhi") * lax.axis_size("core")
    query_normed = queries * lax.rsqrt(query_sq[:, None] / full_width + 1e-06) * query_gain
    key_normed = keys_proj * lax.rsqrt(key_sq[:, None] / full_width + 1e-06) * key_gain
    local_rows = jnp.arange(tok_rows, dtype=jnp.int32)
    block_of = jnp.where(local_rows < half_rows, own, 2 * ctx_count - 1 - own)
    token_ids = block_of * half_rows + local_rows % half_rows
    position = token_ids - request_start(token_ids, prompt_lengths)
    query_rot = rotate(query_normed, position)
    key_rot = rotate(key_normed, position)

    packed = jnp.concatenate(
        [
            query_rot.reshape(tok_rows, head_count, HD),
            key_rot.reshape(tok_rows, head_count, HD),
            values.reshape(tok_rows, head_count, HD),
        ],
        axis=2,
    )
    got = lax.all_to_all(packed, CL, split_axis=1, concat_axis=0, tiled=True)
    got = got.reshape(ncl, tok_rows, 3 * HD)
    lower = got[:, :half_rows].reshape(ncl * half_rows, 3 * HD)
    upper = got[::-1, half_rows:].reshape(ncl * half_rows, 3 * HD)
    mine = jnp.concatenate([lower, upper], axis=0)
    q_head = mine[:, :HD]
    kv_mine = mine[:, HD:]

    yh = lax.axis_index("yhi")
    kv_other = lax.ppermute(kv_mine, "yhi", swap)
    kv_pair = jnp.where(yh == 0, jnp.concatenate([kv_mine, kv_other], axis=0), jnp.concatenate([kv_other, kv_mine], axis=0))
    kv_all = z_ring(kv_pair, nz)

    span = ncl * half_rows
    total_tokens = 2 * ctx_count * half_rows
    r = jnp.arange(span, dtype=jnp.int32)
    q_tokens = jnp.concatenate([cg * span + r, total_tokens - (cg + 1) * span + r])
    q_lo = request_start(q_tokens, prompt_lengths)
    info = jnp.stack(
        [
            q_lo[0] // KB,
            cg,
            q_lo[span] // KB,
            2 * groups - 1 - cg,
            (z_idx * nyh) % groups,
            jnp.asarray(groups, jnp.int32),
        ]
    ).astype(jnp.int32)
    out_head = attention(info, q_head, kv_all, q_tokens[:, None], q_lo[:, None])

    out_lower = out_head[:span].reshape(ncl, half_rows, HD)
    out_upper = out_head[span:].reshape(ncl, half_rows, HD)[::-1]
    out_send = jnp.stack([out_lower, out_upper], axis=1).reshape(ncl, tok_rows, HD)

    picked = kv_all.reshape(groups, 2, ncl, half_rows, 2 * HD)
    picked = lax.dynamic_slice_in_dim(picked, cg * ncl, ncl, axis=3)
    doubled = jnp.concatenate([picked, picked], axis=0)
    natural = lax.dynamic_slice_in_dim(doubled, (groups - (z_idx * nyh) % groups) % groups, groups, axis=0)
    cache_lower = natural[:, 0].reshape(groups * ncl, ncl, 2 * HD)
    cache_upper = natural[::-1, 1].reshape(groups * ncl, ncl, 2 * HD)
    cache = jnp.concatenate([cache_lower, cache_upper], axis=0).transpose(1, 0, 2)
    send = jnp.concatenate([out_send, cache], axis=2)
    recv = lax.all_to_all(send, CL, split_axis=0, concat_axis=0, tiled=True)
    recv = recv.transpose(1, 0, 2)
    attn_out = recv[:, :, :HD].reshape(tok_rows, local_width)
    key_cache = recv[:, :, HD : 2 * HD].reshape(tok_rows, local_width)
    value_cache = recv[:, :, 2 * HD :].reshape(tok_rows, local_width)
    return attn_out, key_cache, value_cache


def solution(mesh):
    ctx_size = mesh.shape["ctx"]
    tp_size = mesh.shape["tp"]
    nz = 8
    split = Mesh(
        mesh.devices.reshape(nz, 2, 2, ctx_size // (nz * 4), tp_size // 2, 2),
        ("z", "yhi", "ylo", "xlo", "xhi", "core"),
    )
    rows = P(CTX, TP)
    placed = (rows, P(None, TP), P(None, TP), P(None, TP), P(TP), P(TP), P())
    return jax.shard_map(
        per_device,
        mesh=split,
        in_specs=placed,
        out_specs=(rows, rows, rows),
        check_vma=False,
    )
```

profile of v0, /device:TPU:96, one launch (start us, length us, event | category | flops | bytes accessed | tf_op | source)
XLA Modules:
  0.0 122.8 jit_solution(2961310441464923419)
XLA Ops:
  0.6 3.1 %collective-permute-start = (bf16[128,1024]{1,0:T(8,128)(2,1)}, bf16[128,1024]{1,0:T(8,128)(2,1)S(1)}, u32[]{:S(2)}, u32[]{:S(2)}) collective-permute-start(bf16[128,1024]{1,0:T(8,128)(2,1)} %param.7), channel_id=1, source_target_pairs={{0,2},{2,0},{1,3},{3,1},{4,6},{6,4},{5,7},{7,5},{8,10},{10,8},{9,1... | collective-permute-start | bytes 786440 | tf_op jit(solution)/shard_map/ppermute | solution.py:148
  5.4 5.1 %collective-permute-done = bf16[128,1024]{1,0:T(8,128)(2,1)S(1)} collective-permute-done((bf16[128,1024]{1,0:T(8,128)(2,1)}, bf16[128,1024]{1,0:T(8,128)(2,1)S(1)}, u32[]{:S(2)}, u32[]{:S(2)}) %collective-permute-start) | collective-permute-done | bytes 262176 | tf_op jit(solution)/shard_map/ppermute | solution.py:148
  10.5 1.2 maximum_select_fusion.1
  11.8 1.8 %collective-permute-done.1 = bf16[128,2048]{1,0:T(8,128)(2,1)S(1)} collective-permute-done((bf16[128,2048]{1,0:T(8,128)(2,1)S(1)}, bf16[128,2048]{1,0:T(8,128)(2,1)S(1)}, u32[]{:S(2)}, u32[]{:S(2)}) %collective-permute-start.1) | collective-permute-done | bytes 524320 | tf_op jit(solution)/shard_map/ppermute | solution.py:150
  13.7 3.1 %multiply_reduce_fusion.1 = (f32[128]{0:T(128)S(1)}, f32[128,512]{1,0:T(8,128)S(1)}) fusion(bf16[4096,512]{1,0:T(8,128)(2,1)} %param.8, bf16[128,1024]{1,0:T(8,128)(2,1)S(1)} %get-tuple-element.18, bf16[128,1024]{1,0:T(8,128)(2,1)S(1)} %get-tuple-element.16, bf16[128,1024]{1,0:T(8,128)(2,1)S(1)} %get-tuple-element.17, ...), kind=kOutput, calls=%fused_computation.18 | convolution fusion | flops 545914752 | bytes 5505537 | tf_op jit(solution)/shard_map/dot_general | solution.py:155
  17.9 3.1 %collective-permute-start.2 = (f32[2,128]{1,0:T(2,128)S(1)}, f32[2,128]{1,0:T(2,128)S(1)}, u32[]{:S(2)}, u32[]{:S(2)}) collective-permute-start(f32[2,128]{1,0:T(2,128)S(1)} %pad_maximum_fusion.4), channel_id=1, source_target_pairs={{0,2},{2,0},{1,3},{3,1},{4,6},{6,4},{5,7},{7,5},{8,10},{10,8},{9,1... | collective-permute-start | bytes 3080 | tf_op jit(solution)/shard_map/ppermute | solution.py:159
  21.4 1.8 %collective-permute-done.2 = f32[2,128]{1,0:T(2,128)S(1)} collective-permute-done((f32[2,128]{1,0:T(2,128)S(1)}, f32[2,128]{1,0:T(2,128)S(1)}, u32[]{:S(2)}, u32[]{:S(2)}) %collective-permute-start.2) | collective-permute-done | bytes 1056 | tf_op jit(solution)/shard_map/ppermute | solution.py:159
  25.6 11.0 %all_to_all.20 = bf16[128,4,384]{2,0,1:T(8,128)(2,1)S(1)} all-to-all(bf16[128,4,384]{2,0,1:T(8,128)(2,1)S(1)} %concatenate.49), channel_id=1, replica_groups=mesh['z'=8,'yhi'=2,'ylo'=2,'xlo'=2,'xhi'=2,'core'=2] {'ylo','xlo'}, dimensions={1} | all-to-all | bytes 786432 | tf_op jit(solution)/shard_map/all_to_all | solution.py:181
  36.7 3.0 %collective-permute-start.4 = (bf16[512,256]{1,0:T(8,128)(2,1)S(1)}, bf16[512,256]{1,0:T(8,128)(2,1)S(1)}, u32[]{:S(2)}, u32[]{:S(2)}) collective-permute-start(bf16[512,256]{1,0:T(8,128)(2,1)S(1)} %pad_maximum_fusion.1), channel_id=1, source_target_pairs={{0,16},{16,0},{1,17},{17,1},{2,18},{18,2},{3,19},{19,3},{4,20},{20... | collective-permute-start | bytes 786440 | tf_op jit(solution)/shard_map/ppermute | solution.py:190
  39.7 5.3 %collective-permute-done.4 = bf16[512,256]{1,0:T(8,128)(2,1)S(1)} collective-permute-done((bf16[512,256]{1,0:T(8,128)(2,1)S(1)}, bf16[512,256]{1,0:T(8,128)(2,1)S(1)}, u32[]{:S(2)}, u32[]{:S(2)}) %collective-permute-start.4) | collective-permute-done | bytes 262176 | tf_op jit(solution)/shard_map/ppermute | solution.py:190
  45.0 0.9 constant_dynamic-update-slice_fusion.8
  45.9 3.1 %collective-permute-start.8 = (bf16[1024,256]{1,0:T(8,128)(2,1)S(1)}, bf16[1024,256]{1,0:T(8,128)(2,1)S(1)}, u32[]{:S(2)}, u32[]{:S(2)}) collective-permute-start(bf16[1024,256]{1,0:T(8,128)(2,1)S(1)} %get-tuple-element.10), channel_id=1, source_target_pairs={{0,32},{32,64},{64,96},{96,128},{128,160},{160,192},{192,224},{224... | collective-permute-start | bytes 1572872 | tf_op jit(solution)/shard_map/ppermute | solution.py:120
  49.0 9.0 %collective-permute-done.8 = bf16[1024,256]{1,0:T(8,128)(2,1)S(1)} collective-permute-done((bf16[1024,256]{1,0:T(8,128)(2,1)S(1)}, bf16[1024,256]{1,0:T(8,128)(2,1)S(1)}, u32[]{:S(2)}, u32[]{:S(2)}) %collective-permute-start.8) | collective-permute-done | bytes 524320 | tf_op jit(solution)/shard_map/ppermute | solution.py:120
  58.0 3.7 %collective-permute-start.9 = (bf16[1024,256]{1,0:T(8,128)(2,1)S(1)}, bf16[1024,256]{1,0:T(8,128)(2,1)S(1)}, u32[]{:S(2)}, u32[]{:S(2)}) collective-permute-start(bf16[1024,256]{1,0:T(8,128)(2,1)S(1)} %collective-permute-done.8), channel_id=1, source_target_pairs={{0,32},{32,64},{64,96},{96,128},{128,160},{160,192},{192,224},{224... | collective-permute-start | bytes 1572872 | tf_op jit(solution)/shard_map/ppermute | solution.py:120
  61.7 8.4 %collective-permute-done.9 = bf16[1024,256]{1,0:T(8,128)(2,1)S(1)} collective-permute-done((bf16[1024,256]{1,0:T(8,128)(2,1)S(1)}, bf16[1024,256]{1,0:T(8,128)(2,1)S(1)}, u32[]{:S(2)}, u32[]{:S(2)}) %collective-permute-start.9) | collective-permute-done | bytes 524320 | tf_op jit(solution)/shard_map/ppermute | solution.py:120
  70.1 3.7 %collective-permute-start.10 = (bf16[1024,256]{1,0:T(8,128)(2,1)S(1)}, bf16[1024,256]{1,0:T(8,128)(2,1)S(1)}, u32[]{:S(2)}, u32[]{:S(2)}) collective-permute-start(bf16[1024,256]{1,0:T(8,128)(2,1)S(1)} %collective-permute-done.9), channel_id=1, source_target_pairs={{0,32},{32,64},{64,96},{96,128},{128,160},{160,192},{192,224},{224... | collective-permute-start | bytes 1572872 | tf_op jit(solution)/shard_map/ppermute | solution.py:120
  82.8 3.5 %collective-permute-start.11 = (bf16[512,256]{1,0:T(8,128)(2,1)S(1)}, bf16[512,256]{1,0:T(8,128)(2,1)S(1)}, u32[]{:S(2)}, u32[]{:S(2)}) collective-permute-start(bf16[512,256]{1,0:T(8,128)(2,1)S(1)} %slice.114), channel_id=1, source_target_pairs={{0,32},{32,64},{64,96},{96,128},{128,160},{160,192},{192,224},{224... | collective-permute-start | bytes 786440 | tf_op jit(solution)/shard_map/ppermute | solution.py:124
  87.3 0.9 constant_dynamic-update-slice_fusion.6
  89.0 1.2 %collective-permute-done.11 = bf16[512,256]{1,0:T(8,128)(2,1)S(1)} collective-permute-done((bf16[512,256]{1,0:T(8,128)(2,1)S(1)}, bf16[512,256]{1,0:T(8,128)(2,1)S(1)}, u32[]{:S(2)}, u32[]{:S(2)}) %collective-permute-start.11) | collective-permute-done | bytes 262176 | tf_op jit(solution)/shard_map/ppermute | solution.py:124
  90.9 3.9 %collective-permute-done.12 = bf16[512,256]{1,0:T(8,128)(2,1)S(1)} collective-permute-done((bf16[512,256]{1,0:T(8,128)(2,1)S(1)}, bf16[512,256]{1,0:T(8,128)(2,1)S(1)}, u32[]{:S(2)}, u32[]{:S(2)}) %collective-permute-start.12) | collective-permute-done | bytes 262176 | tf_op jit(solution)/shard_map/ppermute | solution.py:125
  98.0 9.7 %shard_map.94 = bf16[512,128]{1,0:T(8,128)(2,1)} custom-call(s32[6]{0:T(128)} %stack.38.info_ref, bf16[512,128]{1,0:T(8,128)(2,1)} %pad_maximum_fusion.2.q_ref, bf16[8192,256]{1,0:T(8,128)(2,1)} %constant_dynamic-update-slice_fusion.kv_ref, s32[512,1]{1,0:T(8,128)} %copy.53.qtok_ref, s32[512,1]{1,0:T(8,128)} %copy.54.qlo_ref), custom_call_target="tpu_custom_call" | custom-call | tf_op jit(solution)/shard_map/pallas_call | solution.py:97
  107.7 0.9 fusion.14
  108.6 1.2 constant_dynamic-slice_fusion
  110.5 9.8 %all_to_all.21 = bf16[4,128,384]{2,1,0:T(8,128)(2,1)S(1)} all-to-all(bf16[4,128,384]{2,1,0:T(8,128)(2,1)S(1)} %pad_maximum_fusion), channel_id=1, replica_groups=mesh['z'=8,'yhi'=2,'ylo'=2,'xlo'=2,'xhi'=2,'core'=2] {'ylo','xlo'}, dimensions={0} | all-to-all | bytes 786432 | tf_op jit(solution)/shard_map/all_to_all | solution.py:223
  (78 shorter events, 18.4 us)
Async XLA Ops:
  0.6 9.8 %collective-permute-start = (bf16[128,1024]{1,0:T(8,128)(2,1)}, bf16[128,1024]{1,0:T(8,128)(2,1)S(1)}, u32[]{:S(2)}, u32[]{:S(2)}) collective-permute-start(bf16[128,1024]{1,0:T(8,128)(2,1)} %param.7), channel_id=1, source_target_pairs={{0,2},{2,0},{1,3},{3,1},{4,6},{6,4},{5,7},{7,5},{8,10},{10,8},{9,1... | collective-permute-start | bytes 786440 | tf_op jit(solution)/shard_map/ppermute | solution.py:148
  11.6 2.0 %collective-permute-start.1 = (bf16[128,2048]{1,0:T(8,128)(2,1)S(1)}, bf16[128,2048]{1,0:T(8,128)(2,1)S(1)}, u32[]{:S(2)}, u32[]{:S(2)}) collective-permute-start(bf16[128,2048]{1,0:T(8,128)(2,1)S(1)} %maximum_select_fusion.1), channel_id=1, source_target_pairs={{0,1},{1,0},{2,3},{3,2},{4,5},{5,4},{6,7},{7,6},{8,9},{9,8},{10,11... | collective-permute-start | bytes 1572872 | tf_op jit(solution)/shard_map/ppermute | solution.py:150
  13.7 3.5 %copy-start.2 = (bf16[4096,512]{1,0:T(8,128)(2,1)S(1)}, bf16[4096,512]{1,0:T(8,128)(2,1)}, u32[]{:S(2)}) copy-start(bf16[4096,512]{1,0:T(8,128)(2,1)} %param.9) | copy-start | bytes 12582916
  17.1 6.1 %copy-start.3 = (bf16[4096,512]{1,0:T(8,128)(2,1)S(1)}, bf16[4096,512]{1,0:T(8,128)(2,1)}, u32[]{:S(2)}) copy-start(bf16[4096,512]{1,0:T(8,128)(2,1)} %param.10) | copy-start | bytes 12582916
  17.9 5.2 %collective-permute-start.2 = (f32[2,128]{1,0:T(2,128)S(1)}, f32[2,128]{1,0:T(2,128)S(1)}, u32[]{:S(2)}, u32[]{:S(2)}) collective-permute-start(f32[2,128]{1,0:T(2,128)S(1)} %pad_maximum_fusion.4), channel_id=1, source_target_pairs={{0,2},{2,0},{1,3},{3,1},{4,6},{6,4},{5,7},{7,5},{8,10},{10,8},{9,1... | collective-permute-start | bytes 3080 | tf_op jit(solution)/shard_map/ppermute | solution.py:159
  23.1 1.3 %copy-start = (f32[512]{0:T(512)S(1)}, f32[512]{0:T(512)}, u32[]{:S(2)}) copy-start(f32[512]{0:T(512)} %param.12) | copy-start | bytes 6148
  23.1 1.3 %copy-start.1 = (f32[512]{0:T(512)S(1)}, f32[512]{0:T(512)}, u32[]{:S(2)}) copy-start(f32[512]{0:T(512)} %param.11) | copy-start | bytes 6148
  23.1 1.2 %collective-permute-start.3 = (f32[2,128]{1,0:T(2,128)S(1)}, f32[2,128]{1,0:T(2,128)S(1)}, u32[]{:S(2)}, u32[]{:S(2)}) collective-permute-start(f32[2,128]{1,0:T(2,128)S(1)} %fusion.4), channel_id=1, source_target_pairs={{0,1},{1,0},{2,3},{3,2},{4,5},{5,4},{6,7},{7,6},{8,9},{9,8},{10,11... | collective-permute-start | bytes 3080 | tf_op jit(solution)/shard_map/ppermute | solution.py:160
  36.7 8.3 %collective-permute-start.4 = (bf16[512,256]{1,0:T(8,128)(2,1)S(1)}, bf16[512,256]{1,0:T(8,128)(2,1)S(1)}, u32[]{:S(2)}, u32[]{:S(2)}) collective-permute-start(bf16[512,256]{1,0:T(8,128)(2,1)S(1)} %pad_maximum_fusion.1), channel_id=1, source_target_pairs={{0,16},{16,0},{1,17},{17,1},{2,18},{18,2},{3,19},{19,3},{4,20},{20... | collective-permute-start | bytes 786440 | tf_op jit(solution)/shard_map/ppermute | solution.py:190
  45.9 12.1 %collective-permute-start.8 = (bf16[1024,256]{1,0:T(8,128)(2,1)S(1)}, bf16[1024,256]{1,0:T(8,128)(2,1)S(1)}, u32[]{:S(2)}, u32[]{:S(2)}) collective-permute-start(bf16[1024,256]{1,0:T(8,128)(2,1)S(1)} %get-tuple-element.10), channel_id=1, source_target_pairs={{0,32},{32,64},{64,96},{96,128},{128,160},{160,192},{192,224},{224... | collective-permute-start | bytes 1572872 | tf_op jit(solution)/shard_map/ppermute | solution.py:120
  49.0 12.7 %collective-permute-start.5 = (bf16[1024,256]{1,0:T(8,128)(2,1)S(1)}, bf16[1024,256]{1,0:T(8,128)(2,1)S(1)}, u32[]{:S(2)}, u32[]{:S(2)}) collective-permute-start(bf16[1024,256]{1,0:T(8,128)(2,1)S(1)} %get-tuple-element.10), channel_id=1, source_target_pairs={{0,224},{32,0},{64,32},{96,64},{128,96},{160,128},{192,160},{224,1... | collective-permute-start | bytes 1572872 | tf_op jit(solution)/shard_map/ppermute | solution.py:121
  58.0 12.1 %collective-permute-start.9 = (bf16[1024,256]{1,0:T(8,128)(2,1)S(1)}, bf16[1024,256]{1,0:T(8,128)(2,1)S(1)}, u32[]{:S(2)}, u32[]{:S(2)}) collective-permute-start(bf16[1024,256]{1,0:T(8,128)(2,1)S(1)} %collective-permute-done.8), channel_id=1, source_target_pairs={{0,32},{32,64},{64,96},{96,128},{128,160},{160,192},{192,224},{224... | collective-permute-start | bytes 1572872 | tf_op jit(solution)/shard_map/ppermute | solution.py:120
  61.7 12.1 %collective-permute-start.6 = (bf16[1024,256]{1,0:T(8,128)(2,1)S(1)}, bf16[1024,256]{1,0:T(8,128)(2,1)S(1)}, u32[]{:S(2)}, u32[]{:S(2)}) collective-permute-start(bf16[1024,256]{1,0:T(8,128)(2,1)S(1)} %collective-permute-done.5), channel_id=1, source_target_pairs={{0,224},{32,0},{64,32},{96,64},{128,96},{160,128},{192,160},{224,1... | collective-permute-start | bytes 1572872 | tf_op jit(solution)/shard_map/ppermute | solution.py:121
  70.1 12.7 %collective-permute-start.10 = (bf16[1024,256]{1,0:T(8,128)(2,1)S(1)}, bf16[1024,256]{1,0:T(8,128)(2,1)S(1)}, u32[]{:S(2)}, u32[]{:S(2)}) collective-permute-start(bf16[1024,256]{1,0:T(8,128)(2,1)S(1)} %collective-permute-done.9), channel_id=1, source_target_pairs={{0,32},{32,64},{64,96},{96,128},{128,160},{160,192},{192,224},{224... | collective-permute-start | bytes 1572872 | tf_op jit(solution)/shard_map/ppermute | solution.py:120
  73.8 13.3 %collective-permute-start.7 = (bf16[1024,256]{1,0:T(8,128)(2,1)S(1)}, bf16[1024,256]{1,0:T(8,128)(2,1)S(1)}, u32[]{:S(2)}, u32[]{:S(2)}) collective-permute-start(bf16[1024,256]{1,0:T(8,128)(2,1)S(1)} %collective-permute-done.6), channel_id=1, source_target_pairs={{0,224},{32,0},{64,32},{96,64},{128,96},{160,128},{192,160},{224,1... | collective-permute-start | bytes 1572872 | tf_op jit(solution)/shard_map/ppermute | solution.py:121
  82.8 7.4 %collective-permute-start.11 = (bf16[512,256]{1,0:T(8,128)(2,1)S(1)}, bf16[512,256]{1,0:T(8,128)(2,1)S(1)}, u32[]{:S(2)}, u32[]{:S(2)}) collective-permute-start(bf16[512,256]{1,0:T(8,128)(2,1)S(1)} %slice.114), channel_id=1, source_target_pairs={{0,32},{32,64},{64,96},{96,128},{128,160},{160,192},{192,224},{224... | collective-permute-start | bytes 786440 | tf_op jit(solution)/shard_map/ppermute | solution.py:124
  87.2 7.7 %collective-permute-start.12 = (bf16[512,256]{1,0:T(8,128)(2,1)S(1)}, bf16[512,256]{1,0:T(8,128)(2,1)S(1)}, u32[]{:S(2)}, u32[]{:S(2)}) collective-permute-start(bf16[512,256]{1,0:T(8,128)(2,1)S(1)} %slice.115), channel_id=1, source_target_pairs={{0,224},{32,0},{64,32},{96,64},{128,96},{160,128},{192,160},{224,1... | collective-permute-start | bytes 786440 | tf_op jit(solution)/shard_map/ppermute | solution.py:125
where the time goes:
time: 125 us; the launch traced here: 123 us
  waiting for transfers between devices  36.8 us (29%)
  starting transfers between devices  23.6 us (19%)
  blocking collectives  20.8 us (17%)
  local copies, waits for them, and re-layouts  15.5 us (12%)
  Pallas kernels  9.66 us (8%)
  between operations  6.19 us (5%)
  other arithmetic  5.67 us (5%)
  matrix products  4.66 us (4%)
    ppermute x3, waiting for transfers between devices, z_ring(): fwd.append(lax.ppermute(fwd[-1], 'z', [(i, (i + 1) % n) for i in range(n)]))  17.3 us
    all_to_all x1, blocking collectives, per_device(): got = lax.all_to_all(packed, CL, split_axis=1, concat_axis=0, tiled=True)  11 us
    ppermute x3, starting transfers between devices, z_ring(): fwd.append(lax.ppermute(fwd[-1], 'z', [(i, (i + 1) % n) for i in range(n)]))  10.5 us
    all_to_all x1, blocking collectives, per_device(): recv = lax.all_to_all(send, CL, split_axis=0, concat_axis=0, tiled=True)  9.77 us
    pallas_call x1, Pallas kernels, attention(): pl.pallas_call(attn_kernel, out_shape=jax.ShapeDtypeStruct((rows, HD), jn...  9.66 us
    unnamed x18, local copies, waits for them, and re-layouts  8.27 us
    ppermute x1, waiting for transfers between devices, per_device(): kv_other = lax.ppermute(kv_mine, 'yhi', swap)  5.28 us
    ppermute x1, waiting for transfers between devices, per_device(): across = lax.ppermute(hidden_in, 'xhi', swap)  5.07 us
  transfers between devices with their start and end apart: 13, of which 9 were waited for; matrix products, arithmetic and copies ran while one was open for 8% of the time, Pallas kernels for 0%

commit v1 on v0

--- a/solution.py
+++ b/solution.py
@@ -44,87 +44,85 @@
     return jnp.sum(jnp.where(onehot, starts[None, :], 0), axis=1)
 
 
-def attn_kernel(info_ref, q_ref, kv_ref, qtok_ref, qlo_ref, o_ref):
+def part_kernel(nb, info_ref, q_ref, kv_ref, qtok_ref, qlo_ref, m_in, l_in, acc_in, m_out, l_out, acc_out):
     blk = pl.program_id(0)
-    lo = info_ref[2 * blk]
-    hi = info_ref[2 * blk + 1]
-    shift = info_ref[4]
-    groups = info_ref[5]
-    nblocks = 2 * groups
-    q = q_ref[...]
-    qtok = qtok_ref[...]
-    qlo = qlo_ref[...]
-    rows = q.shape[0]
+    lo = info_ref[nb + 2 * blk]
+    hi = info_ref[nb + 2 * blk + 1]
+    m_out[...] = m_in[...]
+    l_out[...] = l_in[...]
+    acc_out[...] = acc_in[...]
     scale = HD ** (-0.5)
-
-    def body(kb, carry):
-        peak, total, acc = carry
-        upper = kb >= groups
-        group = jnp.where(upper, nblocks - 1 - kb, kb)
-        slot = (group - shift + groups) % groups
-        start = pl.multiple_of((slot * 2 + upper.astype(jnp.int32)) * KB, KB)
-        block = kv_ref[pl.ds(start, KB), :]
-        keys = block[:, :HD]
-        vals = block[:, HD:]
-        scores = (
-            lax.dot_general(q, keys, (((1,), (1,)), ((), ())), preferred_element_type=jnp.float32)
-            * scale
-        )
-        ktok = kb * KB + lax.broadcasted_iota(jnp.int32, (1, KB), 1)
-        visible = (ktok >= qlo) & (ktok <= qtok)
-        masked = jnp.where(visible, scores, -1e30)
-        new_peak = jnp.maximum(peak, jnp.max(masked, axis=1, keepdims=True))
-        weights = jnp.where(visible, jnp.exp(masked - new_peak), 0.0)
-        factor = jnp.exp(peak - new_peak)
-        total = total * factor + jnp.sum(weights, axis=1, keepdims=True)
-        acc = acc * factor + jnp.dot(
-            weights.astype(jnp.bfloat16), vals, preferred_element_type=jnp.float32
-        )
-        return new_peak, total, acc
-
-    start_state = (
-        jnp.full((rows, 1), -1e30, jnp.float32),
-        jnp.zeros((rows, 1), jnp.float32),
-        jnp.zeros((rows, HD), jnp.float32),
-    )
-    _, total, acc = lax.fori_loop(lo, hi + 1, body, start_state)
-    o_ref[...] = (acc / total).astype(o_ref.dtype)
-
-
-def attention(info, q, kv, qtok, qlo):
+    for j in range(nb):
+        kb = info_ref[j]
+
+        @pl.when((kb >= lo) & (kb <= hi))
+        def _():
+            block = kv_ref[j * KB : (j + 1) * KB, :]
+            keys = block[:, :HD]
+            vals = block[:, HD:]
+            scores = (
+                lax.dot_general(q_ref[...], keys, (((1,), (1,)), ((), ())), preferred_element_type=jnp.float32)
+                * scale
+            )
+            ktok = kb * KB + lax.broadcasted_iota(jnp.int32, (1, KB), 1)
+            visible = (ktok >= qlo_ref[...]) & (ktok <= qtok_ref[...])
+            masked = jnp.where(visible, scores, -1e30)
+            peak = m_out[...]
+            new_peak = jnp.maximum(peak, jnp.max(masked, axis=1, keepdims=True))
+            weights = jnp.where(visible, jnp.exp(masked - new_peak), 0.0)
+            factor = jnp.exp(peak - new_peak)
+            l_out[...] = l_out[...] * factor + jnp.sum(weights, axis=1, keepdims=True)
+            acc_out[...] = acc_out[...] * factor + jnp.dot(
+                weights.astype(jnp.bfloat16), vals, preferred_element_type=jnp.float32
+            )
+            m_out[...] = new_peak
+
+
+def attend_part(info, q, kv, qtok, qlo, state):
     rows = q.shape[0]
     half = rows // 2
+    nb = kv.shape[0] // KB
+    row_spec = lambda width: pl.BlockSpec((half, width), lambda i, info: (i, 0))
     return pl.pallas_call(
-        attn_kernel,
-        out_shape=jax.ShapeDtypeStruct((rows, HD), jnp.bfloat16),
+        functools.partial(part_kernel, nb),
+        out_shape=(
+            jax.ShapeDtypeStruct((rows, 1), jnp.float32),
+            jax.ShapeDtypeStruct((rows, 1), jnp.float32),
+            jax.ShapeDtypeStruct((rows, HD), jnp.float32),
+        ),
         grid_spec=pltpu.PrefetchScalarGridSpec(
             num_scalar_prefetch=1,
             grid=(2,),
             in_specs=[
-                pl.BlockSpec((half, HD), lambda i, info: (i, 0)),
+                row_spec(HD),
                 pl.BlockSpec(kv.shape, lambda i, info: (0, 0)),
-                pl.BlockSpec((half, 1), lambda i, info: (i, 0)),
-                pl.BlockSpec((half, 1), lambda i, info: (i, 0)),
+                row_spec(1),
+                row_spec(1),
+                row_spec(1),
+                row_spec(1),
+                row_spec(HD),
             ],
-            out_specs=pl.BlockSpec((half, HD), lambda i, info: (i, 0)),
+            out_specs=(row_spec(1), row_spec(1), row_spec(HD)),
         ),
-    )(info, q, kv, qtok, qlo)
+    )(info, q, kv, qtok, qlo, *state)
 
 
 def z_ring(part, n):
     fwd = [part]
     bwd = [part]
     steps = n // 2
+    arrived = [(0, part)]
     for step in range(1, steps + 1):
         if step < steps:
+            bwd.append(lax.ppermute(bwd[-1], "z", [(i, (i - 1) % n) for i in range(n)]))
             fwd.append(lax.ppermute(fwd[-1], "z", [(i, (i + 1) % n) for i in range(n)]))
-            bwd.append(lax.ppermute(bwd[-1], "z", [(i, (i - 1) % n) for i in range(n)]))
+            arrived.append((step, bwd[-1]))
+            arrived.append((n - step, fwd[-1]))
         else:
             cut = part.shape[0] // 2
-            far_a = lax.ppermute(fwd[-1][:cut], "z", [(i, (i + 1) % n) for i in range(n)])
-            far_b = lax.ppermute(bwd[-1][cut:], "z", [(i, (i - 1) % n) for i in range(n)])
-    ordered = bwd[: steps] + [far_a, far_b] + fwd[1:steps][::-1]
-    return jnp.concatenate(ordered, axis=0)
+            arrived.append((steps, lax.ppermute(fwd[-1][:cut], "z", [(i, (i + 1) % n) for i in range(n)])))
+            arrived.append((steps, lax.ppermute(bwd[-1][cut:], "z", [(i, (i - 1) % n) for i in range(n)])))
+    return arrived
 
 
 def per_device(hidden_in, w_query, w_key, w_value, query_gain, key_gain, prompt_lengths):
@@ -189,31 +187,42 @@
     yh = lax.axis_index("yhi")
     kv_other = lax.ppermute(kv_mine, "yhi", swap)
     kv_pair = jnp.where(yh == 0, jnp.concatenate([kv_mine, kv_other], axis=0), jnp.concatenate([kv_other, kv_mine], axis=0))
-    kv_all = z_ring(kv_pair, nz)
+    arrived = z_ring(kv_pair, nz)
 
     span = ncl * half_rows
     total_tokens = 2 * ctx_count * half_rows
     r = jnp.arange(span, dtype=jnp.int32)
     q_tokens = jnp.concatenate([cg * span + r, total_tokens - (cg + 1) * span + r])
     q_lo = request_start(q_tokens, prompt_lengths)
-    info = jnp.stack(
-        [
-            q_lo[0] // KB,
-            cg,
-            q_lo[span] // KB,
-            2 * groups - 1 - cg,
-            (z_idx * nyh) % groups,
-            jnp.asarray(groups, jnp.int32),
-        ]
-    ).astype(jnp.int32)
-    out_head = attention(info, q_head, kv_all, q_tokens[:, None], q_lo[:, None])
+    bounds = jnp.stack([q_lo[0] // KB, cg, q_lo[span] // KB, 2 * groups - 1 - cg]).astype(jnp.int32)
+    rows_q = 2 * span
+    state = (
+        jnp.full((rows_q, 1), -1e30, jnp.float32),
+        jnp.zeros((rows_q, 1), jnp.float32),
+        jnp.zeros((rows_q, HD), jnp.float32),
+    )
+    picked_parts = {}
+    seen = {}
+    for dist, part in arrived:
+        first = seen.get(dist, 0)
+        chunks = part.shape[0] // span
+        seen[dist] = first + chunks // 2
+        ids = []
+        for j in range(chunks):
+            group_j = (2 * ((z_idx + dist) % nz) + first + j // 2) % groups
+            ids.append(group_j if j % 2 == 0 else 2 * groups - 1 - group_j)
+        info = jnp.concatenate([jnp.stack(ids).astype(jnp.int32), bounds])
+        state = attend_part(info, q_head, part, q_tokens[:, None], q_lo[:, None], state)
+        sub = part.reshape(chunks // 2, 2, ncl, half_rows, 2 * HD)
+        picked_parts.setdefault(dist, []).append(lax.dynamic_slice_in_dim(sub, cg * ncl, ncl, axis=3))
+    _, total, acc = state
+    out_head = (acc / total).astype(jnp.bfloat16)
 
     out_lower = out_head[:span].reshape(ncl, half_rows, HD)
     out_upper = out_head[span:].reshape(ncl, half_rows, HD)[::-1]
     out_send = jnp.stack([out_lower, out_upper], axis=1).reshape(ncl, tok_rows, HD)
 
-    picked = kv_all.reshape(groups, 2, ncl, half_rows, 2 * HD)
-    picked = lax.dynamic_slice_in_dim(picked, cg * ncl, ncl, axis=3)
+    picked = jnp.concatenate([p for dist in range(nz) for p in picked_parts[dist]], axis=0)
     doubled = jnp.concatenate([picked, picked], axis=0)
     natural = lax.dynamic_slice_in_dim(doubled, (groups - (z_idx * nyh) % groups) % groups, groups, axis=0)
     cache_lower = natural[:, 0].reshape(groups * ncl, ncl, 2 * HD)

time: 125 us -> 168 us (1.34)
  Pallas kernels: 9.66 us -> 40.9 us
  local copies, waits for them, and re-layouts: 15.5 us -> 31.2 us
  waiting for transfers between devices: 36.8 us -> 32.8 us
  starting transfers between devices: 23.6 us -> 21.3 us
    pallas_call x1 -> x9, Pallas kernels: 9.66 us -> 40.9 us  [attend_part(): pl.pallas_call(functools.partial(part_kernel, nb), out_shape=(jax.ShapeDt...]
    ppermute x3, waiting for transfers between devices: 0.01 us -> 18.4 us  [z_ring(): bwd.append(lax.ppermute(bwd[-1], 'z', [(i, (i - 1) % n) for i in range(n)]))]
    ppermute x3, waiting for transfers between devices: 17.3 us -> 0.01 us  [z_ring(): fwd.append(lax.ppermute(fwd[-1], 'z', [(i, (i + 1) % n) for i in range(n)]))]
    unnamed x18 -> x46, local copies, waits for them, and re-layouts: 8.27 us -> 18.9 us
    concatenate x1 -> x10, local copies, waits for them, and re-layouts: 0.82 us -> 6.39 us  [the longest x9 5.52 us: per_device(): info = jnp.concatenate([jnp.stack(ids).astype(jnp.int32), bounds])]
    ppermute x1, waiting for transfers between devices: 3.91 us -> 0.01 us  [z_ring(): lax.ppermute(bwd[-1][cut:], 'z', [(i, (i - 1) % n) for i in range(n)])]
    ppermute x1, starting transfers between devices: 3.48 us -> 1.04 us  [z_ring(): lax.ppermute(fwd[-1][:cut], 'z', [(i, (i + 1) % n) for i in range(n)])]
    broadcast_in_dim x1 -> x4, local copies, waits for them, and re-layouts: 0.86 us -> 3.07 us  [the longest x1 0.86 us: per_device(): q_lo[:, None]]
  transfers between devices with their start and end apart: 13 -> 13, of which waited for: 9 -> 7; matrix products, arithmetic and copies ran while one was open for 8% -> 11% of each run, Pallas kernels for 0% -> 22%
where the time goes in v1:
time: 168 us; the launch traced here: 165 us
  Pallas kernels  40.9 us (24%)
  waiting for transfers between devices  32.8 us (20%)
  local copies, waits for them, and re-layouts  31.2 us (19%)
  starting transfers between devices  21.3 us (13%)
  blocking collectives  21.1 us (13%)
  other arithmetic  6.84 us (4%)
  between operations  6.55 us (4%)
  matrix products  4.66 us (3%)
    pallas_call x9, Pallas kernels, attend_part(): pl.pallas_call(functools.partial(part_kernel, nb), out_shape=(jax.ShapeDt...  40.9 us
    unnamed x46, local copies, waits for them, and re-layouts  18.9 us
    ppermute x3, waiting for transfers between devices, z_ring(): bwd.append(lax.ppermute(bwd[-1], 'z', [(i, (i - 1) % n) for i in range(n)]))  18.4 us
    all_to_all x1, blocking collectives, per_device(): got = lax.all_to_all(packed, CL, split_axis=1, concat_axis=0, tiled=True)  11 us
    all_to_all x1, blocking collectives, per_device(): recv = lax.all_to_all(send, CL, split_axis=0, concat_axis=0, tiled=True)  10.1 us
    ppermute x3, starting transfers between devices, z_ring(): fwd.append(lax.ppermute(fwd[-1], 'z', [(i, (i + 1) % n) for i in range(n)]))  9.58 us
    concatenate x9, local copies, waits for them, and re-layouts, per_device(): info = jnp.concatenate([jnp.stack(ids).astype(jnp.int32), bounds])  5.52 us
    ppermute x1, waiting for transfers between devices, per_device(): kv_other = lax.ppermute(kv_mine, 'yhi', swap)  5.29 us
  transfers between devices with their start and end apart: 13, of which 7 were waited for; matrix products, arithmetic and copies ran while one was open for 11% of the time, Pallas kernels for 22%

profile of v1, /device:TPU:96, one launch (start us, length us, event | category | flops | bytes accessed | tf_op | source)
XLA Modules:
  0.0 165.3 jit_solution(14237495002912342680)
XLA Ops:
  0.6 3.1 %collective-permute-start = (bf16[128,1024]{1,0:T(8,128)(2,1)}, bf16[128,1024]{1,0:T(8,128)(2,1)S(1)}, u32[]{:S(2)}, u32[]{:S(2)}) collective-permute-start(bf16[128,1024]{1,0:T(8,128)(2,1)} %param.7), channel_id=1, source_target_pairs={{0,2},{2,0},{1,3},{3,1},{4,6},{6,4},{5,7},{7,5},{8,10},{10,8},{9,1... | collective-permute-start | bytes 786440 | tf_op jit(solution)/shard_map/ppermute | solution.py:146
  5.4 5.1 %collective-permute-done = bf16[128,1024]{1,0:T(8,128)(2,1)S(1)} collective-permute-done((bf16[128,1024]{1,0:T(8,128)(2,1)}, bf16[128,1024]{1,0:T(8,128)(2,1)S(1)}, u32[]{:S(2)}, u32[]{:S(2)}) %collective-permute-start) | collective-permute-done | bytes 262176 | tf_op jit(solution)/shard_map/ppermute | solution.py:146
  11.8 1.8 %collective-permute-done.1 = bf16[128,2048]{1,0:T(8,128)(2,1)S(1)} collective-permute-done((bf16[128,2048]{1,0:T(8,128)(2,1)S(1)}, bf16[128,2048]{1,0:T(8,128)(2,1)S(1)}, u32[]{:S(2)}, u32[]{:S(2)}) %collective-permute-start.1) | collective-permute-done | bytes 524320 | tf_op jit(solution)/shard_map/ppermute | solution.py:148
  13.7 3.1 %multiply_reduce_fusion.1 = (f32[128]{0:T(128)S(1)}, f32[128,512]{1,0:T(8,128)S(1)}) fusion(bf16[4096,512]{1,0:T(8,128)(2,1)} %param.8, bf16[128,1024]{1,0:T(8,128)(2,1)S(1)} %get-tuple-element.70, bf16[128,1024]{1,0:T(8,128)(2,1)S(1)} %get-tuple-element.68, bf16[128,1024]{1,0:T(8,128)(2,1)S(1)} %get-tuple-element.69, ...), kind=kOutput, calls=%fused_computation.16 | convolution fusion | flops 545914752 | bytes 5505537 | tf_op jit(solution)/shard_map/dot_general | solution.py:153
  18.0 3.1 %collective-permute-start.2 = (f32[2,128]{1,0:T(2,128)S(1)}, f32[2,128]{1,0:T(2,128)S(1)}, u32[]{:S(2)}, u32[]{:S(2)}) collective-permute-start(f32[2,128]{1,0:T(2,128)S(1)} %pad_maximum_fusion.4), channel_id=1, source_target_pairs={{0,2},{2,0},{1,3},{3,1},{4,6},{6,4},{5,7},{7,5},{8,10},{10,8},{9,1... | collective-permute-start | bytes 3080 | tf_op jit(solution)/shard_map/ppermute | solution.py:157
  21.4 1.7 %collective-permute-done.2 = f32[2,128]{1,0:T(2,128)S(1)} collective-permute-done((f32[2,128]{1,0:T(2,128)S(1)}, f32[2,128]{1,0:T(2,128)S(1)}, u32[]{:S(2)}, u32[]{:S(2)}) %collective-permute-start.2) | collective-permute-done | bytes 1056 | tf_op jit(solution)/shard_map/ppermute | solution.py:157
  25.6 11.0 %all_to_all.20 = bf16[128,4,384]{2,0,1:T(8,128)(2,1)S(1)} all-to-all(bf16[128,4,384]{2,0,1:T(8,128)(2,1)S(1)} %concatenate.85), channel_id=1, replica_groups=mesh['z'=8,'yhi'=2,'ylo'=2,'xlo'=2,'xhi'=2,'core'=2] {'ylo','xlo'}, dimensions={1} | all-to-all | bytes 786432 | tf_op jit(solution)/shard_map/all_to_all | solution.py:179
  36.7 3.0 %collective-permute-start.4 = (bf16[512,256]{1,0:T(8,128)(2,1)S(1)}, bf16[512,256]{1,0:T(8,128)(2,1)S(1)}, u32[]{:S(2)}, u32[]{:S(2)}) collective-permute-start(bf16[512,256]{1,0:T(8,128)(2,1)S(1)} %pad_maximum_fusion.1), channel_id=1, source_target_pairs={{0,16},{16,0},{1,17},{17,1},{2,18},{18,2},{3,19},{19,3},{4,20},{20... | collective-permute-start | bytes 786440 | tf_op jit(solution)/shard_map/ppermute | solution.py:188
  39.7 5.3 %collective-permute-done.4 = bf16[512,256]{1,0:T(8,128)(2,1)S(1)} collective-permute-done((bf16[512,256]{1,0:T(8,128)(2,1)S(1)}, bf16[512,256]{1,0:T(8,128)(2,1)S(1)}, u32[]{:S(2)}, u32[]{:S(2)}) %collective-permute-start.4) | collective-permute-done | bytes 262176 | tf_op jit(solution)/shard_map/ppermute | solution.py:188
  45.4 3.1 %collective-permute-start.9 = (bf16[1024,256]{1,0:T(8,128)(2,1)S(1)}, bf16[1024,256]{1,0:T(8,128)(2,1)S(1)}, u32[]{:S(2)}, u32[]{:S(2)}) collective-permute-start(bf16[1024,256]{1,0:T(8,128)(2,1)S(1)} %maximum_select_fusion.2.kv_ref), channel_id=1, source_target_pairs={{0,32},{32,64},{64,96},{96,128},{128,160},{160,192},{192,224},{224... | collective-permute-start | bytes 1572872 | tf_op jit(solution)/shard_map/ppermute | solution.py:118
  48.6 9.6 %collective-permute-done.5.kv_ref = bf16[1024,256]{1,0:T(8,128)(2,1)S(1)} collective-permute-done((bf16[1024,256]{1,0:T(8,128)(2,1)S(1)}, bf16[1024,256]{1,0:T(8,128)(2,1)S(1)}, u32[]{:S(2)}, u32[]{:S(2)}) %collective-permute-start.5) | collective-permute-done | bytes 524320 | tf_op jit(solution)/shard_map/ppermute | solution.py:117
  58.2 3.2 %collective-permute-start.10 = (bf16[1024,256]{1,0:T(8,128)(2,1)S(1)}, bf16[1024,256]{1,0:T(8,128)(2,1)S(1)}, u32[]{:S(2)}, u32[]{:S(2)}) collective-permute-start(bf16[1024,256]{1,0:T(8,128)(2,1)S(1)} %collective-permute-done.9.kv_ref), channel_id=1, source_target_pairs={{0,32},{32,64},{64,96},{96,128},{128,160},{160,192},{192,224},{224... | collective-permute-start | bytes 1572872 | tf_op jit(solution)/shard_map/ppermute | solution.py:118
  61.4 8.8 %collective-permute-done.6.kv_ref = bf16[1024,256]{1,0:T(8,128)(2,1)} collective-permute-done((bf16[1024,256]{1,0:T(8,128)(2,1)S(1)}, bf16[1024,256]{1,0:T(8,128)(2,1)}, u32[]{:S(2)}, u32[]{:S(2)}) %collective-permute-start.6) | collective-permute-done | bytes 524320 | tf_op jit(solution)/shard_map/ppermute | solution.py:117
  70.3 3.2 %collective-permute-start.11 = (bf16[1024,256]{1,0:T(8,128)(2,1)S(1)}, bf16[1024,256]{1,0:T(8,128)(2,1)S(1)}, u32[]{:S(2)}, u32[]{:S(2)}) collective-permute-start(bf16[1024,256]{1,0:T(8,128)(2,1)S(1)} %collective-permute-done.10.kv_ref), channel_id=1, source_target_pairs={{0,32},{32,64},{64,96},{96,128},{128,160},{160,192},{192,224},{224... | collective-permute-start | bytes 1572872 | tf_op jit(solution)/shard_map/ppermute | solution.py:118
  89.8 4.9 %shard_map.94 = (f32[512,1]{1,0:T(8,128)}, f32[512,1]{1,0:T(8,128)}, f32[512,128]{1,0:T(8,128)}) custom-call(s32[8]{0:T(128)} %concatenate.96.info_ref, bf16[512,128]{1,0:T(8,128)(2,1)} %pad_maximum_fusion.2.q_ref, bf16[1024,256]{1,0:T(8,128)(2,1)} %copy-done, s32[512,1]{1,0:T(8,128)} %copy.117.qtok_ref, s32[512,1]{1,0:T(8,128)} %copy.118.qlo_ref, ...), custom_call_target="tpu_custom_call" | custom-call | tf_op jit(solution)/shard_map/pallas_call | solution.py:86
  99.1 4.3 %shard_map.95 = (f32[512,1]{1,0:T(8,128)}, f32[512,1]{1,0:T(8,128)}, f32[512,128]{1,0:T(8,128)}) custom-call(s32[8]{0:T(128)} %concatenate.95.info_ref, bf16[512,128]{1,0:T(8,128)(2,1)} %pad_maximum_fusion.2.q_ref, bf16[1024,256]{1,0:T(8,128)(2,1)} %copy-done.4, s32[512,1]{1,0:T(8,128)} %copy.117.qtok_ref, s32[512,1]{1,0:T(8,128)} %copy.118.qlo_ref, ...), custom_call_target="tpu_custom_call" | custom-call | tf_op jit(solution)/shard_map/pallas_call | solution.py:86
  103.4 4.3 %shard_map.96 = (f32[512,1]{1,0:T(8,128)}, f32[512,1]{1,0:T(8,128)}, f32[512,128]{1,0:T(8,128)}) custom-call(s32[8]{0:T(128)} %concatenate.94.info_ref, bf16[512,128]{1,0:T(8,128)(2,1)} %pad_maximum_fusion.2.q_ref, bf16[1024,256]{1,0:T(8,128)(2,1)} %copy-done.3, s32[512,1]{1,0:T(8,128)} %copy.117.qtok_ref, s32[512,1]{1,0:T(8,128)} %copy.118.qlo_ref, ...), custom_call_target="tpu_custom_call" | custom-call | tf_op jit(solution)/shard_map/pallas_call | solution.py:86
  107.7 4.4 %shard_map.97 = (f32[512,1]{1,0:T(8,128)}, f32[512,1]{1,0:T(8,128)}, f32[512,128]{1,0:T(8,128)}) custom-call(s32[8]{0:T(128)} %concatenate.93.info_ref, bf16[512,128]{1,0:T(8,128)(2,1)} %pad_maximum_fusion.2.q_ref, bf16[1024,256]{1,0:T(8,128)(2,1)} %collective-permute-done.6.kv_ref, s32[512,1]{1,0:T(8,128)} %copy.117.qtok_ref, s32[512,1]{1,0:T(8,128)} %copy.118.qlo_ref, ...), custom_call_target="tpu_custom_call" | custom-call | tf_op jit(solution)/shard_map/pallas_call | solution.py:86
  112.2 4.3 %shard_map.98 = (f32[512,1]{1,0:T(8,128)}, f32[512,1]{1,0:T(8,128)}, f32[512,128]{1,0:T(8,128)}) custom-call(s32[8]{0:T(128)} %concatenate.92.info_ref, bf16[512,128]{1,0:T(8,128)(2,1)} %pad_maximum_fusion.2.q_ref, bf16[1024,256]{1,0:T(8,128)(2,1)} %copy-done.5, s32[512,1]{1,0:T(8,128)} %copy.117.qtok_ref, s32[512,1]{1,0:T(8,128)} %copy.118.qlo_ref, ...), custom_call_target="tpu_custom_call" | custom-call | tf_op jit(solution)/shard_map/pallas_call | solution.py:86
  117.4 5.5 %shard_map.99 = (f32[512,1]{1,0:T(8,128)}, f32[512,1]{1,0:T(8,128)}, f32[512,128]{1,0:T(8,128)}) custom-call(s32[8]{0:T(128)} %concatenate.91.info_ref, bf16[512,128]{1,0:T(8,128)(2,1)} %pad_maximum_fusion.2.q_ref, bf16[1024,256]{1,0:T(8,128)(2,1)} %copy-done.2, s32[512,1]{1,0:T(8,128)} %copy.117.qtok_ref, s32[512,1]{1,0:T(8,128)} %copy.118.qlo_ref, ...), custom_call_target="tpu_custom_call" | custom-call | tf_op jit(solution)/shard_map/pallas_call | solution.py:86
  122.9 4.3 %shard_map.100 = (f32[512,1]{1,0:T(8,128)}, f32[512,1]{1,0:T(8,128)}, f32[512,128]{1,0:T(8,128)}) custom-call(s32[8]{0:T(128)} %concatenate.90.info_ref, bf16[512,128]{1,0:T(8,128)(2,1)} %pad_maximum_fusion.2.q_ref, bf16[1024,256]{1,0:T(8,128)(2,1)} %copy-done.1, s32[512,1]{1,0:T(8,128)} %copy.117.qtok_ref, s32[512,1]{1,0:T(8,128)} %copy.118.qlo_ref, ...), custom_call_target="tpu_custom_call" | custom-call | tf_op jit(solution)/shard_map/pallas_call | solution.py:86
  128.8 4.2 %shard_map.101 = (f32[512,1]{1,0:T(8,128)}, f32[512,1]{1,0:T(8,128)}, f32[512,128]{1,0:T(8,128)}) custom-call(s32[6]{0:T(128)} %concatenate.89.info_ref, bf16[512,128]{1,0:T(8,128)(2,1)} %pad_maximum_fusion.2.q_ref, bf16[512,256]{1,0:T(8,128)(2,1)} %copy-done.6, s32[512,1]{1,0:T(8,128)} %copy.117.qtok_ref, s32[512,1]{1,0:T(8,128)} %copy.118.qlo_ref, ...), custom_call_target="tpu_custom_call" | custom-call | tf_op jit(solution)/shard_map/pallas_call | solution.py:86
  133.8 4.4 %shard_map.102 = (f32[512,1]{1,0:T(8,128)}, f32[512,1]{1,0:T(8,128)}, f32[512,128]{1,0:T(8,128)}) custom-call(s32[6]{0:T(128)} %concatenate.80.info_ref, bf16[512,128]{1,0:T(8,128)(2,1)} %pad_maximum_fusion.2.q_ref, bf16[512,256]{1,0:T(8,128)(2,1)} %copy-done.7, s32[512,1]{1,0:T(8,128)} %copy.117.qtok_ref, s32[512,1]{1,0:T(8,128)} %copy.118.qlo_ref, ...), custom_call_target="tpu_custom_call" | custom-call | tf_op jit(solution)/shard_map/pallas_call | solution.py:86
  152.6 10.1 %all_to_all.21 = bf16[4,128,384]{2,1,0:T(8,128)(2,1)S(1)} all-to-all(bf16[4,128,384]{2,1,0:T(8,128)(2,1)S(1)} %pad_maximum_fusion), channel_id=1, replica_groups=mesh['z'=8,'yhi'=2,'ylo'=2,'xlo'=2,'xhi'=2,'core'=2] {'ylo','xlo'}, dimensions={0} | all-to-all | bytes 786432 | tf_op jit(solution)/shard_map/all_to_all | solution.py:232
  (125 shorter events, 42.5 us)
Async XLA Ops:
  0.6 9.8 %collective-permute-start = (bf16[128,1024]{1,0:T(8,128)(2,1)}, bf16[128,1024]{1,0:T(8,128)(2,1)S(1)}, u32[]{:S(2)}, u32[]{:S(2)}) collective-permute-start(bf16[128,1024]{1,0:T(8,128)(2,1)} %param.7), channel_id=1, source_target_pairs={{0,2},{2,0},{1,3},{3,1},{4,6},{6,4},{5,7},{7,5},{8,10},{10,8},{9,1... | collective-permute-start | bytes 786440 | tf_op jit(solution)/shard_map/ppermute | solution.py:146
  11.7 2.0 %collective-permute-start.1 = (bf16[128,2048]{1,0:T(8,128)(2,1)S(1)}, bf16[128,2048]{1,0:T(8,128)(2,1)S(1)}, u32[]{:S(2)}, u32[]{:S(2)}) collective-permute-start(bf16[128,2048]{1,0:T(8,128)(2,1)S(1)} %maximum_select_fusion.1), channel_id=1, source_target_pairs={{0,1},{1,0},{2,3},{3,2},{4,5},{5,4},{6,7},{7,6},{8,9},{9,8},{10,11... | collective-permute-start | bytes 1572872 | tf_op jit(solution)/shard_map/ppermute | solution.py:148
  13.7 3.5 %copy-start.11 = (bf16[4096,512]{1,0:T(8,128)(2,1)S(1)}, bf16[4096,512]{1,0:T(8,128)(2,1)}, u32[]{:S(2)}) copy-start(bf16[4096,512]{1,0:T(8,128)(2,1)} %param.9) | copy-start | bytes 12582916
  17.2 6.1 %copy-start.12 = (bf16[4096,512]{1,0:T(8,128)(2,1)S(1)}, bf16[4096,512]{1,0:T(8,128)(2,1)}, u32[]{:S(2)}) copy-start(bf16[4096,512]{1,0:T(8,128)(2,1)} %param.10) | copy-start | bytes 12582916
  18.0 5.2 %collective-permute-start.2 = (f32[2,128]{1,0:T(2,128)S(1)}, f32[2,128]{1,0:T(2,128)S(1)}, u32[]{:S(2)}, u32[]{:S(2)}) collective-permute-start(f32[2,128]{1,0:T(2,128)S(1)} %pad_maximum_fusion.4), channel_id=1, source_target_pairs={{0,2},{2,0},{1,3},{3,1},{4,6},{6,4},{5,7},{7,5},{8,10},{10,8},{9,1... | collective-permute-start | bytes 3080 | tf_op jit(solution)/shard_map/ppermute | solution.py:157
  23.1 1.3 copy-start.9
  23.2 1.3 copy-start.10
  23.2 1.2 collective-permute-start.3
  36.7 8.3 %collective-permute-start.4 = (bf16[512,256]{1,0:T(8,128)(2,1)S(1)}, bf16[512,256]{1,0:T(8,128)(2,1)S(1)}, u32[]{:S(2)}, u32[]{:S(2)}) collective-permute-start(bf16[512,256]{1,0:T(8,128)(2,1)S(1)} %pad_maximum_fusion.1), channel_id=1, source_target_pairs={{0,16},{16,0},{1,17},{17,1},{2,18},{18,2},{3,19},{19,3},{4,20},{20... | collective-permute-start | bytes 786440 | tf_op jit(solution)/shard_map/ppermute | solution.py:188
  45.2 44.6 %copy-start = (bf16[1024,256]{1,0:T(8,128)(2,1)}, bf16[1024,256]{1,0:T(8,128)(2,1)S(1)}, u32[]{:S(2)}) copy-start(bf16[1024,256]{1,0:T(8,128)(2,1)S(1)} %maximum_select_fusion.2.kv_ref) | copy-start | bytes 1572868
  45.2 12.9 %collective-permute-start.5 = (bf16[1024,256]{1,0:T(8,128)(2,1)S(1)}, bf16[1024,256]{1,0:T(8,128)(2,1)S(1)}, u32[]{:S(2)}, u32[]{:S(2)}) collective-permute-start(bf16[1024,256]{1,0:T(8,128)(2,1)S(1)} %maximum_select_fusion.2.kv_ref), channel_id=1, source_target_pairs={{0,224},{32,0},{64,32},{96,64},{128,96},{160,128},{192,160},{224,1... | collective-permute-start | bytes 1572872 | tf_op jit(solution)/shard_map/ppermute | solution.py:117
  45.4 12.7 %collective-permute-start.9 = (bf16[1024,256]{1,0:T(8,128)(2,1)S(1)}, bf16[1024,256]{1,0:T(8,128)(2,1)S(1)}, u32[]{:S(2)}, u32[]{:S(2)}) collective-permute-start(bf16[1024,256]{1,0:T(8,128)(2,1)S(1)} %maximum_select_fusion.2.kv_ref), channel_id=1, source_target_pairs={{0,32},{32,64},{64,96},{96,128},{128,160},{160,192},{192,224},{224... | collective-permute-start | bytes 1572872 | tf_op jit(solution)/shard_map/ppermute | solution.py:118
  58.2 40.3 %copy-start.4 = (bf16[1024,256]{1,0:T(8,128)(2,1)}, bf16[1024,256]{1,0:T(8,128)(2,1)S(1)}, u32[]{:S(2)}) copy-start(bf16[1024,256]{1,0:T(8,128)(2,1)S(1)} %collective-permute-done.5.kv_ref) | copy-start | bytes 1572868
  58.2 12.1 %collective-permute-start.6 = (bf16[1024,256]{1,0:T(8,128)(2,1)S(1)}, bf16[1024,256]{1,0:T(8,128)(2,1)}, u32[]{:S(2)}, u32[]{:S(2)}) collective-permute-start(bf16[1024,256]{1,0:T(8,128)(2,1)S(1)} %collective-permute-done.5.kv_ref), channel_id=1, source_target_pairs={{0,224},{32,0},{64,32},{96,64},{128,96},{160,128},{192,160},{224,1... | collective-permute-start | bytes 1572872 | tf_op jit(solution)/shard_map/ppermute | solution.py:117
  58.2 36.6 %copy-start.3 = (bf16[1024,256]{1,0:T(8,128)(2,1)}, bf16[1024,256]{1,0:T(8,128)(2,1)S(1)}, u32[]{:S(2)}) copy-start(bf16[1024,256]{1,0:T(8,128)(2,1)S(1)} %collective-permute-done.9.kv_ref) | copy-start | bytes 1572868
  58.2 12.1 %collective-permute-start.10 = (bf16[1024,256]{1,0:T(8,128)(2,1)S(1)}, bf16[1024,256]{1,0:T(8,128)(2,1)S(1)}, u32[]{:S(2)}, u32[]{:S(2)}) collective-permute-start(bf16[1024,256]{1,0:T(8,128)(2,1)S(1)} %collective-permute-done.9.kv_ref), channel_id=1, source_target_pairs={{0,32},{32,64},{64,96},{96,128},{128,160},{160,192},{192,224},{224... | collective-permute-start | bytes 1572872 | tf_op jit(solution)/shard_map/ppermute | solution.py:118
  70.2 27.0 %collective-permute-start.7 = (bf16[1024,256]{1,0:T(8,128)(2,1)}, bf16[1024,256]{1,0:T(8,128)(2,1)S(1)}, u32[]{:S(2)}, u32[]{:S(2)}) collective-permute-start(bf16[1024,256]{1,0:T(8,128)(2,1)} %collective-permute-done.6.kv_ref), channel_id=1, source_target_pairs={{0,224},{32,0},{64,32},{96,64},{128,96},{160,128},{192,160},{224,1... | collective-permute-start | bytes 1572872 | tf_op jit(solution)/shard_map/ppermute | solution.py:117
  70.3 24.5 %copy-start.5 = (bf16[1024,256]{1,0:T(8,128)(2,1)}, bf16[1024,256]{1,0:T(8,128)(2,1)S(1)}, u32[]{:S(2)}) copy-start(bf16[1024,256]{1,0:T(8,128)(2,1)S(1)} %collective-permute-done.10.kv_ref) | copy-start | bytes 1572868
  70.3 26.0 %collective-permute-start.11 = (bf16[1024,256]{1,0:T(8,128)(2,1)S(1)}, bf16[1024,256]{1,0:T(8,128)(2,1)S(1)}, u32[]{:S(2)}, u32[]{:S(2)}) collective-permute-start(bf16[1024,256]{1,0:T(8,128)(2,1)S(1)} %collective-permute-done.10.kv_ref), channel_id=1, source_target_pairs={{0,32},{32,64},{64,96},{96,128},{128,160},{160,192},{192,224},{224... | collective-permute-start | bytes 1572872 | tf_op jit(solution)/shard_map/ppermute | solution.py:118
  96.2 11.5 %copy-start.1 = (bf16[1024,256]{1,0:T(8,128)(2,1)}, bf16[1024,256]{1,0:T(8,128)(2,1)S(1)}, u32[]{:S(2)}) copy-start(bf16[1024,256]{1,0:T(8,128)(2,1)S(1)} %collective-permute-done.11.kv_ref) | copy-start | bytes 1572868
  96.2 31.9 %collective-permute-start.12 = (bf16[512,256]{1,0:T(8,128)(2,1)S(1)}, bf16[512,256]{1,0:T(8,128)(2,1)S(1)}, u32[]{:S(2)}, u32[]{:S(2)}) collective-permute-start(bf16[512,256]{1,0:T(8,128)(2,1)S(1)} %slice.115), channel_id=1, source_target_pairs={{0,32},{32,64},{64,96},{96,128},{128,160},{160,192},{192,224},{224... | collective-permute-start | bytes 786440 | tf_op jit(solution)/shard_map/ppermute | solution.py:123
  97.3 10.4 %copy-start.2 = (bf16[1024,256]{1,0:T(8,128)(2,1)}, bf16[1024,256]{1,0:T(8,128)(2,1)S(1)}, u32[]{:S(2)}) copy-start(bf16[1024,256]{1,0:T(8,128)(2,1)S(1)} %collective-permute-done.7.kv_ref) | copy-start | bytes 1572868
  97.3 35.7 %collective-permute-start.8 = (bf16[512,256]{1,0:T(8,128)(2,1)S(1)}, bf16[512,256]{1,0:T(8,128)(2,1)S(1)}, u32[]{:S(2)}, u32[]{:S(2)}) collective-permute-start(bf16[512,256]{1,0:T(8,128)(2,1)S(1)} %slice.114), channel_id=1, source_target_pairs={{0,224},{32,0},{64,32},{96,64},{128,96},{160,128},{192,160},{224,1... | collective-permute-start | bytes 786440 | tf_op jit(solution)/shard_map/ppermute | solution.py:124
  107.7 8.8 %copy-start.8 = (bf16[32,2,4,4,256]{4,3,2,1,0:T(4,128)(2,1)S(1)}, bf16[32,2,4,4,256]{4,3,2,1,0:T(4,128)(2,1)}, u32[]{:S(2)}) copy-start(bf16[32,2,4,4,256]{4,3,2,1,0:T(4,128)(2,1)} %constant_dynamic-update-slice_fusion.16) | copy-start | bytes 1572868
  (2 other events, 1.4 us)

commit v2 on v1

--- a/solution.py
+++ b/solution.py
@@ -44,85 +44,87 @@
     return jnp.sum(jnp.where(onehot, starts[None, :], 0), axis=1)
 
 
-def part_kernel(nb, info_ref, q_ref, kv_ref, qtok_ref, qlo_ref, m_in, l_in, acc_in, m_out, l_out, acc_out):
+def attn_kernel(counts, info_ref, q_ref, qtok_ref, qlo_ref, *refs):
+    parts = refs[: len(counts)]
+    o_ref, m_ref, l_ref, acc_ref = refs[len(counts) :]
     blk = pl.program_id(0)
-    lo = info_ref[nb + 2 * blk]
-    hi = info_ref[nb + 2 * blk + 1]
-    m_out[...] = m_in[...]
-    l_out[...] = l_in[...]
-    acc_out[...] = acc_in[...]
+    total_blocks = sum(counts)
+    lo = info_ref[total_blocks + 2 * blk]
+    hi = info_ref[total_blocks + 2 * blk + 1]
+    m_ref[...] = jnp.full(m_ref.shape, -1e30, jnp.float32)
+    l_ref[...] = jnp.zeros(l_ref.shape, jnp.float32)
+    acc_ref[...] = jnp.zeros(acc_ref.shape, jnp.float32)
     scale = HD ** (-0.5)
-    for j in range(nb):
-        kb = info_ref[j]
-
-        @pl.when((kb >= lo) & (kb <= hi))
-        def _():
-            block = kv_ref[j * KB : (j + 1) * KB, :]
-            keys = block[:, :HD]
-            vals = block[:, HD:]
-            scores = (
-                lax.dot_general(q_ref[...], keys, (((1,), (1,)), ((), ())), preferred_element_type=jnp.float32)
-                * scale
-            )
-            ktok = kb * KB + lax.broadcasted_iota(jnp.int32, (1, KB), 1)
-            visible = (ktok >= qlo_ref[...]) & (ktok <= qtok_ref[...])
-            masked = jnp.where(visible, scores, -1e30)
-            peak = m_out[...]
-            new_peak = jnp.maximum(peak, jnp.max(masked, axis=1, keepdims=True))
-            weights = jnp.where(visible, jnp.exp(masked - new_peak), 0.0)
-            factor = jnp.exp(peak - new_peak)
-            l_out[...] = l_out[...] * factor + jnp.sum(weights, axis=1, keepdims=True)
-            acc_out[...] = acc_out[...] * factor + jnp.dot(
-                weights.astype(jnp.bfloat16), vals, preferred_element_type=jnp.float32
-            )
-            m_out[...] = new_peak
-
-
-def attend_part(info, q, kv, qtok, qlo, state):
+    slot = 0
+    for part_ref, count in zip(parts, counts):
+        for j in range(count):
+            kb = info_ref[slot]
+            slot += 1
+
+            @pl.when((kb >= lo) & (kb <= hi))
+            def _(kb=kb, part_ref=part_ref, j=j):
+                block = part_ref[j * KB : (j + 1) * KB, :]
+                keys = block[:, :HD]
+                vals = block[:, HD:]
+                scores = (
+                    lax.dot_general(q_ref[...], keys, (((1,), (1,)), ((), ())), preferred_element_type=jnp.float32)
+                    * scale
+                )
+                ktok = kb * KB + lax.broadcasted_iota(jnp.int32, (1, KB), 1)
+                visible = (ktok >= qlo_ref[...]) & (ktok <= qtok_ref[...])
+                masked = jnp.where(visible, scores, -1e30)
+                peak = m_ref[...]
+                new_peak = jnp.maximum(peak, jnp.max(masked, axis=1, keepdims=True))
+                weights = jnp.where(visible, jnp.exp(masked - new_peak), 0.0)
+                factor = jnp.exp(peak - new_peak)
+                l_ref[...] = l_ref[...] * factor + jnp.sum(weights, axis=1, keepdims=True)
+                acc_ref[...] = acc_ref[...] * factor + jnp.dot(
+                    weights.astype(jnp.bfloat16), vals, preferred_element_type=jnp.float32
+                )
+                m_ref[...] = new_peak
+
+    o_ref[...] = (acc_ref[...] / l_ref[...]).astype(o_ref.dtype)
+
+
+def attention(info, q, qtok, qlo, parts):
     rows = q.shape[0]
     half = rows // 2
-    nb = kv.shape[0] // KB
+    counts = tuple(part.shape[0] // KB for part in parts)
     row_spec = lambda width: pl.BlockSpec((half, width), lambda i, info: (i, 0))
     return pl.pallas_call(
-        functools.partial(part_kernel, nb),
-        out_shape=(
-            jax.ShapeDtypeStruct((rows, 1), jnp.float32),
-            jax.ShapeDtypeStruct((rows, 1), jnp.float32),
-            jax.ShapeDtypeStruct((rows, HD), jnp.float32),
-        ),
+        functools.partial(attn_kernel, counts),
+        out_shape=jax.ShapeDtypeStruct((rows, HD), jnp.bfloat16),
         grid_spec=pltpu.PrefetchScalarGridSpec(
             num_scalar_prefetch=1,
             grid=(2,),
-            in_specs=[
-                row_spec(HD),
-                pl.BlockSpec(kv.shape, lambda i, info: (0, 0)),
-                row_spec(1),
-                row_spec(1),
-                row_spec(1),
-                row_spec(1),
-                row_spec(HD),
+            in_specs=[row_spec(HD), row_spec(1), row_spec(1)]
+            + [pl.BlockSpec(part.shape, lambda i, info: (0, 0)) for part in parts],
+            out_specs=row_spec(HD),
+            scratch_shapes=[
+                pltpu.VMEM((half, 1), jnp.float32),
+                pltpu.VMEM((half, 1), jnp.float32),
+                pltpu.VMEM((half, HD), jnp.float32),
             ],
-            out_specs=(row_spec(1), row_spec(1), row_spec(HD)),
         ),
-    )(info, q, kv, qtok, qlo, *state)
+    )(info, q, qtok, qlo, *parts)
 
 
 def z_ring(part, n):
     fwd = [part]
     bwd = [part]
     steps = n // 2
-    arrived = [(0, part)]
     for step in range(1, steps + 1):
         if step < steps:
+            fwd.append(lax.ppermute(fwd[-1], "z", [(i, (i + 1) % n) for i in range(n)]))
             bwd.append(lax.ppermute(bwd[-1], "z", [(i, (i - 1) % n) for i in range(n)]))
-            fwd.append(lax.ppermute(fwd[-1], "z", [(i, (i + 1) % n) for i in range(n)]))
-            arrived.append((step, bwd[-1]))
-            arrived.append((n - step, fwd[-1]))
         else:
             cut = part.shape[0] // 2
-            arrived.append((steps, lax.ppermute(fwd[-1][:cut], "z", [(i, (i + 1) % n) for i in range(n)])))
-            arrived.append((steps, lax.ppermute(bwd[-1][cut:], "z", [(i, (i - 1) % n) for i in range(n)])))
-    return arrived
+            far_a = lax.ppermute(fwd[-1][:cut], "z", [(i, (i + 1) % n) for i in range(n)])
+            far_b = lax.ppermute(bwd[-1][cut:], "z", [(i, (i - 1) % n) for i in range(n)])
+    far = [(steps, far_a), (steps, far_b)]
+    near = [(d, bwd[d]) for d in range(steps)]
+    back = [(n - d, fwd[d]) for d in range(steps - 1, 0, -1)]
+    return near + far + back
 
 
 def per_device(hidden_in, w_query, w_key, w_value, query_gain, key_gain, prompt_lengths):
@@ -194,35 +196,32 @@
     r = jnp.arange(span, dtype=jnp.int32)
     q_tokens = jnp.concatenate([cg * span + r, total_tokens - (cg + 1) * span + r])
     q_lo = request_start(q_tokens, prompt_lengths)
-    bounds = jnp.stack([q_lo[0] // KB, cg, q_lo[span] // KB, 2 * groups - 1 - cg]).astype(jnp.int32)
-    rows_q = 2 * span
-    state = (
-        jnp.full((rows_q, 1), -1e30, jnp.float32),
-        jnp.zeros((rows_q, 1), jnp.float32),
-        jnp.zeros((rows_q, HD), jnp.float32),
-    )
-    picked_parts = {}
+    ids = []
     seen = {}
     for dist, part in arrived:
         first = seen.get(dist, 0)
         chunks = part.shape[0] // span
         seen[dist] = first + chunks // 2
-        ids = []
         for j in range(chunks):
             group_j = (2 * ((z_idx + dist) % nz) + first + j // 2) % groups
             ids.append(group_j if j % 2 == 0 else 2 * groups - 1 - group_j)
-        info = jnp.concatenate([jnp.stack(ids).astype(jnp.int32), bounds])
-        state = attend_part(info, q_head, part, q_tokens[:, None], q_lo[:, None], state)
-        sub = part.reshape(chunks // 2, 2, ncl, half_rows, 2 * HD)
-        picked_parts.setdefault(dist, []).append(lax.dynamic_slice_in_dim(sub, cg * ncl, ncl, axis=3))
-    _, total, acc = state
-    out_head = (acc / total).astype(jnp.bfloat16)
+    info = jnp.stack(ids + [q_lo[0] // KB, cg, q_lo[span] // KB, 2 * groups - 1 - cg]).astype(jnp.int32)
+    parts = [part for _, part in arrived]
+    out_head = attention(info, q_head, q_tokens[:, None], q_lo[:, None], parts)
 
     out_lower = out_head[:span].reshape(ncl, half_rows, HD)
     out_upper = out_head[span:].reshape(ncl, half_rows, HD)[::-1]
     out_send = jnp.stack([out_lower, out_upper], axis=1).reshape(ncl, tok_rows, HD)
 
-    picked = jnp.concatenate([p for dist in range(nz) for p in picked_parts[dist]], axis=0)
+    picked = jnp.concatenate(
+        [
+            lax.dynamic_slice_in_dim(
+                part.reshape(part.shape[0] // (2 * span), 2, ncl, half_rows, 2 * HD), cg * ncl, ncl, axis=3
+            )
+            for part in parts
+        ],
+        axis=0,
+    )
     doubled = jnp.concatenate([picked, picked], axis=0)
     natural = lax.dynamic_slice_in_dim(doubled, (groups - (z_idx * nyh) % groups) % groups, groups, axis=0)
     cache_lower = natural[:, 0].reshape(groups * ncl, ncl, 2 * HD)

time: 168 us -> 146 us (0.87)
  Pallas kernels: 40.9 us -> 15.1 us
  waiting for transfers between devices: 32.8 us -> 36.2 us
  other arithmetic: 6.84 us -> 4.65 us
  starting transfers between devices: 21.3 us -> 23.4 us
    pallas_call x9 -> x1, Pallas kernels: 40.9 us -> 15.1 us  [attention(): pl.pallas_call(functools.partial(attn_kernel, counts), out_shape=jax.Shap...]
    ppermute x3, waiting for transfers between devices: 18.4 us -> 0.01 us  [z_ring(): bwd.append(lax.ppermute(bwd[-1], 'z', [(i, (i - 1) % n) for i in range(n)]))]
    ppermute x3, waiting for transfers between devices: 0.01 us -> 17 us  [z_ring(): fwd.append(lax.ppermute(fwd[-1], 'z', [(i, (i + 1) % n) for i in range(n)]))]
    unnamed x46 -> x42, local copies, waits for them, and re-layouts: 18.9 us -> 24.7 us
    concatenate x9 -> x0, local copies, waits for them, and re-layouts: 5.52 us -> none  [per_device(): info = jnp.concatenate([jnp.stack(ids).astype(jnp.int32), bounds])]
    ppermute x1, waiting for transfers between devices: 0.01 us -> 3.9 us  [z_ring(): lax.ppermute(bwd[-1][cut:], 'z', [(i, (i - 1) % n) for i in range(n)])]
    ppermute x1, starting transfers between devices: 1.04 us -> 3.31 us  [z_ring(): lax.ppermute(fwd[-1][:cut], 'z', [(i, (i + 1) % n) for i in range(n)])]
    broadcast_in_dim x4 -> x1, local copies, waits for them, and re-layouts: 3.07 us -> 0.86 us  [per_device(): out_head = attention(info, q_head, q_tokens[:, None], q_lo[:, None], parts)]
  transfers between devices with their start and end apart: 13 -> 13, of which waited for: 7 -> 9; matrix products, arithmetic and copies ran while one was open for 11% -> 7% of each run, Pallas kernels for 22% -> 0%
where the time goes in v2:
time: 146 us; the launch traced here: 144 us
  waiting for transfers between devices  36.2 us (25%)
  local copies, waits for them, and re-layouts  32.4 us (22%)
  starting transfers between devices  23.4 us (16%)
  blocking collectives  20.8 us (14%)
  Pallas kernels  15.1 us (10%)
  between operations  6.67 us (5%)
  matrix products  4.66 us (3%)
  other arithmetic  4.65 us (3%)
    unnamed x42, local copies, waits for them, and re-layouts  24.7 us
    ppermute x3, waiting for transfers between devices, z_ring(): fwd.append(lax.ppermute(fwd[-1], 'z', [(i, (i + 1) % n) for i in range(n)]))  17 us
    pallas_call x1, Pallas kernels, attention(): pl.pallas_call(functools.partial(attn_kernel, counts), out_shape=jax.Shap...  15.1 us
    all_to_all x1, blocking collectives, per_device(): got = lax.all_to_all(packed, CL, split_axis=1, concat_axis=0, tiled=True)  11 us
    ppermute x3, starting transfers between devices, z_ring(): fwd.append(lax.ppermute(fwd[-1], 'z', [(i, (i + 1) % n) for i in range(n)]))  10.6 us
    all_to_all x1, blocking collectives, per_device(): recv = lax.all_to_all(send, CL, split_axis=0, concat_axis=0, tiled=True)  9.77 us
    ppermute x1, waiting for transfers between devices, per_device(): kv_other = lax.ppermute(kv_mine, 'yhi', swap)  5.29 us
    ppermute x1, waiting for transfers between devices, per_device(): across = lax.ppermute(hidden_in, 'xhi', swap)  5.07 us
  transfers between devices with their start and end apart: 13, of which 9 were waited for; matrix products, arithmetic and copies ran while one was open for 7% of the time, Pallas kernels for 0%

profile of v2, /device:TPU:96, one launch (start us, length us, event | category | flops | bytes accessed | tf_op | source)
XLA Modules:
  0.0 143.9 jit_solution(9758126209326249215)
XLA Ops:
  0.6 3.1 %collective-permute-start = (bf16[128,1024]{1,0:T(8,128)(2,1)}, bf16[128,1024]{1,0:T(8,128)(2,1)S(1)}, u32[]{:S(2)}, u32[]{:S(2)}) collective-permute-start(bf16[128,1024]{1,0:T(8,128)(2,1)} %param.7), channel_id=1, source_target_pairs={{0,2},{2,0},{1,3},{3,1},{4,6},{6,4},{5,7},{7,5},{8,10},{10,8},{9,1... | collective-permute-start | bytes 786440 | tf_op jit(solution)/shard_map/ppermute | solution.py:148
  5.4 5.1 %collective-permute-done = bf16[128,1024]{1,0:T(8,128)(2,1)S(1)} collective-permute-done((bf16[128,1024]{1,0:T(8,128)(2,1)}, bf16[128,1024]{1,0:T(8,128)(2,1)S(1)}, u32[]{:S(2)}, u32[]{:S(2)}) %collective-permute-start) | collective-permute-done | bytes 262176 | tf_op jit(solution)/shard_map/ppermute | solution.py:148
  11.8 1.8 %collective-permute-done.1 = bf16[128,2048]{1,0:T(8,128)(2,1)S(1)} collective-permute-done((bf16[128,2048]{1,0:T(8,128)(2,1)S(1)}, bf16[128,2048]{1,0:T(8,128)(2,1)S(1)}, u32[]{:S(2)}, u32[]{:S(2)}) %collective-permute-start.1) | collective-permute-done | bytes 524320 | tf_op jit(solution)/shard_map/ppermute | solution.py:150
  13.7 3.1 %multiply_reduce_fusion.1 = (f32[128]{0:T(128)S(1)}, f32[128,512]{1,0:T(8,128)S(1)}) fusion(bf16[4096,512]{1,0:T(8,128)(2,1)} %param.8, bf16[128,1024]{1,0:T(8,128)(2,1)S(1)} %get-tuple-element.18, bf16[128,1024]{1,0:T(8,128)(2,1)S(1)} %get-tuple-element.16, bf16[128,1024]{1,0:T(8,128)(2,1)S(1)} %get-tuple-element.17, ...), kind=kOutput, calls=%fused_computation.15 | convolution fusion | flops 545914752 | bytes 5505537 | tf_op jit(solution)/shard_map/dot_general | solution.py:155
  18.0 3.1 %collective-permute-start.2 = (f32[2,128]{1,0:T(2,128)S(1)}, f32[2,128]{1,0:T(2,128)S(1)}, u32[]{:S(2)}, u32[]{:S(2)}) collective-permute-start(f32[2,128]{1,0:T(2,128)S(1)} %pad_maximum_fusion.4), channel_id=1, source_target_pairs={{0,2},{2,0},{1,3},{3,1},{4,6},{6,4},{5,7},{7,5},{8,10},{10,8},{9,1... | collective-permute-start | bytes 3080 | tf_op jit(solution)/shard_map/ppermute | solution.py:159
  21.4 1.7 %collective-permute-done.2 = f32[2,128]{1,0:T(2,128)S(1)} collective-permute-done((f32[2,128]{1,0:T(2,128)S(1)}, f32[2,128]{1,0:T(2,128)S(1)}, u32[]{:S(2)}, u32[]{:S(2)}) %collective-permute-start.2) | collective-permute-done | bytes 1056 | tf_op jit(solution)/shard_map/ppermute | solution.py:159
  25.6 11.0 %all_to_all.20 = bf16[128,4,384]{2,0,1:T(8,128)(2,1)S(1)} all-to-all(bf16[128,4,384]{2,0,1:T(8,128)(2,1)S(1)} %concatenate.48), channel_id=1, replica_groups=mesh['z'=8,'yhi'=2,'ylo'=2,'xlo'=2,'xhi'=2,'core'=2] {'ylo','xlo'}, dimensions={1} | all-to-all | bytes 786432 | tf_op jit(solution)/shard_map/all_to_all | solution.py:181
  36.7 3.0 %collective-permute-start.4 = (bf16[512,256]{1,0:T(8,128)(2,1)S(1)}, bf16[512,256]{1,0:T(8,128)(2,1)S(1)}, u32[]{:S(2)}, u32[]{:S(2)}) collective-permute-start(bf16[512,256]{1,0:T(8,128)(2,1)S(1)} %pad_maximum_fusion.1), channel_id=1, source_target_pairs={{0,16},{16,0},{1,17},{17,1},{2,18},{18,2},{3,19},{19,3},{4,20},{20... | collective-permute-start | bytes 786440 | tf_op jit(solution)/shard_map/ppermute | solution.py:190
  39.7 5.3 %collective-permute-done.4 = bf16[512,256]{1,0:T(8,128)(2,1)S(1)} collective-permute-done((bf16[512,256]{1,0:T(8,128)(2,1)S(1)}, bf16[512,256]{1,0:T(8,128)(2,1)S(1)}, u32[]{:S(2)}, u32[]{:S(2)}) %collective-permute-start.4) | collective-permute-done | bytes 262176 | tf_op jit(solution)/shard_map/ppermute | solution.py:190
  45.2 3.2 %collective-permute-start.8 = (bf16[1024,256]{1,0:T(8,128)(2,1)S(1)}, bf16[1024,256]{1,0:T(8,128)(2,1)S(1)}, u32[]{:S(2)}, u32[]{:S(2)}) collective-permute-start(bf16[1024,256]{1,0:T(8,128)(2,1)S(1)} %maximum_select_fusion.2.refs_0_), channel_id=1, source_target_pairs={{0,32},{32,64},{64,96},{96,128},{128,160},{160,192},{192,224},{224... | collective-permute-start | bytes 1572872 | tf_op jit(solution)/shard_map/ppermute | solution.py:118
  48.4 9.0 %collective-permute-done.8.refs_8_ = bf16[1024,256]{1,0:T(8,128)(2,1)S(1)} collective-permute-done((bf16[1024,256]{1,0:T(8,128)(2,1)S(1)}, bf16[1024,256]{1,0:T(8,128)(2,1)S(1)}, u32[]{:S(2)}, u32[]{:S(2)}) %collective-permute-start.8) | collective-permute-done | bytes 524320 | tf_op jit(solution)/shard_map/ppermute | solution.py:118
  57.4 3.7 %collective-permute-start.9 = (bf16[1024,256]{1,0:T(8,128)(2,1)S(1)}, bf16[1024,256]{1,0:T(8,128)(2,1)S(1)}, u32[]{:S(2)}, u32[]{:S(2)}) collective-permute-start(bf16[1024,256]{1,0:T(8,128)(2,1)S(1)} %collective-permute-done.8.refs_8_), channel_id=1, source_target_pairs={{0,32},{32,64},{64,96},{96,128},{128,160},{160,192},{192,224},{224... | collective-permute-start | bytes 1572872 | tf_op jit(solution)/shard_map/ppermute | solution.py:118
  61.4 8.1 %collective-permute-done.9.refs_7_ = bf16[1024,256]{1,0:T(8,128)(2,1)S(1)} collective-permute-done((bf16[1024,256]{1,0:T(8,128)(2,1)S(1)}, bf16[1024,256]{1,0:T(8,128)(2,1)S(1)}, u32[]{:S(2)}, u32[]{:S(2)}) %collective-permute-start.9) | collective-permute-done | bytes 524320 | tf_op jit(solution)/shard_map/ppermute | solution.py:118
  69.5 3.7 %collective-permute-start.10 = (bf16[1024,256]{1,0:T(8,128)(2,1)S(1)}, bf16[1024,256]{1,0:T(8,128)(2,1)S(1)}, u32[]{:S(2)}, u32[]{:S(2)}) collective-permute-start(bf16[1024,256]{1,0:T(8,128)(2,1)S(1)} %collective-permute-done.9.refs_7_), channel_id=1, source_target_pairs={{0,32},{32,64},{64,96},{96,128},{128,160},{160,192},{192,224},{224... | collective-permute-start | bytes 1572872 | tf_op jit(solution)/shard_map/ppermute | solution.py:118
  83.0 3.3 %collective-permute-start.11 = (bf16[512,256]{1,0:T(8,128)(2,1)S(1)}, bf16[512,256]{1,0:T(8,128)(2,1)S(1)}, u32[]{:S(2)}, u32[]{:S(2)}) collective-permute-start(bf16[512,256]{1,0:T(8,128)(2,1)S(1)} %slice.114), channel_id=1, source_target_pairs={{0,32},{32,64},{64,96},{96,128},{128,160},{160,192},{192,224},{224... | collective-permute-start | bytes 786440 | tf_op jit(solution)/shard_map/ppermute | solution.py:122
  87.2 1.5 %constant_dynamic-update-slice_fusion.15 = bf16[32,2,4,4,256]{4,3,2,1,0:T(4,128)(2,1)} fusion(bf16[32,2,4,4,256]{4,3,2,1,0:T(4,128)(2,1)} %constant_dynamic-update-slice_fusion.16, bf16[2,2,4,64,256]{4,3,2,1,0:T(8,128)(2,1)} %bitcast.60, s32[]{:T(128)S(6)} %select_n.303), kind=kLoop, calls=%fused_computation.37 | loop fusion | bytes 65540
  90.2 3.9 %collective-permute-done.12.refs_5_ = bf16[512,256]{1,0:T(8,128)(2,1)} collective-permute-done((bf16[512,256]{1,0:T(8,128)(2,1)S(1)}, bf16[512,256]{1,0:T(8,128)(2,1)}, u32[]{:S(2)}, u32[]{:S(2)}) %collective-permute-start.12) | collective-permute-done | bytes 262176 | tf_op jit(solution)/shard_map/ppermute | solution.py:123
  94.2 15.1 %shard_map.94 = bf16[512,128]{1,0:T(8,128)(2,1)} custom-call(s32[36]{0:T(128)} %stack.162.info_ref, bf16[512,128]{1,0:T(8,128)(2,1)} %pad_maximum_fusion.2.q_ref, s32[512,1]{1,0:T(8,128)} %copy.53.qtok_ref, s32[512,1]{1,0:T(8,128)} %copy.54.qlo_ref, bf16[1024,256]{1,0:T(8,128)(2,1)} %copy-done, bf16[1024,256]{1,0:T(8,128)(2,1)} %copy-done.5, ...), custom_call_target="tpu_custom_call" | custom-call | tf_op jit(solution)/shard_map/pallas_call | solution.py:94
  114.4 1.5 %constant_dynamic-update-slice_fusion.10 = bf16[32,2,4,4,256]{4,3,2,1,0:T(4,128)(2,1)} fusion(bf16[32,2,4,4,256]{4,3,2,1,0:T(4,128)(2,1)} %constant_dynamic-update-slice_fusion.11, bf16[2,2,4,64,256]{4,3,2,1,0:T(8,128)(2,1)} %bitcast.102, s32[]{:T(128)S(6)} %select_n.303), kind=kLoop, calls=%fused_computation.32 | loop fusion | bytes 65540
  115.8 1.5 %constant_dynamic-update-slice_fusion.9 = bf16[32,2,4,4,256]{4,3,2,1,0:T(4,128)(2,1)} fusion(bf16[32,2,4,4,256]{4,3,2,1,0:T(4,128)(2,1)} %constant_dynamic-update-slice_fusion.10, bf16[2,2,4,64,256]{4,3,2,1,0:T(8,128)(2,1)} %bitcast.100, s32[]{:T(128)S(6)} %select_n.303), kind=kLoop, calls=%fused_computation.31 | loop fusion | bytes 65540
  117.3 1.5 %constant_dynamic-update-slice_fusion.8 = bf16[32,2,4,4,256]{4,3,2,1,0:T(4,128)(2,1)} fusion(bf16[32,2,4,4,256]{4,3,2,1,0:T(4,128)(2,1)} %constant_dynamic-update-slice_fusion.9, bf16[2,2,4,64,256]{4,3,2,1,0:T(8,128)(2,1)} %bitcast.89, s32[]{:T(128)S(6)} %select_n.303), kind=kLoop, calls=%fused_computation.30 | loop fusion | bytes 65540
  125.9 1.5 %constant_dynamic-update-slice_fusion.2 = bf16[32,2,4,4,256]{4,3,2,1,0:T(4,128)(2,1)} fusion(bf16[32,2,4,4,256]{4,3,2,1,0:T(4,128)(2,1)} %constant_dynamic-update-slice_fusion.3, bf16[2,2,4,64,256]{4,3,2,1,0:T(8,128)(2,1)} %bitcast.97, s32[]{:T(128)S(6)} %select_n.303), kind=kLoop, calls=%fused_computation.24 | loop fusion | bytes 65540
  128.8 1.5 %constant_dynamic-update-slice_fusion = bf16[32,2,4,4,256]{4,3,2,1,0:T(4,128)(2,1)} fusion(bf16[32,2,4,4,256]{4,3,2,1,0:T(4,128)(2,1)} %constant_dynamic-update-slice_fusion.1, bf16[2,2,4,64,256]{4,3,2,1,0:T(8,128)(2,1)} %bitcast.101, s32[]{:T(128)S(6)} %select_n.303), kind=kLoop, calls=%fused_computation.22 | loop fusion | bytes 65540 | tf_op jit(solution)/shard_map/concatenate | solution.py:225
  131.6 9.8 %all_to_all.21 = bf16[4,128,384]{2,1,0:T(8,128)(2,1)S(1)} all-to-all(bf16[4,128,384]{2,1,0:T(8,128)(2,1)S(1)} %pad_maximum_fusion), channel_id=1, replica_groups=mesh['z'=8,'yhi'=2,'ylo'=2,'xlo'=2,'xhi'=2,'core'=2] {'ylo','xlo'}, dimensions={0} | all-to-all | bytes 786432 | tf_op jit(solution)/shard_map/all_to_all | solution.py:231
  (100 shorter events, 31.5 us)
Async XLA Ops:
  0.6 9.8 %collective-permute-start = (bf16[128,1024]{1,0:T(8,128)(2,1)}, bf16[128,1024]{1,0:T(8,128)(2,1)S(1)}, u32[]{:S(2)}, u32[]{:S(2)}) collective-permute-start(bf16[128,1024]{1,0:T(8,128)(2,1)} %param.7), channel_id=1, source_target_pairs={{0,2},{2,0},{1,3},{3,1},{4,6},{6,4},{5,7},{7,5},{8,10},{10,8},{9,1... | collective-permute-start | bytes 786440 | tf_op jit(solution)/shard_map/ppermute | solution.py:148
  11.7 2.0 %collective-permute-start.1 = (bf16[128,2048]{1,0:T(8,128)(2,1)S(1)}, bf16[128,2048]{1,0:T(8,128)(2,1)S(1)}, u32[]{:S(2)}, u32[]{:S(2)}) collective-permute-start(bf16[128,2048]{1,0:T(8,128)(2,1)S(1)} %maximum_select_fusion.1), channel_id=1, source_target_pairs={{0,1},{1,0},{2,3},{3,2},{4,5},{5,4},{6,7},{7,6},{8,9},{9,8},{10,11... | collective-permute-start | bytes 1572872 | tf_op jit(solution)/shard_map/ppermute | solution.py:150
  13.7 3.5 %copy-start.9 = (bf16[4096,512]{1,0:T(8,128)(2,1)S(1)}, bf16[4096,512]{1,0:T(8,128)(2,1)}, u32[]{:S(2)}) copy-start(bf16[4096,512]{1,0:T(8,128)(2,1)} %param.9) | copy-start | bytes 12582916
  17.2 6.1 %copy-start.10 = (bf16[4096,512]{1,0:T(8,128)(2,1)S(1)}, bf16[4096,512]{1,0:T(8,128)(2,1)}, u32[]{:S(2)}) copy-start(bf16[4096,512]{1,0:T(8,128)(2,1)} %param.10) | copy-start | bytes 12582916
  18.0 5.2 %collective-permute-start.2 = (f32[2,128]{1,0:T(2,128)S(1)}, f32[2,128]{1,0:T(2,128)S(1)}, u32[]{:S(2)}, u32[]{:S(2)}) collective-permute-start(f32[2,128]{1,0:T(2,128)S(1)} %pad_maximum_fusion.4), channel_id=1, source_target_pairs={{0,2},{2,0},{1,3},{3,1},{4,6},{6,4},{5,7},{7,5},{8,10},{10,8},{9,1... | collective-permute-start | bytes 3080 | tf_op jit(solution)/shard_map/ppermute | solution.py:159
  23.1 1.3 copy-start.7
  23.2 1.3 copy-start.8
  23.2 1.2 collective-permute-start.3
  36.7 8.3 %collective-permute-start.4 = (bf16[512,256]{1,0:T(8,128)(2,1)S(1)}, bf16[512,256]{1,0:T(8,128)(2,1)S(1)}, u32[]{:S(2)}, u32[]{:S(2)}) collective-permute-start(bf16[512,256]{1,0:T(8,128)(2,1)S(1)} %pad_maximum_fusion.1), channel_id=1, source_target_pairs={{0,16},{16,0},{1,17},{17,1},{2,18},{18,2},{3,19},{19,3},{4,20},{20... | collective-permute-start | bytes 786440 | tf_op jit(solution)/shard_map/ppermute | solution.py:190
  45.2 48.9 %copy-start = (bf16[1024,256]{1,0:T(8,128)(2,1)}, bf16[1024,256]{1,0:T(8,128)(2,1)S(1)}, u32[]{:S(2)}) copy-start(bf16[1024,256]{1,0:T(8,128)(2,1)S(1)} %maximum_select_fusion.2.refs_0_) | copy-start | bytes 1572868
  45.2 12.2 %collective-permute-start.8 = (bf16[1024,256]{1,0:T(8,128)(2,1)S(1)}, bf16[1024,256]{1,0:T(8,128)(2,1)S(1)}, u32[]{:S(2)}, u32[]{:S(2)}) collective-permute-start(bf16[1024,256]{1,0:T(8,128)(2,1)S(1)} %maximum_select_fusion.2.refs_0_), channel_id=1, source_target_pairs={{0,32},{32,64},{64,96},{96,128},{128,160},{160,192},{192,224},{224... | collective-permute-start | bytes 1572872 | tf_op jit(solution)/shard_map/ppermute | solution.py:118
  48.4 12.7 %collective-permute-start.5 = (bf16[1024,256]{1,0:T(8,128)(2,1)S(1)}, bf16[1024,256]{1,0:T(8,128)(2,1)S(1)}, u32[]{:S(2)}, u32[]{:S(2)}) collective-permute-start(bf16[1024,256]{1,0:T(8,128)(2,1)S(1)} %maximum_select_fusion.2.refs_0_), channel_id=1, source_target_pairs={{0,224},{32,0},{64,32},{96,64},{128,96},{160,128},{192,160},{224,1... | collective-permute-start | bytes 1572872 | tf_op jit(solution)/shard_map/ppermute | solution.py:119
  57.4 36.7 %copy-start.3 = (bf16[1024,256]{1,0:T(8,128)(2,1)}, bf16[1024,256]{1,0:T(8,128)(2,1)S(1)}, u32[]{:S(2)}) copy-start(bf16[1024,256]{1,0:T(8,128)(2,1)S(1)} %collective-permute-done.8.refs_8_) | copy-start | bytes 1572868
  57.4 12.1 %collective-permute-start.9 = (bf16[1024,256]{1,0:T(8,128)(2,1)S(1)}, bf16[1024,256]{1,0:T(8,128)(2,1)S(1)}, u32[]{:S(2)}, u32[]{:S(2)}) collective-permute-start(bf16[1024,256]{1,0:T(8,128)(2,1)S(1)} %collective-permute-done.8.refs_8_), channel_id=1, source_target_pairs={{0,32},{32,64},{64,96},{96,128},{128,160},{160,192},{192,224},{224... | collective-permute-start | bytes 1572872 | tf_op jit(solution)/shard_map/ppermute | solution.py:118
  61.1 33.0 %copy-start.5 = (bf16[1024,256]{1,0:T(8,128)(2,1)}, bf16[1024,256]{1,0:T(8,128)(2,1)S(1)}, u32[]{:S(2)}) copy-start(bf16[1024,256]{1,0:T(8,128)(2,1)S(1)} %collective-permute-done.5.refs_1_) | copy-start | bytes 1572868
  61.1 12.1 %collective-permute-start.6 = (bf16[1024,256]{1,0:T(8,128)(2,1)S(1)}, bf16[1024,256]{1,0:T(8,128)(2,1)}, u32[]{:S(2)}, u32[]{:S(2)}) collective-permute-start(bf16[1024,256]{1,0:T(8,128)(2,1)S(1)} %collective-permute-done.5.refs_1_), channel_id=1, source_target_pairs={{0,224},{32,0},{64,32},{96,64},{128,96},{160,128},{192,160},{224,1... | collective-permute-start | bytes 1572872 | tf_op jit(solution)/shard_map/ppermute | solution.py:119
  69.5 24.7 %copy-start.4 = (bf16[1024,256]{1,0:T(8,128)(2,1)}, bf16[1024,256]{1,0:T(8,128)(2,1)S(1)}, u32[]{:S(2)}) copy-start(bf16[1024,256]{1,0:T(8,128)(2,1)S(1)} %collective-permute-done.9.refs_7_) | copy-start | bytes 1572868
  69.5 13.5 %collective-permute-start.10 = (bf16[1024,256]{1,0:T(8,128)(2,1)S(1)}, bf16[1024,256]{1,0:T(8,128)(2,1)S(1)}, u32[]{:S(2)}, u32[]{:S(2)}) collective-permute-start(bf16[1024,256]{1,0:T(8,128)(2,1)S(1)} %collective-permute-done.9.refs_7_), channel_id=1, source_target_pairs={{0,32},{32,64},{64,96},{96,128},{128,160},{160,192},{192,224},{224... | collective-permute-start | bytes 1572872 | tf_op jit(solution)/shard_map/ppermute | solution.py:118
  73.2 13.2 %collective-permute-start.7 = (bf16[1024,256]{1,0:T(8,128)(2,1)}, bf16[1024,256]{1,0:T(8,128)(2,1)S(1)}, u32[]{:S(2)}, u32[]{:S(2)}) collective-permute-start(bf16[1024,256]{1,0:T(8,128)(2,1)} %collective-permute-done.6.refs_2_), channel_id=1, source_target_pairs={{0,224},{32,0},{64,32},{96,64},{128,96},{160,128},{192,160},{224,1... | collective-permute-start | bytes 1572872 | tf_op jit(solution)/shard_map/ppermute | solution.py:119
  83.0 11.2 %copy-start.1 = (bf16[1024,256]{1,0:T(8,128)(2,1)}, bf16[1024,256]{1,0:T(8,128)(2,1)S(1)}, u32[]{:S(2)}) copy-start(bf16[1024,256]{1,0:T(8,128)(2,1)S(1)} %collective-permute-done.10.refs_6_) | copy-start | bytes 1572868
  83.0 7.2 %collective-permute-start.11 = (bf16[512,256]{1,0:T(8,128)(2,1)S(1)}, bf16[512,256]{1,0:T(8,128)(2,1)S(1)}, u32[]{:S(2)}, u32[]{:S(2)}) collective-permute-start(bf16[512,256]{1,0:T(8,128)(2,1)S(1)} %slice.114), channel_id=1, source_target_pairs={{0,32},{32,64},{64,96},{96,128},{128,160},{160,192},{192,224},{224... | collective-permute-start | bytes 786440 | tf_op jit(solution)/shard_map/ppermute | solution.py:122
  86.4 7.8 %copy-start.2 = (bf16[1024,256]{1,0:T(8,128)(2,1)}, bf16[1024,256]{1,0:T(8,128)(2,1)S(1)}, u32[]{:S(2)}) copy-start(bf16[1024,256]{1,0:T(8,128)(2,1)S(1)} %collective-permute-done.7.refs_3_) | copy-start | bytes 1572868
  86.4 7.8 %collective-permute-start.12 = (bf16[512,256]{1,0:T(8,128)(2,1)S(1)}, bf16[512,256]{1,0:T(8,128)(2,1)}, u32[]{:S(2)}, u32[]{:S(2)}) collective-permute-start(bf16[512,256]{1,0:T(8,128)(2,1)S(1)} %slice.115), channel_id=1, source_target_pairs={{0,224},{32,0},{64,32},{96,64},{128,96},{160,128},{192,160},{224,1... | collective-permute-start | bytes 786440 | tf_op jit(solution)/shard_map/ppermute | solution.py:123
  90.2 3.9 %copy-start.6 = (bf16[512,256]{1,0:T(8,128)(2,1)}, bf16[512,256]{1,0:T(8,128)(2,1)S(1)}, u32[]{:S(2)}) copy-start(bf16[512,256]{1,0:T(8,128)(2,1)S(1)} %collective-permute-done.11.refs_4_) | copy-start | bytes 786436

commit v3 on v0

--- a/solution.py
+++ b/solution.py
@@ -48,8 +48,10 @@
     blk = pl.program_id(0)
     lo = info_ref[2 * blk]
     hi = info_ref[2 * blk + 1]
-    shift = info_ref[4]
-    groups = info_ref[5]
+    z_own = info_ref[4]
+    core_own = info_ref[5]
+    nz = info_ref[6]
+    groups = 2 * nz
     nblocks = 2 * groups
     q = q_ref[...]
     qtok = qtok_ref[...]
@@ -61,8 +63,9 @@
         peak, total, acc = carry
         upper = kb >= groups
         group = jnp.where(upper, nblocks - 1 - kb, kb)
-        slot = (group - shift + groups) % groups
-        start = pl.multiple_of((slot * 2 + upper.astype(jnp.int32)) * KB, KB)
+        dist = (group // 2 - z_own + nz) % nz
+        other = (group % 2 != core_own).astype(jnp.int32)
+        start = pl.multiple_of(((other * nz + dist) * 2 + upper.astype(jnp.int32)) * KB, KB)
         block = kv_ref[pl.ds(start, KB), :]
         keys = block[:, :HD]
         vals = block[:, HD:]
@@ -124,7 +127,7 @@
             far_a = lax.ppermute(fwd[-1][:cut], "z", [(i, (i + 1) % n) for i in range(n)])
             far_b = lax.ppermute(bwd[-1][cut:], "z", [(i, (i - 1) % n) for i in range(n)])
     ordered = bwd[: steps] + [far_a, far_b] + fwd[1:steps][::-1]
-    return jnp.concatenate(ordered, axis=0)
+    return ordered
 
 
 def per_device(hidden_in, w_query, w_key, w_value, query_gain, key_gain, prompt_lengths):
@@ -187,23 +190,30 @@
     kv_mine = mine[:, HD:]
 
     yh = lax.axis_index("yhi")
-    kv_other = lax.ppermute(kv_mine, "yhi", swap)
-    kv_pair = jnp.where(yh == 0, jnp.concatenate([kv_mine, kv_other], axis=0), jnp.concatenate([kv_other, kv_mine], axis=0))
-    kv_all = z_ring(kv_pair, nz)
-
+    pair_axes = ("yhi", "core")
+    crossed = lax.ppermute(mine, pair_axes, [(1, 2), (2, 1)])
+    mine = jnp.where(yh == core, mine, crossed)
+    q_head = mine[:, :HD]
+    kv_mine = mine[:, HD:]
+    ring_parts = z_ring(kv_mine, nz)
+    sibling_parts = [lax.ppermute(p, "core", swap) for p in ring_parts]
+    kv_all = jnp.concatenate(ring_parts + sibling_parts, axis=0)
+
+    q_group = z_idx * nyh + core
     span = ncl * half_rows
     total_tokens = 2 * ctx_count * half_rows
     r = jnp.arange(span, dtype=jnp.int32)
-    q_tokens = jnp.concatenate([cg * span + r, total_tokens - (cg + 1) * span + r])
+    q_tokens = jnp.concatenate([q_group * span + r, total_tokens - (q_group + 1) * span + r])
     q_lo = request_start(q_tokens, prompt_lengths)
     info = jnp.stack(
         [
             q_lo[0] // KB,
-            cg,
+            q_group,
             q_lo[span] // KB,
-            2 * groups - 1 - cg,
-            (z_idx * nyh) % groups,
-            jnp.asarray(groups, jnp.int32),
+            2 * groups - 1 - q_group,
+            z_idx,
+            core,
+            jnp.asarray(nz, jnp.int32),
         ]
     ).astype(jnp.int32)
     out_head = attention(info, q_head, kv_all, q_tokens[:, None], q_lo[:, None])
@@ -212,14 +222,18 @@
     out_upper = out_head[span:].reshape(ncl, half_rows, HD)[::-1]
     out_send = jnp.stack([out_lower, out_upper], axis=1).reshape(ncl, tok_rows, HD)
 
-    picked = kv_all.reshape(groups, 2, ncl, half_rows, 2 * HD)
-    picked = lax.dynamic_slice_in_dim(picked, cg * ncl, ncl, axis=3)
-    doubled = jnp.concatenate([picked, picked], axis=0)
-    natural = lax.dynamic_slice_in_dim(doubled, (groups - (z_idx * nyh) % groups) % groups, groups, axis=0)
+    picked = kv_all.reshape(2, nz, 2, ncl, half_rows, 2 * HD)
+    picked = lax.dynamic_slice_in_dim(picked, q_group * ncl, ncl, axis=4)
+    doubled = jnp.concatenate([picked, picked], axis=1)
+    by_z = lax.dynamic_slice_in_dim(doubled, (nz - z_idx) % nz, nz, axis=1)
+    by_half = jnp.where(core == 0, by_z, by_z[::-1])
+    natural = by_half.transpose(1, 0, 2, 3, 4, 5).reshape(groups, 2, ncl, ncl, 2 * HD)
     cache_lower = natural[:, 0].reshape(groups * ncl, ncl, 2 * HD)
     cache_upper = natural[::-1, 1].reshape(groups * ncl, ncl, 2 * HD)
     cache = jnp.concatenate([cache_lower, cache_upper], axis=0).transpose(1, 0, 2)
     send = jnp.concatenate([out_send, cache], axis=2)
+    crossed_back = lax.ppermute(send, pair_axes, [(1, 2), (2, 1)])
+    send = jnp.where(yh == core, send, crossed_back)
     recv = lax.all_to_all(send, CL, split_axis=0, concat_axis=0, tiled=True)
     recv = recv.transpose(1, 0, 2)
     attn_out = recv[:, :, :HD].reshape(tok_rows, local_width)

time: 125 us -> 139 us (1.11)
  the two profiles are of different devices: /device:TPU:96 before, /device:TPU:97 now
where the time goes in v3:
time: 139 us; the launch traced here: 137 us
  starting transfers between devices  37.6 us (27%)
  waiting for transfers between devices  33.6 us (24%)
  local copies, waits for them, and re-layouts  22.5 us (16%)
  blocking collectives  17 us (12%)
  Pallas kernels  11.3 us (8%)
  between operations  5.95 us (4%)
  matrix products  4.66 us (3%)
  other arithmetic  4.44 us (3%)
    unnamed x28, local copies, waits for them, and re-layouts  13.9 us
    pallas_call x1, Pallas kernels, attention(): pl.pallas_call(attn_kernel, out_shape=jax.ShapeDtypeStruct((rows, HD), jn...  11.3 us
    ppermute x3, waiting for transfers between devices, z_ring(): fwd.append(lax.ppermute(fwd[-1], 'z', [(i, (i + 1) % n) for i in range(n)]))  10.7 us
    ppermute x3, starting transfers between devices, z_ring(): fwd.append(lax.ppermute(fwd[-1], 'z', [(i, (i + 1) % n) for i in range(n)]))  9.37 us
    all_to_all x1, blocking collectives, per_device(): got = lax.all_to_all(packed, CL, split_axis=1, concat_axis=0, tiled=True)  9.33 us
    all_to_all x1, blocking collectives, per_device(): recv = lax.all_to_all(send, CL, split_axis=0, concat_axis=0, tiled=True)  7.67 us
    ppermute x1, waiting for transfers between devices, per_device(): crossed_back = lax.ppermute(send, pair_axes, [(1, 2), (2, 1)])  7.55 us
    ppermute x1, starting transfers between devices, per_device(): crossed = lax.ppermute(mine, pair_axes, [(1, 2), (2, 1)])  6.45 us
  transfers between devices with their start and end apart: 23, of which 11 were waited for; matrix products, arithmetic and copies ran while one was open for 13% of the time, Pallas kernels for 0%

profile of v3, /device:TPU:97, one launch (start us, length us, event | category | flops | bytes accessed | tf_op | source)
XLA Modules:
  0.0 137.1 jit_solution(4124070305170069439)
XLA Ops:
  0.6 2.8 %collective-permute-start = (bf16[128,1024]{1,0:T(8,128)(2,1)}, bf16[128,1024]{1,0:T(8,128)(2,1)S(1)}, u32[]{:S(2)}, u32[]{:S(2)}) collective-permute-start(bf16[128,1024]{1,0:T(8,128)(2,1)} %param.7), channel_id=1, source_target_pairs={{0,2},{2,0},{1,3},{3,1},{4,6},{6,4},{5,7},{7,5},{8,10},{10,8},{9,1... | collective-permute-start | bytes 786440 | tf_op jit(solution)/shard_map/ppermute | solution.py:151
  5.1 4.5 %collective-permute-done = bf16[128,1024]{1,0:T(8,128)(2,1)S(1)} collective-permute-done((bf16[128,1024]{1,0:T(8,128)(2,1)}, bf16[128,1024]{1,0:T(8,128)(2,1)S(1)}, u32[]{:S(2)}, u32[]{:S(2)}) %collective-permute-start) | collective-permute-done | bytes 262176 | tf_op jit(solution)/shard_map/ppermute | solution.py:151
  10.8 1.6 %collective-permute-start.1 = (bf16[128,2048]{1,0:T(8,128)(2,1)S(1)}, bf16[128,2048]{1,0:T(8,128)(2,1)S(1)}, u32[]{:S(2)}, u32[]{:S(2)}) collective-permute-start(bf16[128,2048]{1,0:T(8,128)(2,1)S(1)} %maximum_select_fusion.1), channel_id=1, source_target_pairs={{0,1},{1,0},{2,3},{3,2},{4,5},{5,4},{6,7},{7,6},{8,9},{9,8},{10,11... | collective-permute-start | bytes 1572872 | tf_op jit(solution)/shard_map/ppermute | solution.py:153
  12.5 1.5 %collective-permute-done.1 = bf16[128,2048]{1,0:T(8,128)(2,1)S(1)} collective-permute-done((bf16[128,2048]{1,0:T(8,128)(2,1)S(1)}, bf16[128,2048]{1,0:T(8,128)(2,1)S(1)}, u32[]{:S(2)}, u32[]{:S(2)}) %collective-permute-start.1) | collective-permute-done | bytes 524320 | tf_op jit(solution)/shard_map/ppermute | solution.py:153
  14.0 3.1 %multiply_reduce_fusion.1 = (f32[128]{0:T(128)S(1)}, f32[128,512]{1,0:T(8,128)S(1)}) fusion(bf16[4096,512]{1,0:T(8,128)(2,1)} %param.8, bf16[128,1024]{1,0:T(8,128)(2,1)S(1)} %get-tuple-element.16, bf16[128,1024]{1,0:T(8,128)(2,1)S(1)} %get-tuple-element.14, bf16[128,1024]{1,0:T(8,128)(2,1)S(1)} %get-tuple-element.15, ...), kind=kOutput, calls=%fused_computation.20 | convolution fusion | flops 545914752 | bytes 5505537 | tf_op jit(solution)/shard_map/dot_general | solution.py:158
  18.3 2.8 %collective-permute-start.2 = (f32[2,128]{1,0:T(2,128)S(1)}, f32[2,128]{1,0:T(2,128)S(1)}, u32[]{:S(2)}, u32[]{:S(2)}) collective-permute-start(f32[2,128]{1,0:T(2,128)S(1)} %pad_maximum_fusion.3), channel_id=1, source_target_pairs={{0,2},{2,0},{1,3},{3,1},{4,6},{6,4},{5,7},{7,5},{8,10},{10,8},{9,1... | collective-permute-start | bytes 3080 | tf_op jit(solution)/shard_map/ppermute | solution.py:162
  22.3 1.6 %collective-permute-start.3 = (f32[2,128]{1,0:T(2,128)S(1)}, f32[2,128]{1,0:T(2,128)S(1)}, u32[]{:S(2)}, u32[]{:S(2)}) collective-permute-start(f32[2,128]{1,0:T(2,128)S(1)} %fusion.4), channel_id=1, source_target_pairs={{0,1},{1,0},{2,3},{3,2},{4,5},{5,4},{6,7},{7,6},{8,9},{9,8},{10,11... | collective-permute-start | bytes 3080 | tf_op jit(solution)/shard_map/ppermute | solution.py:163
  25.9 9.3 %all_to_all.20 = bf16[128,4,384]{2,0,1:T(8,128)(2,1)S(1)} all-to-all(bf16[128,4,384]{2,0,1:T(8,128)(2,1)S(1)} %concatenate.43), channel_id=1, replica_groups=mesh['z'=8,'yhi'=2,'ylo'=2,'xlo'=2,'xhi'=2,'core'=2] {'ylo','xlo'}, dimensions={1} | all-to-all | bytes 786432 | tf_op jit(solution)/shard_map/all_to_all | solution.py:184
  35.4 6.5 %collective-permute-start.4 = (bf16[512,384]{1,0:T(8,128)(2,1)S(1)}, bf16[512,384]{1,0:T(8,128)(2,1)S(1)}, u32[]{:S(2)}, u32[]{:S(2)}) collective-permute-start(bf16[512,384]{1,0:T(8,128)(2,1)S(1)} %pad_maximum_fusion), channel_id=1, source_target_pairs={{1,16},{16,1},{3,18},{18,3},{5,20},{20,5},{7,22},{22,7},{9,24},{24... | collective-permute-start | bytes 1179656 | tf_op jit(solution)/shard_map/ppermute | solution.py:194
  41.8 5.4 %collective-permute-done.4 = bf16[512,384]{1,0:T(8,128)(2,1)S(1)} collective-permute-done((bf16[512,384]{1,0:T(8,128)(2,1)S(1)}, bf16[512,384]{1,0:T(8,128)(2,1)S(1)}, u32[]{:S(2)}, u32[]{:S(2)}) %collective-permute-start.4) | collective-permute-done | bytes 393248 | tf_op jit(solution)/shard_map/ppermute | solution.py:194
  48.1 2.8 %collective-permute-start.8 = (bf16[512,256]{1,0:T(8,128)(2,1)S(1)}, bf16[512,256]{1,0:T(8,128)(2,1)S(1)}, u32[]{:S(2)}, u32[]{:S(2)}) collective-permute-start(bf16[512,256]{1,0:T(8,128)(2,1)S(1)} %get-tuple-element.20), channel_id=1, source_target_pairs={{0,32},{32,64},{64,96},{96,128},{128,160},{160,192},{192,224},{224... | collective-permute-start | bytes 786440 | tf_op jit(solution)/shard_map/ppermute | solution.py:123
  51.0 5.0 %collective-permute-done.8 = bf16[512,256]{1,0:T(8,128)(2,1)S(1)} collective-permute-done((bf16[512,256]{1,0:T(8,128)(2,1)S(1)}, bf16[512,256]{1,0:T(8,128)(2,1)S(1)}, u32[]{:S(2)}, u32[]{:S(2)}) %collective-permute-start.8) | collective-permute-done | bytes 262176 | tf_op jit(solution)/shard_map/ppermute | solution.py:123
  56.0 3.1 %collective-permute-start.9 = (bf16[512,256]{1,0:T(8,128)(2,1)S(1)}, bf16[512,256]{1,0:T(8,128)(2,1)S(1)}, u32[]{:S(2)}, u32[]{:S(2)}) collective-permute-start(bf16[512,256]{1,0:T(8,128)(2,1)S(1)} %collective-permute-done.8), channel_id=1, source_target_pairs={{0,32},{32,64},{64,96},{96,128},{128,160},{160,192},{192,224},{224... | collective-permute-start | bytes 786440 | tf_op jit(solution)/shard_map/ppermute | solution.py:123
  59.5 5.7 %collective-permute-done.9 = bf16[512,256]{1,0:T(8,128)(2,1)S(1)} collective-permute-done((bf16[512,256]{1,0:T(8,128)(2,1)S(1)}, bf16[512,256]{1,0:T(8,128)(2,1)S(1)}, u32[]{:S(2)}, u32[]{:S(2)}) %collective-permute-start.9) | collective-permute-done | bytes 262176 | tf_op jit(solution)/shard_map/ppermute | solution.py:123
  65.2 3.4 %collective-permute-start.10 = (bf16[512,256]{1,0:T(8,128)(2,1)S(1)}, bf16[512,256]{1,0:T(8,128)(2,1)S(1)}, u32[]{:S(2)}, u32[]{:S(2)}) collective-permute-start(bf16[512,256]{1,0:T(8,128)(2,1)S(1)} %collective-permute-done.9), channel_id=1, source_target_pairs={{0,32},{32,64},{64,96},{96,128},{128,160},{160,192},{192,224},{224... | collective-permute-start | bytes 786440 | tf_op jit(solution)/shard_map/ppermute | solution.py:123
  78.6 2.7 %collective-permute-start.11 = (bf16[256,256]{1,0:T(8,128)(2,1)S(1)}, bf16[256,256]{1,0:T(8,128)(2,1)S(1)}, u32[]{:S(2)}, u32[]{:S(2)}) collective-permute-start(bf16[256,256]{1,0:T(8,128)(2,1)S(1)} %slice.116), channel_id=1, source_target_pairs={{0,32},{32,64},{64,96},{96,128},{128,160},{160,192},{192,224},{224... | collective-permute-start | bytes 393224 | tf_op jit(solution)/shard_map/ppermute | solution.py:127
  83.7 1.4 collective-permute-start.15
  85.7 1.9 %collective-permute-done.12 = bf16[256,256]{1,0:T(8,128)(2,1)S(1)} collective-permute-done((bf16[256,256]{1,0:T(8,128)(2,1)S(1)}, bf16[256,256]{1,0:T(8,128)(2,1)S(1)}, u32[]{:S(2)}, u32[]{:S(2)}) %collective-permute-start.12) | collective-permute-done | bytes 131104 | tf_op jit(solution)/shard_map/ppermute | solution.py:128
  87.6 1.6 %collective-permute-start.20 = (bf16[512,256]{1,0:T(8,128)(2,1)S(1)}, bf16[512,256]{1,0:T(8,128)(2,1)S(1)}, u32[]{:S(2)}, u32[]{:S(2)}) collective-permute-start(bf16[512,256]{1,0:T(8,128)(2,1)S(1)} %collective-permute-done.9), channel_id=1, source_target_pairs={{0,1},{1,0},{2,3},{3,2},{4,5},{5,4},{6,7},{7,6},{8,9},{9,8},{10,11... | collective-permute-start | bytes 786440 | tf_op jit(solution)/shard_map/ppermute | solution.py:199
  99.4 11.3 %shard_map.94 = bf16[512,128]{1,0:T(8,128)(2,1)} custom-call(s32[7]{0:T(128)} %stack.42.info_ref, bf16[512,128]{1,0:T(8,128)(2,1)} %slice.114.q_ref, bf16[8192,256]{1,0:T(8,128)(2,1)} %constant_dynamic-update-slice_fusion.kv_ref, s32[512,1]{1,0:T(8,128)} %copy.56.qtok_ref, s32[512,1]{1,0:T(8,128)} %copy.57.qlo_ref), custom_call_target="tpu_custom_call" | custom-call | tf_op jit(solution)/shard_map/pallas_call | solution.py:100
  111.6 1.2 constant_dynamic-slice_fusion
  113.8 5.4 %collective-permute-start.22 = (bf16[4,128,384]{2,1,0:T(8,128)(2,1)S(1)}, bf16[4,128,384]{2,1,0:T(8,128)(2,1)S(1)}, u32[]{:S(2)}, u32[]{:S(2)}) collective-permute-start(bf16[4,128,384]{2,1,0:T(8,128)(2,1)S(1)} %pad_maximum_fusion.1), channel_id=1, source_target_pairs={{1,16},{16,1},{3,18},{18,3},{5,20},{20,5},{7,22},{22,7},{9,24},{24... | collective-permute-start | bytes 1179656 | tf_op jit(solution)/shard_map/ppermute | solution.py:235
  119.2 7.6 %collective-permute-done.22 = bf16[4,128,384]{2,1,0:T(8,128)(2,1)S(1)} collective-permute-done((bf16[4,128,384]{2,1,0:T(8,128)(2,1)S(1)}, bf16[4,128,384]{2,1,0:T(8,128)(2,1)S(1)}, u32[]{:S(2)}, u32[]{:S(2)}) %collective-permute-start.22) | collective-permute-done | bytes 393248 | tf_op jit(solution)/shard_map/ppermute | solution.py:235
  126.8 7.7 %all_to_all.21 = bf16[4,128,384]{2,1,0:T(8,128)(2,1)S(1)} all-to-all(bf16[4,128,384]{2,1,0:T(8,128)(2,1)S(1)} %broadcast_select_fusion.1), channel_id=1, replica_groups=mesh['z'=8,'yhi'=2,'ylo'=2,'xlo'=2,'xhi'=2,'core'=2] {'ylo','xlo'}, dimensions={0} | all-to-all | bytes 786432 | tf_op jit(solution)/shard_map/all_to_all | solution.py:237
  (111 shorter events, 31.0 us)
Async XLA Ops:
  0.6 9.0 %collective-permute-start = (bf16[128,1024]{1,0:T(8,128)(2,1)}, bf16[128,1024]{1,0:T(8,128)(2,1)S(1)}, u32[]{:S(2)}, u32[]{:S(2)}) collective-permute-start(bf16[128,1024]{1,0:T(8,128)(2,1)} %param.7), channel_id=1, source_target_pairs={{0,2},{2,0},{1,3},{3,1},{4,6},{6,4},{5,7},{7,5},{8,10},{10,8},{9,1... | collective-permute-start | bytes 786440 | tf_op jit(solution)/shard_map/ppermute | solution.py:151
  10.8 3.2 %collective-permute-start.1 = (bf16[128,2048]{1,0:T(8,128)(2,1)S(1)}, bf16[128,2048]{1,0:T(8,128)(2,1)S(1)}, u32[]{:S(2)}, u32[]{:S(2)}) collective-permute-start(bf16[128,2048]{1,0:T(8,128)(2,1)S(1)} %maximum_select_fusion.1), channel_id=1, source_target_pairs={{0,1},{1,0},{2,3},{3,2},{4,5},{5,4},{6,7},{7,6},{8,9},{9,8},{10,11... | collective-permute-start | bytes 1572872 | tf_op jit(solution)/shard_map/ppermute | solution.py:153
  17.4 6.5 %copy-start.3 = (bf16[4096,512]{1,0:T(8,128)(2,1)S(1)}, bf16[4096,512]{1,0:T(8,128)(2,1)}, u32[]{:S(2)}) copy-start(bf16[4096,512]{1,0:T(8,128)(2,1)} %param.10) | copy-start | bytes 12582916
  18.3 4.0 %collective-permute-start.2 = (f32[2,128]{1,0:T(2,128)S(1)}, f32[2,128]{1,0:T(2,128)S(1)}, u32[]{:S(2)}, u32[]{:S(2)}) collective-permute-start(f32[2,128]{1,0:T(2,128)S(1)} %pad_maximum_fusion.3), channel_id=1, source_target_pairs={{0,2},{2,0},{1,3},{3,1},{4,6},{6,4},{5,7},{7,5},{8,10},{10,8},{9,1... | collective-permute-start | bytes 3080 | tf_op jit(solution)/shard_map/ppermute | solution.py:162
  22.3 2.4 %collective-permute-start.3 = (f32[2,128]{1,0:T(2,128)S(1)}, f32[2,128]{1,0:T(2,128)S(1)}, u32[]{:S(2)}, u32[]{:S(2)}) collective-permute-start(f32[2,128]{1,0:T(2,128)S(1)} %fusion.4), channel_id=1, source_target_pairs={{0,1},{1,0},{2,3},{3,2},{4,5},{5,4},{6,7},{7,6},{8,9},{9,8},{10,11... | collective-permute-start | bytes 3080 | tf_op jit(solution)/shard_map/ppermute | solution.py:163
  35.4 11.9 %collective-permute-start.4 = (bf16[512,384]{1,0:T(8,128)(2,1)S(1)}, bf16[512,384]{1,0:T(8,128)(2,1)S(1)}, u32[]{:S(2)}, u32[]{:S(2)}) collective-permute-start(bf16[512,384]{1,0:T(8,128)(2,1)S(1)} %pad_maximum_fusion), channel_id=1, source_target_pairs={{1,16},{16,1},{3,18},{18,3},{5,20},{20,5},{7,22},{22,7},{9,24},{24... | collective-permute-start | bytes 1179656 | tf_op jit(solution)/shard_map/ppermute | solution.py:194
  48.1 7.9 %collective-permute-start.8 = (bf16[512,256]{1,0:T(8,128)(2,1)S(1)}, bf16[512,256]{1,0:T(8,128)(2,1)S(1)}, u32[]{:S(2)}, u32[]{:S(2)}) collective-permute-start(bf16[512,256]{1,0:T(8,128)(2,1)S(1)} %get-tuple-element.20), channel_id=1, source_target_pairs={{0,32},{32,64},{64,96},{96,128},{128,160},{160,192},{192,224},{224... | collective-permute-start | bytes 786440 | tf_op jit(solution)/shard_map/ppermute | solution.py:123
  51.0 8.4 %collective-permute-start.5 = (bf16[512,256]{1,0:T(8,128)(2,1)S(1)}, bf16[512,256]{1,0:T(8,128)(2,1)S(1)}, u32[]{:S(2)}, u32[]{:S(2)}) collective-permute-start(bf16[512,256]{1,0:T(8,128)(2,1)S(1)} %get-tuple-element.20), channel_id=1, source_target_pairs={{0,224},{32,0},{64,32},{96,64},{128,96},{160,128},{192,160},{224,1... | collective-permute-start | bytes 786440 | tf_op jit(solution)/shard_map/ppermute | solution.py:124
  56.0 9.2 %collective-permute-start.9 = (bf16[512,256]{1,0:T(8,128)(2,1)S(1)}, bf16[512,256]{1,0:T(8,128)(2,1)S(1)}, u32[]{:S(2)}, u32[]{:S(2)}) collective-permute-start(bf16[512,256]{1,0:T(8,128)(2,1)S(1)} %collective-permute-done.8), channel_id=1, source_target_pairs={{0,32},{32,64},{64,96},{96,128},{128,160},{160,192},{192,224},{224... | collective-permute-start | bytes 786440 | tf_op jit(solution)/shard_map/ppermute | solution.py:123
  59.4 9.3 %collective-permute-start.6 = (bf16[512,256]{1,0:T(8,128)(2,1)S(1)}, bf16[512,256]{1,0:T(8,128)(2,1)S(1)}, u32[]{:S(2)}, u32[]{:S(2)}) collective-permute-start(bf16[512,256]{1,0:T(8,128)(2,1)S(1)} %collective-permute-done.5), channel_id=1, source_target_pairs={{0,224},{32,0},{64,32},{96,64},{128,96},{160,128},{192,160},{224,1... | collective-permute-start | bytes 786440 | tf_op jit(solution)/shard_map/ppermute | solution.py:124
  65.2 13.4 %collective-permute-start.10 = (bf16[512,256]{1,0:T(8,128)(2,1)S(1)}, bf16[512,256]{1,0:T(8,128)(2,1)S(1)}, u32[]{:S(2)}, u32[]{:S(2)}) collective-permute-start(bf16[512,256]{1,0:T(8,128)(2,1)S(1)} %collective-permute-done.9), channel_id=1, source_target_pairs={{0,32},{32,64},{64,96},{96,128},{128,160},{160,192},{192,224},{224... | collective-permute-start | bytes 786440 | tf_op jit(solution)/shard_map/ppermute | solution.py:123
  68.7 13.4 %collective-permute-start.7 = (bf16[512,256]{1,0:T(8,128)(2,1)S(1)}, bf16[512,256]{1,0:T(8,128)(2,1)S(1)}, u32[]{:S(2)}, u32[]{:S(2)}) collective-permute-start(bf16[512,256]{1,0:T(8,128)(2,1)S(1)} %collective-permute-done.6), channel_id=1, source_target_pairs={{0,224},{32,0},{64,32},{96,64},{128,96},{160,128},{192,160},{224,1... | collective-permute-start | bytes 786440 | tf_op jit(solution)/shard_map/ppermute | solution.py:124
  76.7 15.4 %collective-permute-start.13 = (bf16[512,256]{1,0:T(8,128)(2,1)S(1)}, bf16[512,256]{1,0:T(8,128)(2,1)S(1)}, u32[]{:S(2)}, u32[]{:S(2)}) collective-permute-start(bf16[512,256]{1,0:T(8,128)(2,1)S(1)} %get-tuple-element.20), channel_id=1, source_target_pairs={{0,1},{1,0},{2,3},{3,2},{4,5},{5,4},{6,7},{7,6},{8,9},{9,8},{10,11... | collective-permute-start | bytes 786440 | tf_op jit(solution)/shard_map/ppermute | solution.py:199
  77.4 15.4 %collective-permute-start.14 = (bf16[512,256]{1,0:T(8,128)(2,1)S(1)}, bf16[512,256]{1,0:T(8,128)(2,1)S(1)}, u32[]{:S(2)}, u32[]{:S(2)}) collective-permute-start(bf16[512,256]{1,0:T(8,128)(2,1)S(1)} %collective-permute-done.5), channel_id=1, source_target_pairs={{0,1},{1,0},{2,3},{3,2},{4,5},{5,4},{6,7},{7,6},{8,9},{9,8},{10,11... | collective-permute-start | bytes 786440 | tf_op jit(solution)/shard_map/ppermute | solution.py:199
  77.9 20.8 %collective-permute-start.21 = (bf16[512,256]{1,0:T(8,128)(2,1)S(1)}, bf16[512,256]{1,0:T(8,128)(2,1)S(1)}, u32[]{:S(2)}, u32[]{:S(2)}) collective-permute-start(bf16[512,256]{1,0:T(8,128)(2,1)S(1)} %collective-permute-done.8), channel_id=1, source_target_pairs={{0,1},{1,0},{2,3},{3,2},{4,5},{5,4},{6,7},{7,6},{8,9},{9,8},{10,11... | collective-permute-start | bytes 786440 | tf_op jit(solution)/shard_map/ppermute | solution.py:199
  78.6 5.1 %collective-permute-start.11 = (bf16[256,256]{1,0:T(8,128)(2,1)S(1)}, bf16[256,256]{1,0:T(8,128)(2,1)S(1)}, u32[]{:S(2)}, u32[]{:S(2)}) collective-permute-start(bf16[256,256]{1,0:T(8,128)(2,1)S(1)} %slice.116), channel_id=1, source_target_pairs={{0,32},{32,64},{64,96},{96,128},{128,160},{160,192},{192,224},{224... | collective-permute-start | bytes 393224 | tf_op jit(solution)/shard_map/ppermute | solution.py:127
  82.1 5.6 %collective-permute-start.12 = (bf16[256,256]{1,0:T(8,128)(2,1)S(1)}, bf16[256,256]{1,0:T(8,128)(2,1)S(1)}, u32[]{:S(2)}, u32[]{:S(2)}) collective-permute-start(bf16[256,256]{1,0:T(8,128)(2,1)S(1)} %slice.117), channel_id=1, source_target_pairs={{0,224},{32,0},{64,32},{96,64},{128,96},{160,128},{192,160},{224,1... | collective-permute-start | bytes 393224 | tf_op jit(solution)/shard_map/ppermute | solution.py:128
  83.7 10.3 %collective-permute-start.15 = (bf16[512,256]{1,0:T(8,128)(2,1)S(1)}, bf16[512,256]{1,0:T(8,128)(2,1)S(1)}, u32[]{:S(2)}, u32[]{:S(2)}) collective-permute-start(bf16[512,256]{1,0:T(8,128)(2,1)S(1)} %collective-permute-done.6), channel_id=1, source_target_pairs={{0,1},{1,0},{2,3},{3,2},{4,5},{5,4},{6,7},{7,6},{8,9},{9,8},{10,11... | collective-permute-start | bytes 786440 | tf_op jit(solution)/shard_map/ppermute | solution.py:199
  87.6 10.4 %collective-permute-start.20 = (bf16[512,256]{1,0:T(8,128)(2,1)S(1)}, bf16[512,256]{1,0:T(8,128)(2,1)S(1)}, u32[]{:S(2)}, u32[]{:S(2)}) collective-permute-start(bf16[512,256]{1,0:T(8,128)(2,1)S(1)} %collective-permute-done.9), channel_id=1, source_target_pairs={{0,1},{1,0},{2,3},{3,2},{4,5},{5,4},{6,7},{7,6},{8,9},{9,8},{10,11... | collective-permute-start | bytes 786440 | tf_op jit(solution)/shard_map/ppermute | solution.py:199
  92.1 2.7 %collective-permute-start.16 = (bf16[512,256]{1,0:T(8,128)(2,1)S(1)}, bf16[512,256]{1,0:T(8,128)(2,1)S(1)}, u32[]{:S(2)}, u32[]{:S(2)}) collective-permute-start(bf16[512,256]{1,0:T(8,128)(2,1)S(1)} %collective-permute-done.7), channel_id=1, source_target_pairs={{0,1},{1,0},{2,3},{3,2},{4,5},{5,4},{6,7},{7,6},{8,9},{9,8},{10,11... | collective-permute-start | bytes 786440 | tf_op jit(solution)/shard_map/ppermute | solution.py:199
  92.8 4.5 %collective-permute-start.19 = (bf16[512,256]{1,0:T(8,128)(2,1)S(1)}, bf16[512,256]{1,0:T(8,128)(2,1)S(1)}, u32[]{:S(2)}, u32[]{:S(2)}) collective-permute-start(bf16[512,256]{1,0:T(8,128)(2,1)S(1)} %collective-permute-done.10), channel_id=1, source_target_pairs={{0,1},{1,0},{2,3},{3,2},{4,5},{5,4},{6,7},{7,6},{8,9},{9,8},{10,11... | collective-permute-start | bytes 786440 | tf_op jit(solution)/shard_map/ppermute | solution.py:199
  94.0 2.0 %collective-permute-start.17 = (bf16[256,256]{1,0:T(8,128)(2,1)S(1)}, bf16[256,256]{1,0:T(8,128)(2,1)S(1)}, u32[]{:S(2)}, u32[]{:S(2)}) collective-permute-start(bf16[256,256]{1,0:T(8,128)(2,1)S(1)} %collective-permute-done.11), channel_id=1, source_target_pairs={{0,1},{1,0},{2,3},{3,2},{4,5},{5,4},{6,7},{7,6},{8,9},{9,8},{10,11... | collective-permute-start | bytes 393224 | tf_op jit(solution)/shard_map/ppermute | solution.py:199
  94.8 1.9 %collective-permute-start.18 = (bf16[256,256]{1,0:T(8,128)(2,1)S(1)}, bf16[256,256]{1,0:T(8,128)(2,1)S(1)}, u32[]{:S(2)}, u32[]{:S(2)}) collective-permute-start(bf16[256,256]{1,0:T(8,128)(2,1)S(1)} %collective-permute-done.12), channel_id=1, source_target_pairs={{0,1},{1,0},{2,3},{3,2},{4,5},{5,4},{6,7},{7,6},{8,9},{9,8},{10,11... | collective-permute-start | bytes 393224 | tf_op jit(solution)/shard_map/ppermute | solution.py:199
  113.8 13.0 %collective-permute-start.22 = (bf16[4,128,384]{2,1,0:T(8,128)(2,1)S(1)}, bf16[4,128,384]{2,1,0:T(8,128)(2,1)S(1)}, u32[]{:S(2)}, u32[]{:S(2)}) collective-permute-start(bf16[4,128,384]{2,1,0:T(8,128)(2,1)S(1)} %pad_maximum_fusion.1), channel_id=1, source_target_pairs={{1,16},{16,1},{3,18},{18,3},{5,20},{20,5},{7,22},{22,7},{9,24},{24... | collective-permute-start | bytes 1179656 | tf_op jit(solution)/shard_map/ppermute | solution.py:235
  (3 other events, 8.4 us)

commit v4 on v0

--- a/solution.py
+++ b/solution.py
@@ -57,7 +57,14 @@
     rows = q.shape[0]
     scale = HD ** (-0.5)
 
+    first_tok = info_ref[6 + 2 * blk]
+    last_lo = info_ref[7 + 2 * blk]
+
     def body(kb, carry):
+        inside = (kb * KB >= last_lo) & (kb * KB + KB - 1 <= first_tok)
+        return lax.cond(inside, lambda c: step(kb, c, False), lambda c: step(kb, c, True), carry)
+
+    def step(kb, carry, masking):
         peak, total, acc = carry
         upper = kb >= groups
         group = jnp.where(upper, nblocks - 1 - kb, kb)
@@ -70,11 +77,15 @@
             lax.dot_general(q, keys, (((1,), (1,)), ((), ())), preferred_element_type=jnp.float32)
             * scale
         )
-        ktok = kb * KB + lax.broadcasted_iota(jnp.int32, (1, KB), 1)
-        visible = (ktok >= qlo) & (ktok <= qtok)
-        masked = jnp.where(visible, scores, -1e30)
-        new_peak = jnp.maximum(peak, jnp.max(masked, axis=1, keepdims=True))
-        weights = jnp.where(visible, jnp.exp(masked - new_peak), 0.0)
+        if masking:
+            ktok = kb * KB + lax.broadcasted_iota(jnp.int32, (1, KB), 1)
+            visible = (ktok >= qlo) & (ktok <= qtok)
+            masked = jnp.where(visible, scores, -1e30)
+            new_peak = jnp.maximum(peak, jnp.max(masked, axis=1, keepdims=True))
+            weights = jnp.where(visible, jnp.exp(masked - new_peak), 0.0)
+        else:
+            new_peak = jnp.maximum(peak, jnp.max(scores, axis=1, keepdims=True))
+            weights = jnp.exp(scores - new_peak)
         factor = jnp.exp(peak - new_peak)
         total = total * factor + jnp.sum(weights, axis=1, keepdims=True)
         acc = acc * factor + jnp.dot(
@@ -204,6 +215,10 @@
             2 * groups - 1 - cg,
             (z_idx * nyh) % groups,
             jnp.asarray(groups, jnp.int32),
+            q_tokens[0],
+            q_lo[span - 1],
+            q_tokens[span],
+            q_lo[2 * span - 1],
         ]
     ).astype(jnp.int32)
     out_head = attention(info, q_head, kv_all, q_tokens[:, None], q_lo[:, None])

time: 125 us -> 130 us (1.040)
  local copies, waits for them, and re-layouts: 15.5 us -> 19.1 us
  Pallas kernels: 9.66 us -> 11.7 us
    another operation x1, local copies, waits for them, and re-layouts: 0.62 us -> 3.05 us  [per_device(): jnp.stack([q_lo[0] // KB, cg, q_lo[span] // KB, 2 * groups - 1 - cg, z_id...]
    pallas_call x1, Pallas kernels: 9.66 us -> 11.7 us  [attention(): pl.pallas_call(attn_kernel, out_shape=jax.ShapeDtypeStruct((rows, HD), jn...]
    unnamed x18 -> x20, local copies, waits for them, and re-layouts: 8.27 us -> 8.29 us
  transfers between devices with their start and end apart: 13 -> 13, of which waited for: 9 -> 9; matrix products, arithmetic and copies ran while one was open for 8% -> 11% of each run, Pallas kernels for 0% -> 0%
where the time goes in v4:
time: 130 us; the launch traced here: 129 us
  waiting for transfers between devices  36.8 us (28%)
  starting transfers between devices  23.6 us (18%)
  blocking collectives  20.8 us (16%)
  local copies, waits for them, and re-layouts  19.1 us (15%)
  Pallas kernels  11.7 us (9%)
  other arithmetic  6.32 us (5%)
  between operations  5.79 us (4%)
  matrix products  4.66 us (4%)
    ppermute x3, waiting for transfers between devices, z_ring(): fwd.append(lax.ppermute(fwd[-1], 'z', [(i, (i + 1) % n) for i in range(n)]))  17.3 us
    pallas_call x1, Pallas kernels, attention(): pl.pallas_call(attn_kernel, out_shape=jax.ShapeDtypeStruct((rows, HD), jn...  11.7 us
    all_to_all x1, blocking collectives, per_device(): got = lax.all_to_all(packed, CL, split_axis=1, concat_axis=0, tiled=True)  11 us
    ppermute x3, starting transfers between devices, z_ring(): fwd.append(lax.ppermute(fwd[-1], 'z', [(i, (i + 1) % n) for i in range(n)]))  10.5 us
    all_to_all x1, blocking collectives, per_device(): recv = lax.all_to_all(send, CL, split_axis=0, concat_axis=0, tiled=True)  9.77 us
    unnamed x20, local copies, waits for them, and re-layouts  8.29 us
    ppermute x1, waiting for transfers between devices, per_device(): kv_other = lax.ppermute(kv_mine, 'yhi', swap)  5.28 us
    ppermute x1, waiting for transfers between devices, per_device(): across = lax.ppermute(hidden_in, 'xhi', swap)  5.06 us
  transfers between devices with their start and end apart: 13, of which 9 were waited for; matrix products, arithmetic and copies ran while one was open for 11% of the time, Pallas kernels for 0%

profile of v4, /device:TPU:96, one launch (start us, length us, event | category | flops | bytes accessed | tf_op | source)
XLA Modules:
  0.0 128.6 jit_solution(9860433131745486638)
XLA Ops:
  0.6 3.1 %collective-permute-start = (bf16[128,1024]{1,0:T(8,128)(2,1)}, bf16[128,1024]{1,0:T(8,128)(2,1)S(1)}, u32[]{:S(2)}, u32[]{:S(2)}) collective-permute-start(bf16[128,1024]{1,0:T(8,128)(2,1)} %param.7), channel_id=1, source_target_pairs={{0,2},{2,0},{1,3},{3,1},{4,6},{6,4},{5,7},{7,5},{8,10},{10,8},{9,1... | collective-permute-start | bytes 786440 | tf_op jit(solution)/shard_map/ppermute | solution.py:159
  5.4 5.1 %collective-permute-done = bf16[128,1024]{1,0:T(8,128)(2,1)S(1)} collective-permute-done((bf16[128,1024]{1,0:T(8,128)(2,1)}, bf16[128,1024]{1,0:T(8,128)(2,1)S(1)}, u32[]{:S(2)}, u32[]{:S(2)}) %collective-permute-start) | collective-permute-done | bytes 262176 | tf_op jit(solution)/shard_map/ppermute | solution.py:159
  10.5 1.2 maximum_select_fusion.1
  11.8 1.8 %collective-permute-done.1 = bf16[128,2048]{1,0:T(8,128)(2,1)S(1)} collective-permute-done((bf16[128,2048]{1,0:T(8,128)(2,1)S(1)}, bf16[128,2048]{1,0:T(8,128)(2,1)S(1)}, u32[]{:S(2)}, u32[]{:S(2)}) %collective-permute-start.1) | collective-permute-done | bytes 524320 | tf_op jit(solution)/shard_map/ppermute | solution.py:161
  13.7 3.1 %multiply_reduce_fusion.1 = (f32[128]{0:T(128)S(1)}, f32[128,512]{1,0:T(8,128)S(1)}) fusion(bf16[4096,512]{1,0:T(8,128)(2,1)} %param.8, bf16[128,1024]{1,0:T(8,128)(2,1)S(1)} %get-tuple-element.18, bf16[128,1024]{1,0:T(8,128)(2,1)S(1)} %get-tuple-element.16, bf16[128,1024]{1,0:T(8,128)(2,1)S(1)} %get-tuple-element.17, ...), kind=kOutput, calls=%fused_computation.18 | convolution fusion | flops 545914752 | bytes 5505537 | tf_op jit(solution)/shard_map/dot_general | solution.py:166
  17.9 3.1 %collective-permute-start.2 = (f32[2,128]{1,0:T(2,128)S(1)}, f32[2,128]{1,0:T(2,128)S(1)}, u32[]{:S(2)}, u32[]{:S(2)}) collective-permute-start(f32[2,128]{1,0:T(2,128)S(1)} %pad_maximum_fusion.4), channel_id=1, source_target_pairs={{0,2},{2,0},{1,3},{3,1},{4,6},{6,4},{5,7},{7,5},{8,10},{10,8},{9,1... | collective-permute-start | bytes 3080 | tf_op jit(solution)/shard_map/ppermute | solution.py:170
  21.4 1.8 %collective-permute-done.2 = f32[2,128]{1,0:T(2,128)S(1)} collective-permute-done((f32[2,128]{1,0:T(2,128)S(1)}, f32[2,128]{1,0:T(2,128)S(1)}, u32[]{:S(2)}, u32[]{:S(2)}) %collective-permute-start.2) | collective-permute-done | bytes 1056 | tf_op jit(solution)/shard_map/ppermute | solution.py:170
  25.6 11.0 %all_to_all.20 = bf16[128,4,384]{2,0,1:T(8,128)(2,1)S(1)} all-to-all(bf16[128,4,384]{2,0,1:T(8,128)(2,1)S(1)} %concatenate.49), channel_id=1, replica_groups=mesh['z'=8,'yhi'=2,'ylo'=2,'xlo'=2,'xhi'=2,'core'=2] {'ylo','xlo'}, dimensions={1} | all-to-all | bytes 786432 | tf_op jit(solution)/shard_map/all_to_all | solution.py:192
  36.7 3.0 %collective-permute-start.4 = (bf16[512,256]{1,0:T(8,128)(2,1)S(1)}, bf16[512,256]{1,0:T(8,128)(2,1)S(1)}, u32[]{:S(2)}, u32[]{:S(2)}) collective-permute-start(bf16[512,256]{1,0:T(8,128)(2,1)S(1)} %pad_maximum_fusion.1), channel_id=1, source_target_pairs={{0,16},{16,0},{1,17},{17,1},{2,18},{18,2},{3,19},{19,3},{4,20},{20... | collective-permute-start | bytes 786440 | tf_op jit(solution)/shard_map/ppermute | solution.py:201
  39.7 5.3 %collective-permute-done.4 = bf16[512,256]{1,0:T(8,128)(2,1)S(1)} collective-permute-done((bf16[512,256]{1,0:T(8,128)(2,1)S(1)}, bf16[512,256]{1,0:T(8,128)(2,1)S(1)}, u32[]{:S(2)}, u32[]{:S(2)}) %collective-permute-start.4) | collective-permute-done | bytes 262176 | tf_op jit(solution)/shard_map/ppermute | solution.py:201
  45.0 0.9 constant_dynamic-update-slice_fusion.8
  45.9 3.1 %collective-permute-start.8 = (bf16[1024,256]{1,0:T(8,128)(2,1)S(1)}, bf16[1024,256]{1,0:T(8,128)(2,1)S(1)}, u32[]{:S(2)}, u32[]{:S(2)}) collective-permute-start(bf16[1024,256]{1,0:T(8,128)(2,1)S(1)} %get-tuple-element.10), channel_id=1, source_target_pairs={{0,32},{32,64},{64,96},{96,128},{128,160},{160,192},{192,224},{224... | collective-permute-start | bytes 1572872 | tf_op jit(solution)/shard_map/ppermute | solution.py:131
  49.0 9.0 %collective-permute-done.8 = bf16[1024,256]{1,0:T(8,128)(2,1)S(1)} collective-permute-done((bf16[1024,256]{1,0:T(8,128)(2,1)S(1)}, bf16[1024,256]{1,0:T(8,128)(2,1)S(1)}, u32[]{:S(2)}, u32[]{:S(2)}) %collective-permute-start.8) | collective-permute-done | bytes 524320 | tf_op jit(solution)/shard_map/ppermute | solution.py:131
  58.0 3.7 %collective-permute-start.9 = (bf16[1024,256]{1,0:T(8,128)(2,1)S(1)}, bf16[1024,256]{1,0:T(8,128)(2,1)S(1)}, u32[]{:S(2)}, u32[]{:S(2)}) collective-permute-start(bf16[1024,256]{1,0:T(8,128)(2,1)S(1)} %collective-permute-done.8), channel_id=1, source_target_pairs={{0,32},{32,64},{64,96},{96,128},{128,160},{160,192},{192,224},{224... | collective-permute-start | bytes 1572872 | tf_op jit(solution)/shard_map/ppermute | solution.py:131
  61.7 8.4 %collective-permute-done.9 = bf16[1024,256]{1,0:T(8,128)(2,1)S(1)} collective-permute-done((bf16[1024,256]{1,0:T(8,128)(2,1)S(1)}, bf16[1024,256]{1,0:T(8,128)(2,1)S(1)}, u32[]{:S(2)}, u32[]{:S(2)}) %collective-permute-start.9) | collective-permute-done | bytes 524320 | tf_op jit(solution)/shard_map/ppermute | solution.py:131
  70.1 3.7 %collective-permute-start.10 = (bf16[1024,256]{1,0:T(8,128)(2,1)S(1)}, bf16[1024,256]{1,0:T(8,128)(2,1)S(1)}, u32[]{:S(2)}, u32[]{:S(2)}) collective-permute-start(bf16[1024,256]{1,0:T(8,128)(2,1)S(1)} %collective-permute-done.9), channel_id=1, source_target_pairs={{0,32},{32,64},{64,96},{96,128},{128,160},{160,192},{192,224},{224... | collective-permute-start | bytes 1572872 | tf_op jit(solution)/shard_map/ppermute | solution.py:131
  82.9 3.1 %stack.38.info_ref = s32[10]{0:T(128)} concatenate(s32[1]{0:T(128)} %bitcast.3, s32[1]{0:T(128)} %bitcast.4, s32[1]{0:T(128)} %bitcast.6, s32[1]{0:T(128)} %bitcast.7, s32[1]{0:T(128)} %bitcast.8, s32[1]{0:T(128)} %constant.103.clone.1, s32[1]{0:T(128)} %slice.93, s32[1]{0:T(128)} %get-tuple-element.35, s32[1]{0:T(128)} %slice.95, s32[1]{0:T(128)} %get-tuple-element.34), dimensions={0} | concatenate | bytes 80 | tf_op jit(solution)/shard_map/stack | solution.py:210
  86.6 3.5 %collective-permute-start.11 = (bf16[512,256]{1,0:T(8,128)(2,1)S(1)}, bf16[512,256]{1,0:T(8,128)(2,1)S(1)}, u32[]{:S(2)}, u32[]{:S(2)}) collective-permute-start(bf16[512,256]{1,0:T(8,128)(2,1)S(1)} %slice.130), channel_id=1, source_target_pairs={{0,32},{32,64},{64,96},{96,128},{128,160},{160,192},{192,224},{224... | collective-permute-start | bytes 786440 | tf_op jit(solution)/shard_map/ppermute | solution.py:135
  92.7 1.2 collective-permute-done.11
  94.7 3.9 %collective-permute-done.12 = bf16[512,256]{1,0:T(8,128)(2,1)S(1)} collective-permute-done((bf16[512,256]{1,0:T(8,128)(2,1)S(1)}, bf16[512,256]{1,0:T(8,128)(2,1)S(1)}, u32[]{:S(2)}, u32[]{:S(2)}) %collective-permute-start.12) | collective-permute-done | bytes 262176 | tf_op jit(solution)/shard_map/ppermute | solution.py:136
  101.8 11.7 %shard_map.94 = bf16[512,128]{1,0:T(8,128)(2,1)} custom-call(s32[10]{0:T(128)} %stack.38.info_ref, bf16[512,128]{1,0:T(8,128)(2,1)} %pad_maximum_fusion.2.q_ref, bf16[8192,256]{1,0:T(8,128)(2,1)} %constant_dynamic-update-slice_fusion.kv_ref, s32[512,1]{1,0:T(8,128)} %copy.53.qtok_ref, s32[512,1]{1,0:T(8,128)} %copy.54.qlo_ref), custom_call_target="tpu_custom_call" | custom-call | tf_op jit(solution)/shard_map/pallas_call | solution.py:108
  113.5 0.9 fusion.14
  114.4 1.2 constant_dynamic-slice_fusion
  116.3 9.8 %all_to_all.21 = bf16[4,128,384]{2,1,0:T(8,128)(2,1)S(1)} all-to-all(bf16[4,128,384]{2,1,0:T(8,128)(2,1)S(1)} %pad_maximum_fusion), channel_id=1, replica_groups=mesh['z'=8,'yhi'=2,'ylo'=2,'xlo'=2,'xhi'=2,'core'=2] {'ylo','xlo'}, dimensions={0} | all-to-all | bytes 786432 | tf_op jit(solution)/shard_map/all_to_all | solution.py:238
  (82 shorter events, 20.4 us)
Async XLA Ops:
  0.6 9.8 %collective-permute-start = (bf16[128,1024]{1,0:T(8,128)(2,1)}, bf16[128,1024]{1,0:T(8,128)(2,1)S(1)}, u32[]{:S(2)}, u32[]{:S(2)}) collective-permute-start(bf16[128,1024]{1,0:T(8,128)(2,1)} %param.7), channel_id=1, source_target_pairs={{0,2},{2,0},{1,3},{3,1},{4,6},{6,4},{5,7},{7,5},{8,10},{10,8},{9,1... | collective-permute-start | bytes 786440 | tf_op jit(solution)/shard_map/ppermute | solution.py:159
  5.2 11.6 %copy-start.2 = (s32[4]{0:T(128)}, s32[4]{0:T(128)S(1)}, u32[]{:S(2)}) copy-start(s32[4]{0:T(128)S(1)} %bitcast_subtract_fusion) | copy-start | bytes 52
  11.6 2.0 %collective-permute-start.1 = (bf16[128,2048]{1,0:T(8,128)(2,1)S(1)}, bf16[128,2048]{1,0:T(8,128)(2,1)S(1)}, u32[]{:S(2)}, u32[]{:S(2)}) collective-permute-start(bf16[128,2048]{1,0:T(8,128)(2,1)S(1)} %maximum_select_fusion.1), channel_id=1, source_target_pairs={{0,1},{1,0},{2,3},{3,2},{4,5},{5,4},{6,7},{7,6},{8,9},{9,8},{10,11... | collective-permute-start | bytes 1572872 | tf_op jit(solution)/shard_map/ppermute | solution.py:161
  13.7 3.5 %copy-start.3 = (bf16[4096,512]{1,0:T(8,128)(2,1)S(1)}, bf16[4096,512]{1,0:T(8,128)(2,1)}, u32[]{:S(2)}) copy-start(bf16[4096,512]{1,0:T(8,128)(2,1)} %param.9) | copy-start | bytes 12582916
  17.1 6.1 %copy-start.4 = (bf16[4096,512]{1,0:T(8,128)(2,1)S(1)}, bf16[4096,512]{1,0:T(8,128)(2,1)}, u32[]{:S(2)}) copy-start(bf16[4096,512]{1,0:T(8,128)(2,1)} %param.10) | copy-start | bytes 12582916
  17.9 5.2 %collective-permute-start.2 = (f32[2,128]{1,0:T(2,128)S(1)}, f32[2,128]{1,0:T(2,128)S(1)}, u32[]{:S(2)}, u32[]{:S(2)}) collective-permute-start(f32[2,128]{1,0:T(2,128)S(1)} %pad_maximum_fusion.4), channel_id=1, source_target_pairs={{0,2},{2,0},{1,3},{3,1},{4,6},{6,4},{5,7},{7,5},{8,10},{10,8},{9,1... | collective-permute-start | bytes 3080 | tf_op jit(solution)/shard_map/ppermute | solution.py:170
  23.1 1.3 %copy-start = (f32[512]{0:T(512)S(1)}, f32[512]{0:T(512)}, u32[]{:S(2)}) copy-start(f32[512]{0:T(512)} %param.12) | copy-start | bytes 6148
  23.1 1.3 %copy-start.1 = (f32[512]{0:T(512)S(1)}, f32[512]{0:T(512)}, u32[]{:S(2)}) copy-start(f32[512]{0:T(512)} %param.11) | copy-start | bytes 6148
  23.1 1.2 collective-permute-start.3
  36.7 8.3 %collective-permute-start.4 = (bf16[512,256]{1,0:T(8,128)(2,1)S(1)}, bf16[512,256]{1,0:T(8,128)(2,1)S(1)}, u32[]{:S(2)}, u32[]{:S(2)}) collective-permute-start(bf16[512,256]{1,0:T(8,128)(2,1)S(1)} %pad_maximum_fusion.1), channel_id=1, source_target_pairs={{0,16},{16,0},{1,17},{17,1},{2,18},{18,2},{3,19},{19,3},{4,20},{20... | collective-permute-start | bytes 786440 | tf_op jit(solution)/shard_map/ppermute | solution.py:201
  45.9 12.1 %collective-permute-start.8 = (bf16[1024,256]{1,0:T(8,128)(2,1)S(1)}, bf16[1024,256]{1,0:T(8,128)(2,1)S(1)}, u32[]{:S(2)}, u32[]{:S(2)}) collective-permute-start(bf16[1024,256]{1,0:T(8,128)(2,1)S(1)} %get-tuple-element.10), channel_id=1, source_target_pairs={{0,32},{32,64},{64,96},{96,128},{128,160},{160,192},{192,224},{224... | collective-permute-start | bytes 1572872 | tf_op jit(solution)/shard_map/ppermute | solution.py:131
  49.0 12.7 %collective-permute-start.5 = (bf16[1024,256]{1,0:T(8,128)(2,1)S(1)}, bf16[1024,256]{1,0:T(8,128)(2,1)S(1)}, u32[]{:S(2)}, u32[]{:S(2)}) collective-permute-start(bf16[1024,256]{1,0:T(8,128)(2,1)S(1)} %get-tuple-element.10), channel_id=1, source_target_pairs={{0,224},{32,0},{64,32},{96,64},{128,96},{160,128},{192,160},{224,1... | collective-permute-start | bytes 1572872 | tf_op jit(solution)/shard_map/ppermute | solution.py:132
  58.0 12.1 %collective-permute-start.9 = (bf16[1024,256]{1,0:T(8,128)(2,1)S(1)}, bf16[1024,256]{1,0:T(8,128)(2,1)S(1)}, u32[]{:S(2)}, u32[]{:S(2)}) collective-permute-start(bf16[1024,256]{1,0:T(8,128)(2,1)S(1)} %collective-permute-done.8), channel_id=1, source_target_pairs={{0,32},{32,64},{64,96},{96,128},{128,160},{160,192},{192,224},{224... | collective-permute-start | bytes 1572872 | tf_op jit(solution)/shard_map/ppermute | solution.py:131
  61.7 12.1 %collective-permute-start.6 = (bf16[1024,256]{1,0:T(8,128)(2,1)S(1)}, bf16[1024,256]{1,0:T(8,128)(2,1)S(1)}, u32[]{:S(2)}, u32[]{:S(2)}) collective-permute-start(bf16[1024,256]{1,0:T(8,128)(2,1)S(1)} %collective-permute-done.5), channel_id=1, source_target_pairs={{0,224},{32,0},{64,32},{96,64},{128,96},{160,128},{192,160},{224,1... | collective-permute-start | bytes 1572872 | tf_op jit(solution)/shard_map/ppermute | solution.py:132
  70.1 16.5 %collective-permute-start.10 = (bf16[1024,256]{1,0:T(8,128)(2,1)S(1)}, bf16[1024,256]{1,0:T(8,128)(2,1)S(1)}, u32[]{:S(2)}, u32[]{:S(2)}) collective-permute-start(bf16[1024,256]{1,0:T(8,128)(2,1)S(1)} %collective-permute-done.9), channel_id=1, source_target_pairs={{0,32},{32,64},{64,96},{96,128},{128,160},{160,192},{192,224},{224... | collective-permute-start | bytes 1572872 | tf_op jit(solution)/shard_map/ppermute | solution.py:131
  73.8 17.1 %collective-permute-start.7 = (bf16[1024,256]{1,0:T(8,128)(2,1)S(1)}, bf16[1024,256]{1,0:T(8,128)(2,1)S(1)}, u32[]{:S(2)}, u32[]{:S(2)}) collective-permute-start(bf16[1024,256]{1,0:T(8,128)(2,1)S(1)} %collective-permute-done.6), channel_id=1, source_target_pairs={{0,224},{32,0},{64,32},{96,64},{128,96},{160,128},{192,160},{224,1... | collective-permute-start | bytes 1572872 | tf_op jit(solution)/shard_map/ppermute | solution.py:132
  86.6 7.4 %collective-permute-start.11 = (bf16[512,256]{1,0:T(8,128)(2,1)S(1)}, bf16[512,256]{1,0:T(8,128)(2,1)S(1)}, u32[]{:S(2)}, u32[]{:S(2)}) collective-permute-start(bf16[512,256]{1,0:T(8,128)(2,1)S(1)} %slice.130), channel_id=1, source_target_pairs={{0,32},{32,64},{64,96},{96,128},{128,160},{160,192},{192,224},{224... | collective-permute-start | bytes 786440 | tf_op jit(solution)/shard_map/ppermute | solution.py:135
  90.9 7.7 %collective-permute-start.12 = (bf16[512,256]{1,0:T(8,128)(2,1)S(1)}, bf16[512,256]{1,0:T(8,128)(2,1)S(1)}, u32[]{:S(2)}, u32[]{:S(2)}) collective-permute-start(bf16[512,256]{1,0:T(8,128)(2,1)S(1)} %slice.131), channel_id=1, source_target_pairs={{0,224},{32,0},{64,32},{96,64},{128,96},{160,128},{192,160},{224,1... | collective-permute-start | bytes 786440 | tf_op jit(solution)/shard_map/ppermute | solution.py:136

commit v5 on v4

--- a/solution.py
+++ b/solution.py
@@ -135,7 +135,7 @@
             far_a = lax.ppermute(fwd[-1][:cut], "z", [(i, (i + 1) % n) for i in range(n)])
             far_b = lax.ppermute(bwd[-1][cut:], "z", [(i, (i - 1) % n) for i in range(n)])
     ordered = bwd[: steps] + [far_a, far_b] + fwd[1:steps][::-1]
-    return jnp.concatenate(ordered, axis=0)
+    return ordered
 
 
 def per_device(hidden_in, w_query, w_key, w_value, query_gain, key_gain, prompt_lengths):
@@ -182,25 +182,26 @@
     key_rot = rotate(key_normed, position)
 
     packed = jnp.concatenate(
-        [
-            query_rot.reshape(tok_rows, head_count, HD),
-            key_rot.reshape(tok_rows, head_count, HD),
-            values.reshape(tok_rows, head_count, HD),
-        ],
-        axis=2,
-    )
-    got = lax.all_to_all(packed, CL, split_axis=1, concat_axis=0, tiled=True)
-    got = got.reshape(ncl, tok_rows, 3 * HD)
-    lower = got[:, :half_rows].reshape(ncl * half_rows, 3 * HD)
-    upper = got[::-1, half_rows:].reshape(ncl * half_rows, 3 * HD)
-    mine = jnp.concatenate([lower, upper], axis=0)
-    q_head = mine[:, :HD]
-    kv_mine = mine[:, HD:]
+        [key_rot.reshape(tok_rows, head_count, HD), values.reshape(tok_rows, head_count, HD)], axis=2
+    )
+
+    def head_split(per_head):
+        width = per_head.shape[2]
+        got = lax.all_to_all(per_head, CL, split_axis=1, concat_axis=0, tiled=True)
+        got = got.reshape(ncl, tok_rows, width)
+        lower = got[:, :half_rows].reshape(ncl * half_rows, width)
+        upper = got[::-1, half_rows:].reshape(ncl * half_rows, width)
+        return jnp.concatenate([lower, upper], axis=0)
+
+    kv_mine = head_split(packed)
 
     yh = lax.axis_index("yhi")
     kv_other = lax.ppermute(kv_mine, "yhi", swap)
     kv_pair = jnp.where(yh == 0, jnp.concatenate([kv_mine, kv_other], axis=0), jnp.concatenate([kv_other, kv_mine], axis=0))
-    kv_all = z_ring(kv_pair, nz)
+    ring_parts = z_ring(kv_pair, nz)
+    q_late, _ = lax.optimization_barrier((query_rot, ring_parts[1]))
+    q_head = head_split(q_late.reshape(tok_rows, head_count, HD))
+    kv_all = jnp.concatenate(ring_parts, axis=0)
 
     span = ncl * half_rows
     total_tokens = 2 * ctx_count * half_rows

time: 130 us -> 136 us (1.046)
  waiting for transfers between devices: 36.8 us -> 40.8 us
  starting transfers between devices: 23.6 us -> 27.1 us
  blocking collectives: 20.8 us -> 18.4 us
  Pallas kernels: 11.7 us -> 13.2 us
    all_to_all x0 -> x1, waiting for transfers between devices: none -> 4.18 us  [head_split(): got = lax.all_to_all(per_head, CL, split_axis=1, concat_axis=0, tiled=True)]
    all_to_all x0 -> x1, starting transfers between devices: none -> 3.66 us  [head_split(): got = lax.all_to_all(per_head, CL, split_axis=1, concat_axis=0, tiled=True)]
    dot_general x1, matrix products: 3.14 us -> 0.8 us  [per_device(): queries = jnp.dot(pieces, w_query, preferred_element_type=jnp.float32)]
    dot_general x1, matrix products: 0.8 us -> 3.14 us  [per_device(): keys_proj = jnp.dot(pieces, w_key, preferred_element_type=jnp.float32)]
    pallas_call x1, Pallas kernels: 11.7 us -> 13.2 us  [attention(): pl.pallas_call(attn_kernel, out_shape=jax.ShapeDtypeStruct((rows, HD), jn...]
    concatenate x1 -> x4, other arithmetic: 0.02 us -> 1.49 us  [the longest x2 0.68 us: head_split(): return jnp.concatenate([lower, upper], axis=0)]
    all_to_all x1, blocking collectives: 11 us -> 9.61 us  [head_split(): got = lax.all_to_all(per_head, CL, split_axis=1, concat_axis=0, tiled=True)]
    unnamed x20 -> x18, local copies, waits for them, and re-layouts: 8.29 us -> 8.3 us
  transfers between devices with their start and end apart: 13 -> 14, of which waited for: 9 -> 10; matrix products, arithmetic and copies ran while one was open for 11% -> 11% of each run, Pallas kernels for 0% -> 0%
where the time goes in v5:
time: 136 us; the launch traced here: 135 us
  waiting for transfers between devices  40.8 us (30%)
  starting transfers between devices  27.1 us (20%)
  local copies, waits for them, and re-layouts  19.2 us (14%)
  blocking collectives  18.4 us (14%)
  Pallas kernels  13.2 us (10%)
  other arithmetic  6.31 us (5%)
  between operations  5.53 us (4%)
  matrix products  4.66 us (3%)
    ppermute x3, waiting for transfers between devices, z_ring(): fwd.append(lax.ppermute(fwd[-1], 'z', [(i, (i + 1) % n) for i in range(n)]))  17.1 us
    pallas_call x1, Pallas kernels, attention(): pl.pallas_call(attn_kernel, out_shape=jax.ShapeDtypeStruct((rows, HD), jn...  13.2 us
    ppermute x3, starting transfers between devices, z_ring(): fwd.append(lax.ppermute(fwd[-1], 'z', [(i, (i + 1) % n) for i in range(n)]))  10.5 us
    all_to_all x1, blocking collectives, head_split(): got = lax.all_to_all(per_head, CL, split_axis=1, concat_axis=0, tiled=True)  9.61 us
    all_to_all x1, blocking collectives, per_device(): recv = lax.all_to_all(send, CL, split_axis=0, concat_axis=0, tiled=True)  8.82 us
    unnamed x18, local copies, waits for them, and re-layouts  8.3 us
    ppermute x1, waiting for transfers between devices, per_device(): kv_other = lax.ppermute(kv_mine, 'yhi', swap)  5.23 us
    ppermute x1, waiting for transfers between devices, per_device(): across = lax.ppermute(hidden_in, 'xhi', swap)  5.07 us
  transfers between devices with their start and end apart: 14, of which 10 were waited for; matrix products, arithmetic and copies ran while one was open for 11% of the time, Pallas kernels for 0%

profile of v5, /device:TPU:96, one launch (start us, length us, event | category | flops | bytes accessed | tf_op | source)
XLA Modules:
  0.0 135.2 jit_solution(12817828650809285798)
XLA Ops:
  0.6 3.1 %collective-permute-start = (bf16[128,1024]{1,0:T(8,128)(2,1)}, bf16[128,1024]{1,0:T(8,128)(2,1)S(1)}, u32[]{:S(2)}, u32[]{:S(2)}) collective-permute-start(bf16[128,1024]{1,0:T(8,128)(2,1)} %param.7), channel_id=1, source_target_pairs={{0,2},{2,0},{1,3},{3,1},{4,6},{6,4},{5,7},{7,5},{8,10},{10,8},{9,1... | collective-permute-start | bytes 786440 | tf_op jit(solution)/shard_map/ppermute | solution.py:159
  5.4 5.1 %collective-permute-done = bf16[128,1024]{1,0:T(8,128)(2,1)S(1)} collective-permute-done((bf16[128,1024]{1,0:T(8,128)(2,1)}, bf16[128,1024]{1,0:T(8,128)(2,1)S(1)}, u32[]{:S(2)}, u32[]{:S(2)}) %collective-permute-start) | collective-permute-done | bytes 262176 | tf_op jit(solution)/shard_map/ppermute | solution.py:159
  10.5 1.2 maximum_select_fusion.1
  11.8 1.8 %collective-permute-done.1 = bf16[128,2048]{1,0:T(8,128)(2,1)S(1)} collective-permute-done((bf16[128,2048]{1,0:T(8,128)(2,1)S(1)}, bf16[128,2048]{1,0:T(8,128)(2,1)S(1)}, u32[]{:S(2)}, u32[]{:S(2)}) %collective-permute-start.1) | collective-permute-done | bytes 524320 | tf_op jit(solution)/shard_map/ppermute | solution.py:161
  13.7 3.1 %multiply_reduce_fusion = (f32[128]{0:T(128)S(1)}, f32[128,512]{1,0:T(8,128)S(1)}) fusion(bf16[4096,512]{1,0:T(8,128)(2,1)} %param.9, bf16[128,1024]{1,0:T(8,128)(2,1)S(1)} %get-tuple-element.16, bf16[128,1024]{1,0:T(8,128)(2,1)S(1)} %get-tuple-element.14, bf16[128,1024]{1,0:T(8,128)(2,1)S(1)} %get-tuple-element.15, ...), kind=kOutput, calls=%fused_computation.14 | convolution fusion | flops 545914752 | bytes 5505537 | tf_op jit(solution)/shard_map/dot_general | solution.py:167
  17.9 3.1 %collective-permute-start.2 = (f32[2,128]{1,0:T(2,128)S(1)}, f32[2,128]{1,0:T(2,128)S(1)}, u32[]{:S(2)}, u32[]{:S(2)}) collective-permute-start(f32[2,128]{1,0:T(2,128)S(1)} %pad_maximum_fusion.6), channel_id=1, source_target_pairs={{0,2},{2,0},{1,3},{3,1},{4,6},{6,4},{5,7},{7,5},{8,10},{10,8},{9,1... | collective-permute-start | bytes 3080 | tf_op jit(solution)/shard_map/ppermute | solution.py:170
  21.2 1.9 %collective-permute-done.2 = f32[2,128]{1,0:T(2,128)S(1)} collective-permute-done((f32[2,128]{1,0:T(2,128)S(1)}, f32[2,128]{1,0:T(2,128)S(1)}, u32[]{:S(2)}, u32[]{:S(2)}) %collective-permute-start.2) | collective-permute-done | bytes 1056 | tf_op jit(solution)/shard_map/ppermute | solution.py:170
  25.3 9.6 %all_to_all.35 = bf16[128,4,256]{2,0,1:T(8,128)(2,1)S(1)} all-to-all(bf16[128,4,256]{2,0,1:T(8,128)(2,1)S(1)} %pad_maximum_fusion.1), channel_id=1, replica_groups=mesh['z'=8,'yhi'=2,'ylo'=2,'xlo'=2,'xhi'=2,'core'=2] {'ylo','xlo'}, dimensions={1} | all-to-all | bytes 524288 | tf_op jit(solution)/shard_map/all_to_all | solution.py:190
  35.0 3.0 %collective-permute-start.4 = (bf16[512,256]{1,0:T(8,128)(2,1)S(1)}, bf16[512,256]{1,0:T(8,128)(2,1)S(1)}, u32[]{:S(2)}, u32[]{:S(2)}) collective-permute-start(bf16[512,256]{1,0:T(8,128)(2,1)S(1)} %pad_maximum_fusion.2), channel_id=1, source_target_pairs={{0,16},{16,0},{1,17},{17,1},{2,18},{18,2},{3,19},{19,3},{4,20},{20... | collective-permute-start | bytes 786440 | tf_op jit(solution)/shard_map/ppermute | solution.py:199
  38.0 5.2 %collective-permute-done.4 = bf16[512,256]{1,0:T(8,128)(2,1)S(1)} collective-permute-done((bf16[512,256]{1,0:T(8,128)(2,1)S(1)}, bf16[512,256]{1,0:T(8,128)(2,1)S(1)}, u32[]{:S(2)}, u32[]{:S(2)}) %collective-permute-start.4) | collective-permute-done | bytes 262176 | tf_op jit(solution)/shard_map/ppermute | solution.py:199
  44.2 3.1 %collective-permute-start.8 = (bf16[1024,256]{1,0:T(8,128)(2,1)S(1)}, bf16[1024,256]{1,0:T(8,128)(2,1)S(1)}, u32[]{:S(2)}, u32[]{:S(2)}) collective-permute-start(bf16[1024,256]{1,0:T(8,128)(2,1)S(1)} %get-tuple-element.12), channel_id=1, source_target_pairs={{0,32},{32,64},{64,96},{96,128},{128,160},{160,192},{192,224},{224... | collective-permute-start | bytes 1572872 | tf_op jit(solution)/shard_map/ppermute | solution.py:131
  47.3 8.9 %collective-permute-done.8 = bf16[1024,256]{1,0:T(8,128)(2,1)S(1)} collective-permute-done((bf16[1024,256]{1,0:T(8,128)(2,1)S(1)}, bf16[1024,256]{1,0:T(8,128)(2,1)S(1)}, u32[]{:S(2)}, u32[]{:S(2)}) %collective-permute-start.8) | collective-permute-done | bytes 524320 | tf_op jit(solution)/shard_map/ppermute | solution.py:131
  56.2 3.7 %collective-permute-start.9 = (bf16[1024,256]{1,0:T(8,128)(2,1)S(1)}, bf16[1024,256]{1,0:T(8,128)(2,1)S(1)}, u32[]{:S(2)}, u32[]{:S(2)}) collective-permute-start(bf16[1024,256]{1,0:T(8,128)(2,1)S(1)} %collective-permute-done.8), channel_id=1, source_target_pairs={{0,32},{32,64},{64,96},{96,128},{128,160},{160,192},{192,224},{224... | collective-permute-start | bytes 1572872 | tf_op jit(solution)/shard_map/ppermute | solution.py:131
  60.1 8.2 %collective-permute-done.9 = bf16[1024,256]{1,0:T(8,128)(2,1)S(1)} collective-permute-done((bf16[1024,256]{1,0:T(8,128)(2,1)S(1)}, bf16[1024,256]{1,0:T(8,128)(2,1)S(1)}, u32[]{:S(2)}, u32[]{:S(2)}) %collective-permute-start.9) | collective-permute-done | bytes 524320 | tf_op jit(solution)/shard_map/ppermute | solution.py:131
  68.3 3.7 %collective-permute-start.10 = (bf16[1024,256]{1,0:T(8,128)(2,1)S(1)}, bf16[1024,256]{1,0:T(8,128)(2,1)S(1)}, u32[]{:S(2)}, u32[]{:S(2)}) collective-permute-start(bf16[1024,256]{1,0:T(8,128)(2,1)S(1)} %collective-permute-done.9), channel_id=1, source_target_pairs={{0,32},{32,64},{64,96},{96,128},{128,160},{160,192},{192,224},{224... | collective-permute-start | bytes 1572872 | tf_op jit(solution)/shard_map/ppermute | solution.py:131
  79.9 3.1 %stack.38.info_ref = s32[10]{0:T(128)} concatenate(s32[1]{0:T(128)} %bitcast.3, s32[1]{0:T(128)} %bitcast.4, s32[1]{0:T(128)} %bitcast.6, s32[1]{0:T(128)} %bitcast.7, s32[1]{0:T(128)} %bitcast.8, s32[1]{0:T(128)} %constant.103.clone.1, s32[1]{0:T(128)} %slice.93, s32[1]{0:T(128)} %get-tuple-element.35, s32[1]{0:T(128)} %slice.95, s32[1]{0:T(128)} %get-tuple-element.34), dimensions={0} | concatenate | bytes 80 | tf_op jit(solution)/shard_map/stack | solution.py:211
  83.7 3.7 %all-to-all-start.1 = ((bf16[128,4,128]{0,2,1:T(8,128)(2,1)}), bf16[128,4,128]{0,2,1:T(8,128)(2,1)S(1)}, u32[]{:S(2)}, u32[]{:S(2)}) async-start(bf16[128,4,128]{0,2,1:T(8,128)(2,1)} %bitcast.21), calls=%async_computation.1 | async-start | bytes 262144 | tf_op jit(solution)/shard_map/all_to_all | solution.py:190
  88.2 4.2 %all-to-all-done.1 = bf16[128,4,128]{0,2,1:T(8,128)(2,1)S(1)} async-done(((bf16[128,4,128]{0,2,1:T(8,128)(2,1)}), bf16[128,4,128]{0,2,1:T(8,128)(2,1)S(1)}, u32[]{:S(2)}, u32[]{:S(2)}) %all-to-all-start.1) | async-done | bytes 131104 | tf_op jit(solution)/shard_map/all_to_all | solution.py:190
  92.8 3.5 %collective-permute-start.11 = (bf16[512,256]{1,0:T(8,128)(2,1)S(1)}, bf16[512,256]{1,0:T(8,128)(2,1)S(1)}, u32[]{:S(2)}, u32[]{:S(2)}) collective-permute-start(bf16[512,256]{1,0:T(8,128)(2,1)S(1)} %slice.132), channel_id=1, source_target_pairs={{0,32},{32,64},{64,96},{96,128},{128,160},{160,192},{192,224},{224... | collective-permute-start | bytes 786440 | tf_op jit(solution)/shard_map/ppermute | solution.py:135
  98.8 1.4 %collective-permute-done.11 = bf16[512,256]{1,0:T(8,128)(2,1)S(1)} collective-permute-done((bf16[512,256]{1,0:T(8,128)(2,1)S(1)}, bf16[512,256]{1,0:T(8,128)(2,1)S(1)}, u32[]{:S(2)}, u32[]{:S(2)}) %collective-permute-start.11) | collective-permute-done | bytes 262176 | tf_op jit(solution)/shard_map/ppermute | solution.py:135
  100.9 3.7 %collective-permute-done.12 = bf16[512,256]{1,0:T(8,128)(2,1)S(1)} collective-permute-done((bf16[512,256]{1,0:T(8,128)(2,1)S(1)}, bf16[512,256]{1,0:T(8,128)(2,1)S(1)}, u32[]{:S(2)}, u32[]{:S(2)}) %collective-permute-start.12) | collective-permute-done | bytes 262176 | tf_op jit(solution)/shard_map/ppermute | solution.py:136
  107.8 1.2 constant_dynamic-slice_fusion
  109.5 13.2 %shard_map.94 = bf16[512,128]{1,0:T(8,128)(2,1)} custom-call(s32[10]{0:T(128)} %stack.38.info_ref, bf16[512,128]{1,0:T(8,128)(2,1)} %pad_maximum_fusion.4.q_ref, bf16[8192,256]{1,0:T(8,128)(2,1)} %constant_dynamic-update-slice_fusion.kv_ref, s32[512,1]{1,0:T(8,128)} %copy.69.qtok_ref, s32[512,1]{1,0:T(8,128)} %copy.70.qlo_ref), custom_call_target="tpu_custom_call" | custom-call | tf_op jit(solution)/shard_map/pallas_call | solution.py:108
  123.8 8.8 %all_to_all.36 = bf16[4,128,384]{2,1,0:T(8,128)(2,1)S(1)} all-to-all(bf16[4,128,384]{2,1,0:T(8,128)(2,1)S(1)} %pad_maximum_fusion), channel_id=1, replica_groups=mesh['z'=8,'yhi'=2,'ylo'=2,'xlo'=2,'xhi'=2,'core'=2] {'ylo','xlo'}, dimensions={0} | all-to-all | bytes 786432 | tf_op jit(solution)/shard_map/all_to_all | solution.py:239
  (87 shorter events, 22.2 us)
Async XLA Ops:
  0.6 9.8 %collective-permute-start = (bf16[128,1024]{1,0:T(8,128)(2,1)}, bf16[128,1024]{1,0:T(8,128)(2,1)S(1)}, u32[]{:S(2)}, u32[]{:S(2)}) collective-permute-start(bf16[128,1024]{1,0:T(8,128)(2,1)} %param.7), channel_id=1, source_target_pairs={{0,2},{2,0},{1,3},{3,1},{4,6},{6,4},{5,7},{7,5},{8,10},{10,8},{9,1... | collective-permute-start | bytes 786440 | tf_op jit(solution)/shard_map/ppermute | solution.py:159
  11.6 2.0 %collective-permute-start.1 = (bf16[128,2048]{1,0:T(8,128)(2,1)S(1)}, bf16[128,2048]{1,0:T(8,128)(2,1)S(1)}, u32[]{:S(2)}, u32[]{:S(2)}) collective-permute-start(bf16[128,2048]{1,0:T(8,128)(2,1)S(1)} %maximum_select_fusion.1), channel_id=1, source_target_pairs={{0,1},{1,0},{2,3},{3,2},{4,5},{5,4},{6,7},{7,6},{8,9},{9,8},{10,11... | collective-permute-start | bytes 1572872 | tf_op jit(solution)/shard_map/ppermute | solution.py:161
  13.7 3.5 %copy-start.2 = (bf16[4096,512]{1,0:T(8,128)(2,1)S(1)}, bf16[4096,512]{1,0:T(8,128)(2,1)}, u32[]{:S(2)}) copy-start(bf16[4096,512]{1,0:T(8,128)(2,1)} %param.8) | copy-start | bytes 12582916
  17.1 6.1 %copy-start.3 = (bf16[4096,512]{1,0:T(8,128)(2,1)S(1)}, bf16[4096,512]{1,0:T(8,128)(2,1)}, u32[]{:S(2)}) copy-start(bf16[4096,512]{1,0:T(8,128)(2,1)} %param.10) | copy-start | bytes 12582916
  17.9 5.2 %collective-permute-start.2 = (f32[2,128]{1,0:T(2,128)S(1)}, f32[2,128]{1,0:T(2,128)S(1)}, u32[]{:S(2)}, u32[]{:S(2)}) collective-permute-start(f32[2,128]{1,0:T(2,128)S(1)} %pad_maximum_fusion.6), channel_id=1, source_target_pairs={{0,2},{2,0},{1,3},{3,1},{4,6},{6,4},{5,7},{7,5},{8,10},{10,8},{9,1... | collective-permute-start | bytes 3080 | tf_op jit(solution)/shard_map/ppermute | solution.py:170
  23.1 1.3 copy-start
  23.1 1.3 copy-start.1
  23.1 1.2 collective-permute-start.3
  35.0 8.2 %collective-permute-start.4 = (bf16[512,256]{1,0:T(8,128)(2,1)S(1)}, bf16[512,256]{1,0:T(8,128)(2,1)S(1)}, u32[]{:S(2)}, u32[]{:S(2)}) collective-permute-start(bf16[512,256]{1,0:T(8,128)(2,1)S(1)} %pad_maximum_fusion.2), channel_id=1, source_target_pairs={{0,16},{16,0},{1,17},{17,1},{2,18},{18,2},{3,19},{19,3},{4,20},{20... | collective-permute-start | bytes 786440 | tf_op jit(solution)/shard_map/ppermute | solution.py:199
  44.2 12.0 %collective-permute-start.8 = (bf16[1024,256]{1,0:T(8,128)(2,1)S(1)}, bf16[1024,256]{1,0:T(8,128)(2,1)S(1)}, u32[]{:S(2)}, u32[]{:S(2)}) collective-permute-start(bf16[1024,256]{1,0:T(8,128)(2,1)S(1)} %get-tuple-element.12), channel_id=1, source_target_pairs={{0,32},{32,64},{64,96},{96,128},{128,160},{160,192},{192,224},{224... | collective-permute-start | bytes 1572872 | tf_op jit(solution)/shard_map/ppermute | solution.py:131
  47.3 12.6 %collective-permute-start.5 = (bf16[1024,256]{1,0:T(8,128)(2,1)S(1)}, bf16[1024,256]{1,0:T(8,128)(2,1)S(1)}, u32[]{:S(2)}, u32[]{:S(2)}) collective-permute-start(bf16[1024,256]{1,0:T(8,128)(2,1)S(1)} %get-tuple-element.12), channel_id=1, source_target_pairs={{0,224},{32,0},{64,32},{96,64},{128,96},{160,128},{192,160},{224,1... | collective-permute-start | bytes 1572872 | tf_op jit(solution)/shard_map/ppermute | solution.py:132
  56.2 12.1 %collective-permute-start.9 = (bf16[1024,256]{1,0:T(8,128)(2,1)S(1)}, bf16[1024,256]{1,0:T(8,128)(2,1)S(1)}, u32[]{:S(2)}, u32[]{:S(2)}) collective-permute-start(bf16[1024,256]{1,0:T(8,128)(2,1)S(1)} %collective-permute-done.8), channel_id=1, source_target_pairs={{0,32},{32,64},{64,96},{96,128},{128,160},{160,192},{192,224},{224... | collective-permute-start | bytes 1572872 | tf_op jit(solution)/shard_map/ppermute | solution.py:131
  59.9 23.1 %collective-permute-start.6 = (bf16[1024,256]{1,0:T(8,128)(2,1)S(1)}, bf16[1024,256]{1,0:T(8,128)(2,1)S(1)}, u32[]{:S(2)}, u32[]{:S(2)}) collective-permute-start(bf16[1024,256]{1,0:T(8,128)(2,1)S(1)} %collective-permute-done.5), channel_id=1, source_target_pairs={{0,224},{32,0},{64,32},{96,64},{128,96},{160,128},{192,160},{224,1... | collective-permute-start | bytes 1572872 | tf_op jit(solution)/shard_map/ppermute | solution.py:132
  68.3 24.5 %collective-permute-start.10 = (bf16[1024,256]{1,0:T(8,128)(2,1)S(1)}, bf16[1024,256]{1,0:T(8,128)(2,1)S(1)}, u32[]{:S(2)}, u32[]{:S(2)}) collective-permute-start(bf16[1024,256]{1,0:T(8,128)(2,1)S(1)} %collective-permute-done.9), channel_id=1, source_target_pairs={{0,32},{32,64},{64,96},{96,128},{128,160},{160,192},{192,224},{224... | collective-permute-start | bytes 1572872 | tf_op jit(solution)/shard_map/ppermute | solution.py:131
  83.0 13.9 %collective-permute-start.7 = (bf16[1024,256]{1,0:T(8,128)(2,1)S(1)}, bf16[1024,256]{1,0:T(8,128)(2,1)S(1)}, u32[]{:S(2)}, u32[]{:S(2)}) collective-permute-start(bf16[1024,256]{1,0:T(8,128)(2,1)S(1)} %collective-permute-done.6), channel_id=1, source_target_pairs={{0,224},{32,0},{64,32},{96,64},{128,96},{160,128},{192,160},{224,1... | collective-permute-start | bytes 1572872 | tf_op jit(solution)/shard_map/ppermute | solution.py:132
  83.7 8.7 %all-to-all-start.1 = ((bf16[128,4,128]{0,2,1:T(8,128)(2,1)}), bf16[128,4,128]{0,2,1:T(8,128)(2,1)S(1)}, u32[]{:S(2)}, u32[]{:S(2)}) async-start(bf16[128,4,128]{0,2,1:T(8,128)(2,1)} %bitcast.21), calls=%async_computation.1 | async-start | bytes 262144 | tf_op jit(solution)/shard_map/all_to_all | solution.py:190
  92.8 7.4 %collective-permute-start.11 = (bf16[512,256]{1,0:T(8,128)(2,1)S(1)}, bf16[512,256]{1,0:T(8,128)(2,1)S(1)}, u32[]{:S(2)}, u32[]{:S(2)}) collective-permute-start(bf16[512,256]{1,0:T(8,128)(2,1)S(1)} %slice.132), channel_id=1, source_target_pairs={{0,32},{32,64},{64,96},{96,128},{128,160},{160,192},{192,224},{224... | collective-permute-start | bytes 786440 | tf_op jit(solution)/shard_map/ppermute | solution.py:135
  97.0 7.7 %collective-permute-start.12 = (bf16[512,256]{1,0:T(8,128)(2,1)S(1)}, bf16[512,256]{1,0:T(8,128)(2,1)S(1)}, u32[]{:S(2)}, u32[]{:S(2)}) collective-permute-start(bf16[512,256]{1,0:T(8,128)(2,1)S(1)} %slice.133), channel_id=1, source_target_pairs={{0,224},{32,0},{64,32},{96,64},{128,96},{160,128},{192,160},{224,1... | collective-permute-start | bytes 786440 | tf_op jit(solution)/shard_map/ppermute | solution.py:136

commit v6 on v0

--- a/solution.py
+++ b/solution.py
@@ -125,6 +125,10 @@
             far_b = lax.ppermute(bwd[-1][cut:], "z", [(i, (i - 1) % n) for i in range(n)])
     ordered = bwd[: steps] + [far_a, far_b] + fwd[1:steps][::-1]
     return jnp.concatenate(ordered, axis=0)
+
+
+def span_rows(ncl, half_rows):
+    return ncl * half_rows
 
 
 def per_device(hidden_in, w_query, w_key, w_value, query_gain, key_gain, prompt_lengths):
@@ -178,17 +182,16 @@
         ],
         axis=2,
     )
-    got = lax.all_to_all(packed, CL, split_axis=1, concat_axis=0, tiled=True)
-    got = got.reshape(ncl, tok_rows, 3 * HD)
-    lower = got[:, :half_rows].reshape(ncl * half_rows, 3 * HD)
-    upper = got[::-1, half_rows:].reshape(ncl * half_rows, 3 * HD)
-    mine = jnp.concatenate([lower, upper], axis=0)
-    q_head = mine[:, :HD]
-    kv_mine = mine[:, HD:]
-
+    spread = jnp.broadcast_to(packed[:, None], (tok_rows, nyh, head_count, 3 * HD))
+    spread = spread.reshape(tok_rows, nyh * head_count, 3 * HD)
+    got = lax.all_to_all(spread, ("yhi",) + CL, split_axis=1, concat_axis=0, tiled=True)
+    got = got.reshape(nyh, ncl, tok_rows, 3 * HD)
+    lower = got[:, :, :half_rows].reshape(nyh, ncl * half_rows, 3 * HD)
+    upper = got[:, ::-1, half_rows:].reshape(nyh, ncl * half_rows, 3 * HD)
+    both = jnp.concatenate([lower, upper], axis=1)
     yh = lax.axis_index("yhi")
-    kv_other = lax.ppermute(kv_mine, "yhi", swap)
-    kv_pair = jnp.where(yh == 0, jnp.concatenate([kv_mine, kv_other], axis=0), jnp.concatenate([kv_other, kv_mine], axis=0))
+    q_head = lax.dynamic_index_in_dim(both, yh, axis=0, keepdims=False)[:, :HD]
+    kv_pair = both[:, :, HD:].reshape(nyh * 2 * span_rows(ncl, half_rows), 2 * HD)
     kv_all = z_ring(kv_pair, nz)
 
     span = ncl * half_rows

time: 125 us -> 128 us (1.024)
  the two profiles are of different devices: /device:TPU:96 before, /device:TPU:224 now
where the time goes in v6:
time: 128 us; the launch traced here: 130 us
  waiting for transfers between devices  33.6 us (26%)
  blocking collectives  28.1 us (22%)
  local copies, waits for them, and re-layouts  18.5 us (14%)
  Pallas kernels  18 us (14%)
  starting transfers between devices  16.9 us (13%)
  between operations  6.22 us (5%)
  matrix products  4.66 us (4%)
  other arithmetic  4.42 us (3%)
    ppermute x3, waiting for transfers between devices, z_ring(): fwd.append(lax.ppermute(fwd[-1], 'z', [(i, (i + 1) % n) for i in range(n)]))  20.5 us
    all_to_all x1, blocking collectives, per_device(): lax.all_to_all(spread, ('yhi',) + CL, split_axis=1, concat_axis=0, tiled=...  18.4 us
    pallas_call x1, Pallas kernels, attention(): pl.pallas_call(attn_kernel, out_shape=jax.ShapeDtypeStruct((rows, HD), jn...  18 us
    unnamed x23, local copies, waits for them, and re-layouts  10.1 us
    all_to_all x1, blocking collectives, per_device(): recv = lax.all_to_all(send, CL, split_axis=0, concat_axis=0, tiled=True)  9.64 us
    ppermute x1, waiting for transfers between devices, per_device(): across = lax.ppermute(hidden_in, 'xhi', swap)  5.07 us
    ppermute x3, starting transfers between devices, z_ring(): fwd.append(lax.ppermute(fwd[-1], 'z', [(i, (i + 1) % n) for i in range(n)]))  4.28 us
    ppermute x1, waiting for transfers between devices, z_ring(): lax.ppermute(bwd[-1][cut:], 'z', [(i, (i - 1) % n) for i in range(n)])  3.9 us
  transfers between devices with their start and end apart: 12, of which 8 were waited for; matrix products, arithmetic and copies ran while one was open for 9% of the time, Pallas kernels for 0%

profile of v6, /device:TPU:224, one launch (start us, length us, event | category | flops | bytes accessed | tf_op | source)
XLA Modules:
  0.0 130.3 jit_solution(16978033327973694096)
XLA Ops:
  0.6 3.1 %collective-permute-start = (bf16[128,1024]{1,0:T(8,128)(2,1)}, bf16[128,1024]{1,0:T(8,128)(2,1)S(1)}, u32[]{:S(2)}, u32[]{:S(2)}) collective-permute-start(bf16[128,1024]{1,0:T(8,128)(2,1)} %param.7), channel_id=1, source_target_pairs={{0,2},{2,0},{1,3},{3,1},{4,6},{6,4},{5,7},{7,5},{8,10},{10,8},{9,1... | collective-permute-start | bytes 786440 | tf_op jit(solution)/shard_map/ppermute | solution.py:152
  5.4 5.1 %collective-permute-done = bf16[128,1024]{1,0:T(8,128)(2,1)S(1)} collective-permute-done((bf16[128,1024]{1,0:T(8,128)(2,1)}, bf16[128,1024]{1,0:T(8,128)(2,1)S(1)}, u32[]{:S(2)}, u32[]{:S(2)}) %collective-permute-start) | collective-permute-done | bytes 262176 | tf_op jit(solution)/shard_map/ppermute | solution.py:152
  10.5 1.2 maximum_select_fusion.1
  11.8 1.8 %collective-permute-done.1 = bf16[128,2048]{1,0:T(8,128)(2,1)S(1)} collective-permute-done((bf16[128,2048]{1,0:T(8,128)(2,1)S(1)}, bf16[128,2048]{1,0:T(8,128)(2,1)S(1)}, u32[]{:S(2)}, u32[]{:S(2)}) %collective-permute-start.1) | collective-permute-done | bytes 524320 | tf_op jit(solution)/shard_map/ppermute | solution.py:154
  13.7 3.1 %multiply_reduce_fusion.1 = (f32[128]{0:T(128)S(1)}, f32[128,512]{1,0:T(8,128)S(1)}) fusion(bf16[4096,512]{1,0:T(8,128)(2,1)} %param.8, bf16[128,1024]{1,0:T(8,128)(2,1)S(1)} %get-tuple-element.14, bf16[128,1024]{1,0:T(8,128)(2,1)S(1)} %get-tuple-element.12, bf16[128,1024]{1,0:T(8,128)(2,1)S(1)} %get-tuple-element.13, ...), kind=kOutput, calls=%fused_computation.20 | convolution fusion | flops 545914752 | bytes 5505537 | tf_op jit(solution)/shard_map/dot_general | solution.py:159
  17.9 3.1 %collective-permute-start.2 = (f32[2,128]{1,0:T(2,128)S(1)}, f32[2,128]{1,0:T(2,128)S(1)}, u32[]{:S(2)}, u32[]{:S(2)}) collective-permute-start(f32[2,128]{1,0:T(2,128)S(1)} %pad_maximum_fusion.3), channel_id=1, source_target_pairs={{0,2},{2,0},{1,3},{3,1},{4,6},{6,4},{5,7},{7,5},{8,10},{10,8},{9,1... | collective-permute-start | bytes 3080 | tf_op jit(solution)/shard_map/ppermute | solution.py:163
  21.4 1.7 %collective-permute-done.2 = f32[2,128]{1,0:T(2,128)S(1)} collective-permute-done((f32[2,128]{1,0:T(2,128)S(1)}, f32[2,128]{1,0:T(2,128)S(1)}, u32[]{:S(2)}, u32[]{:S(2)}) %collective-permute-start.2) | collective-permute-done | bytes 1056 | tf_op jit(solution)/shard_map/ppermute | solution.py:163
  26.2 18.4 %all_to_all.20 = bf16[128,8,384]{2,0,1:T(8,128)(2,1)S(1)} all-to-all(bf16[128,8,384]{2,0,1:T(8,128)(2,1)S(1)} %bitcast.53), channel_id=1, replica_groups=mesh['z'=8,'yhi'=2,'ylo'=2,'xlo'=2,'xhi'=2,'core'=2] {'yhi','ylo','xlo'}, dimensions={1} | all-to-all | bytes 1572864 | tf_op jit(solution)/shard_map/all_to_all | solution.py:187
  44.9 2.0 %collective-permute-start.4 = (bf16[1024,256]{1,0:T(8,128)(2,1)S(1)}, bf16[1024,256]{1,0:T(8,128)(2,1)S(1)}, u32[]{:S(2)}, u32[]{:S(2)}) collective-permute-start(bf16[1024,256]{1,0:T(8,128)(2,1)S(1)} %bitcast.55), channel_id=1, source_target_pairs={{0,224},{32,0},{64,32},{96,64},{128,96},{160,128},{192,160},{224,1... | collective-permute-start | bytes 1572872 | tf_op jit(solution)/shard_map/ppermute | solution.py:121
  46.9 10.5 %collective-permute-done.7 = bf16[1024,256]{1,0:T(8,128)(2,1)S(1)} collective-permute-done((bf16[1024,256]{1,0:T(8,128)(2,1)S(1)}, bf16[1024,256]{1,0:T(8,128)(2,1)S(1)}, u32[]{:S(2)}, u32[]{:S(2)}) %collective-permute-start.7) | collective-permute-done | bytes 524320 | tf_op jit(solution)/shard_map/ppermute | solution.py:120
  57.4 1.5 %collective-permute-start.8 = (bf16[1024,256]{1,0:T(8,128)(2,1)S(1)}, bf16[1024,256]{1,0:T(8,128)(2,1)S(1)}, u32[]{:S(2)}, u32[]{:S(2)}) collective-permute-start(bf16[1024,256]{1,0:T(8,128)(2,1)S(1)} %collective-permute-done.7), channel_id=1, source_target_pairs={{0,32},{32,64},{64,96},{96,128},{128,160},{160,192},{192,224},{224... | collective-permute-start | bytes 1572872 | tf_op jit(solution)/shard_map/ppermute | solution.py:120
  59.4 9.9 %collective-permute-done.8 = bf16[1024,256]{1,0:T(8,128)(2,1)S(1)} collective-permute-done((bf16[1024,256]{1,0:T(8,128)(2,1)S(1)}, bf16[1024,256]{1,0:T(8,128)(2,1)S(1)}, u32[]{:S(2)}, u32[]{:S(2)}) %collective-permute-start.8) | collective-permute-done | bytes 524320 | tf_op jit(solution)/shard_map/ppermute | solution.py:120
  69.4 2.7 %collective-permute-start.9 = (bf16[1024,256]{1,0:T(8,128)(2,1)S(1)}, bf16[1024,256]{1,0:T(8,128)(2,1)S(1)}, u32[]{:S(2)}, u32[]{:S(2)}) collective-permute-start(bf16[1024,256]{1,0:T(8,128)(2,1)S(1)} %collective-permute-done.8), channel_id=1, source_target_pairs={{0,32},{32,64},{64,96},{96,128},{128,160},{160,192},{192,224},{224... | collective-permute-start | bytes 1572872 | tf_op jit(solution)/shard_map/ppermute | solution.py:120
  78.1 0.9 copy.34.qlo_ref
  79.0 0.9 copy.33.qtok_ref
  82.1 3.5 %collective-permute-start.10 = (bf16[512,256]{1,0:T(8,128)(2,1)S(1)}, bf16[512,256]{1,0:T(8,128)(2,1)S(1)}, u32[]{:S(2)}, u32[]{:S(2)}) collective-permute-start(bf16[512,256]{1,0:T(8,128)(2,1)S(1)} %slice.115), channel_id=1, source_target_pairs={{0,32},{32,64},{64,96},{96,128},{128,160},{160,192},{192,224},{224... | collective-permute-start | bytes 786440 | tf_op jit(solution)/shard_map/ppermute | solution.py:124
  86.5 1.9 %constant_dynamic-update-slice_fusion.6 = bf16[8192,256]{1,0:T(8,128)(2,1)} fusion(bf16[8192,256]{1,0:T(8,128)(2,1)} %constant_dynamic-update-slice_fusion.7, bf16[1024,256]{1,0:T(8,128)(2,1)} %collective-permute-done.5), kind=kLoop, calls=%fused_computation.31 | loop fusion | bytes 1048576
  90.2 3.9 %collective-permute-done.11 = bf16[512,256]{1,0:T(8,128)(2,1)S(1)} collective-permute-done((bf16[512,256]{1,0:T(8,128)(2,1)S(1)}, bf16[512,256]{1,0:T(8,128)(2,1)S(1)}, u32[]{:S(2)}, u32[]{:S(2)}) %collective-permute-start.11) | collective-permute-done | bytes 262176 | tf_op jit(solution)/shard_map/ppermute | solution.py:125
  94.8 0.8 constant_dynamic-update-slice_fusion.2
  95.6 0.9 constant_dynamic-update-slice_fusion.1
  97.3 18.0 %shard_map.94 = bf16[512,128]{1,0:T(8,128)(2,1)} custom-call(s32[6]{0:T(128)} %stack.38.info_ref, bf16[512,128]{1,0:T(8,128)(2,1)} %slice.114.q_ref, bf16[8192,256]{1,0:T(8,128)(2,1)} %constant_dynamic-update-slice_fusion.kv_ref, s32[512,1]{1,0:T(8,128)} %copy.33.qtok_ref, s32[512,1]{1,0:T(8,128)} %copy.34.qlo_ref), custom_call_target="tpu_custom_call" | custom-call | tf_op jit(solution)/shard_map/pallas_call | solution.py:97
  115.3 0.9 fusion.13
  116.2 1.2 constant_dynamic-slice_fusion
  118.1 9.6 %all_to_all.21 = bf16[4,128,384]{2,1,0:T(8,128)(2,1)S(1)} all-to-all(bf16[4,128,384]{2,1,0:T(8,128)(2,1)S(1)} %pad_maximum_fusion.1), channel_id=1, replica_groups=mesh['z'=8,'yhi'=2,'ylo'=2,'xlo'=2,'xhi'=2,'core'=2] {'ylo','xlo'}, dimensions={0} | all-to-all | bytes 786432 | tf_op jit(solution)/shard_map/all_to_all | solution.py:226
  (81 shorter events, 17.4 us)
Async XLA Ops:
  0.6 9.8 %collective-permute-start = (bf16[128,1024]{1,0:T(8,128)(2,1)}, bf16[128,1024]{1,0:T(8,128)(2,1)S(1)}, u32[]{:S(2)}, u32[]{:S(2)}) collective-permute-start(bf16[128,1024]{1,0:T(8,128)(2,1)} %param.7), channel_id=1, source_target_pairs={{0,2},{2,0},{1,3},{3,1},{4,6},{6,4},{5,7},{7,5},{8,10},{10,8},{9,1... | collective-permute-start | bytes 786440 | tf_op jit(solution)/shard_map/ppermute | solution.py:152
  11.6 2.0 %collective-permute-start.1 = (bf16[128,2048]{1,0:T(8,128)(2,1)S(1)}, bf16[128,2048]{1,0:T(8,128)(2,1)S(1)}, u32[]{:S(2)}, u32[]{:S(2)}) collective-permute-start(bf16[128,2048]{1,0:T(8,128)(2,1)S(1)} %maximum_select_fusion.1), channel_id=1, source_target_pairs={{0,1},{1,0},{2,3},{3,2},{4,5},{5,4},{6,7},{7,6},{8,9},{9,8},{10,11... | collective-permute-start | bytes 1572872 | tf_op jit(solution)/shard_map/ppermute | solution.py:154
  13.7 3.5 %copy-start.4 = (bf16[4096,512]{1,0:T(8,128)(2,1)S(1)}, bf16[4096,512]{1,0:T(8,128)(2,1)}, u32[]{:S(2)}) copy-start(bf16[4096,512]{1,0:T(8,128)(2,1)} %param.9) | copy-start | bytes 12582916
  17.1 6.1 %copy-start.5 = (bf16[4096,512]{1,0:T(8,128)(2,1)S(1)}, bf16[4096,512]{1,0:T(8,128)(2,1)}, u32[]{:S(2)}) copy-start(bf16[4096,512]{1,0:T(8,128)(2,1)} %param.10) | copy-start | bytes 12582916
  17.9 5.2 %collective-permute-start.2 = (f32[2,128]{1,0:T(2,128)S(1)}, f32[2,128]{1,0:T(2,128)S(1)}, u32[]{:S(2)}, u32[]{:S(2)}) collective-permute-start(f32[2,128]{1,0:T(2,128)S(1)} %pad_maximum_fusion.3), channel_id=1, source_target_pairs={{0,2},{2,0},{1,3},{3,1},{4,6},{6,4},{5,7},{7,5},{8,10},{10,8},{9,1... | collective-permute-start | bytes 3080 | tf_op jit(solution)/shard_map/ppermute | solution.py:163
  23.1 1.3 copy-start.2
  23.1 1.3 copy-start.3
  23.1 1.2 collective-permute-start.3
  44.8 12.6 %collective-permute-start.7 = (bf16[1024,256]{1,0:T(8,128)(2,1)S(1)}, bf16[1024,256]{1,0:T(8,128)(2,1)S(1)}, u32[]{:S(2)}, u32[]{:S(2)}) collective-permute-start(bf16[1024,256]{1,0:T(8,128)(2,1)S(1)} %bitcast.54), channel_id=1, source_target_pairs={{0,32},{32,64},{64,96},{96,128},{128,160},{160,192},{192,224},{224... | collective-permute-start | bytes 1572872 | tf_op jit(solution)/shard_map/ppermute | solution.py:120
  44.9 14.0 %collective-permute-start.4 = (bf16[1024,256]{1,0:T(8,128)(2,1)S(1)}, bf16[1024,256]{1,0:T(8,128)(2,1)S(1)}, u32[]{:S(2)}, u32[]{:S(2)}) collective-permute-start(bf16[1024,256]{1,0:T(8,128)(2,1)S(1)} %bitcast.55), channel_id=1, source_target_pairs={{0,224},{32,0},{64,32},{96,64},{128,96},{160,128},{192,160},{224,1... | collective-permute-start | bytes 1572872 | tf_op jit(solution)/shard_map/ppermute | solution.py:121
  57.4 12.0 %collective-permute-start.8 = (bf16[1024,256]{1,0:T(8,128)(2,1)S(1)}, bf16[1024,256]{1,0:T(8,128)(2,1)S(1)}, u32[]{:S(2)}, u32[]{:S(2)}) collective-permute-start(bf16[1024,256]{1,0:T(8,128)(2,1)S(1)} %collective-permute-done.7), channel_id=1, source_target_pairs={{0,32},{32,64},{64,96},{96,128},{128,160},{160,192},{192,224},{224... | collective-permute-start | bytes 1572872 | tf_op jit(solution)/shard_map/ppermute | solution.py:120
  58.9 13.3 %copy-start = (bf16[1024,256]{1,0:T(8,128)(2,1)}, bf16[1024,256]{1,0:T(8,128)(2,1)S(1)}, u32[]{:S(2)}) copy-start(bf16[1024,256]{1,0:T(8,128)(2,1)S(1)} %collective-permute-done.4) | copy-start | bytes 1572868
  58.9 13.3 %collective-permute-start.5 = (bf16[1024,256]{1,0:T(8,128)(2,1)S(1)}, bf16[1024,256]{1,0:T(8,128)(2,1)}, u32[]{:S(2)}, u32[]{:S(2)}) collective-permute-start(bf16[1024,256]{1,0:T(8,128)(2,1)S(1)} %collective-permute-done.4), channel_id=1, source_target_pairs={{0,224},{32,0},{64,32},{96,64},{128,96},{160,128},{192,160},{224,1... | collective-permute-start | bytes 1572872 | tf_op jit(solution)/shard_map/ppermute | solution.py:121
  69.4 12.7 %collective-permute-start.9 = (bf16[1024,256]{1,0:T(8,128)(2,1)S(1)}, bf16[1024,256]{1,0:T(8,128)(2,1)S(1)}, u32[]{:S(2)}, u32[]{:S(2)}) collective-permute-start(bf16[1024,256]{1,0:T(8,128)(2,1)S(1)} %collective-permute-done.8), channel_id=1, source_target_pairs={{0,32},{32,64},{64,96},{96,128},{128,160},{160,192},{192,224},{224... | collective-permute-start | bytes 1572872 | tf_op jit(solution)/shard_map/ppermute | solution.py:120
  72.2 14.2 %collective-permute-start.6 = (bf16[1024,256]{1,0:T(8,128)(2,1)}, bf16[1024,256]{1,0:T(8,128)(2,1)S(1)}, u32[]{:S(2)}, u32[]{:S(2)}) collective-permute-start(bf16[1024,256]{1,0:T(8,128)(2,1)} %collective-permute-done.5), channel_id=1, source_target_pairs={{0,224},{32,0},{64,32},{96,64},{128,96},{160,128},{192,160},{224,1... | collective-permute-start | bytes 1572872 | tf_op jit(solution)/shard_map/ppermute | solution.py:121
  80.5 5.0 %copy-start.1 = (bf16[1024,256]{1,0:T(8,128)(2,1)S(1)}, bf16[1024,256]{1,0:T(8,128)(2,1)}, u32[]{:S(2)}) copy-start(bf16[1024,256]{1,0:T(8,128)(2,1)} %copy-done) | copy-start | bytes 1572868
  82.1 7.4 %collective-permute-start.10 = (bf16[512,256]{1,0:T(8,128)(2,1)S(1)}, bf16[512,256]{1,0:T(8,128)(2,1)S(1)}, u32[]{:S(2)}, u32[]{:S(2)}) collective-permute-start(bf16[512,256]{1,0:T(8,128)(2,1)S(1)} %slice.115), channel_id=1, source_target_pairs={{0,32},{32,64},{64,96},{96,128},{128,160},{160,192},{192,224},{224... | collective-permute-start | bytes 786440 | tf_op jit(solution)/shard_map/ppermute | solution.py:124
  86.4 7.7 %collective-permute-start.11 = (bf16[512,256]{1,0:T(8,128)(2,1)S(1)}, bf16[512,256]{1,0:T(8,128)(2,1)S(1)}, u32[]{:S(2)}, u32[]{:S(2)}) collective-permute-start(bf16[512,256]{1,0:T(8,128)(2,1)S(1)} %slice.116), channel_id=1, source_target_pairs={{0,224},{32,0},{64,32},{96,64},{128,96},{160,128},{192,160},{224,1... | collective-permute-start | bytes 786440 | tf_op jit(solution)/shard_map/ppermute | solution.py:125

commit v7 on v0

--- a/solution.py
+++ b/solution.py
@@ -145,16 +145,24 @@
     xh = lax.axis_index("xhi")
     core = lax.axis_index("core")
     swap = [(0, 1), (1, 0)]
+    width = hidden_in.shape[1]
+    ncore = lax.axis_size("core")
+    own_t = xh * ncore + core
+    far_t = (1 - xh) * ncore + core
     across = lax.ppermute(hidden_in, "xhi", swap)
-    pair = jnp.where(xh == 0, jnp.concatenate([hidden_in, across], axis=1), jnp.concatenate([across, hidden_in], axis=1))
+    pair = jnp.concatenate([hidden_in, across], axis=0)
     other = lax.ppermute(pair, "core", swap)
-    width = hidden_in.shape[1]
-    mine_first = jnp.concatenate([pair[:, :width], other[:, :width], pair[:, width:], other[:, width:]], axis=1)
-    theirs_first = jnp.concatenate([other[:, :width], pair[:, :width], other[:, width:], pair[:, width:]], axis=1)
-    pieces = jnp.where(core == 0, mine_first, theirs_first)
-    queries = jnp.dot(pieces, w_query, preferred_element_type=jnp.float32)
-    keys_proj = jnp.dot(pieces, w_key, preferred_element_type=jnp.float32)
-    values = jnp.dot(pieces, w_value, preferred_element_type=jnp.float32).astype(jnp.bfloat16)
+
+    def project(weight):
+        rows_of = lambda t: lax.dynamic_slice_in_dim(weight, t * width, width, axis=0)
+        total = jnp.dot(hidden_in, rows_of(own_t), preferred_element_type=jnp.float32)
+        total = total + jnp.dot(across, rows_of(far_t), preferred_element_type=jnp.float32)
+        total = total + jnp.dot(other[:tok_rows], rows_of(xh * ncore + 1 - core), preferred_element_type=jnp.float32)
+        return total + jnp.dot(other[tok_rows:], rows_of((1 - xh) * ncore + 1 - core), preferred_element_type=jnp.float32)
+
+    queries = project(w_query)
+    keys_proj = project(w_key)
+    values = project(w_value).astype(jnp.bfloat16)
     squares = jnp.stack([jnp.sum(queries * queries, axis=1), jnp.sum(keys_proj * keys_proj, axis=1)])
     squares = squares + lax.ppermute(squares, "xhi", swap)
     squares = squares + lax.ppermute(squares, "core", swap)

time: 125 us -> 128 us (1.024); the launches traced: 123 us -> 127 us
  matrix products: 4.66 us -> 15.1 us
  waiting for transfers between devices: 36.8 us -> 30.8 us
  Pallas kernels: 9.66 us -> 12.8 us
    dot_general x3 -> x12, matrix products: 4.66 us -> 15.1 us  [the longest x3 5.38 us: project(): jnp.dot(hidden_in, rows_of(own_t), preferred_element_type=jnp.float32)]
    ppermute x1, waiting for transfers between devices: 5.07 us -> 0.01 us  [per_device(): across = lax.ppermute(hidden_in, 'xhi', swap)]
    pallas_call x1, Pallas kernels: 9.66 us -> 12.8 us  [attention(): pl.pallas_call(attn_kernel, out_shape=jax.ShapeDtypeStruct((rows, HD), jn...]
    ppermute x1, waiting for transfers between devices: 1.82 us -> 0.01 us  [per_device(): other = lax.ppermute(pair, 'core', swap)]
    unnamed x18 -> x24, local copies, waits for them, and re-layouts: 8.27 us -> 8.49 us
  transfers between devices with their start and end apart: 13 -> 13, of which waited for: 9 -> 7; matrix products, arithmetic and copies ran while one was open for 8% -> 15% of each run, Pallas kernels for 0% -> 0%
where the time goes in v7:
time: 128 us; the launch traced here: 127 us
  waiting for transfers between devices  30.8 us (24%)
  starting transfers between devices  22.6 us (18%)
  blocking collectives  19.8 us (15%)
  local copies, waits for them, and re-layouts  15.3 us (12%)
  matrix products  15.1 us (12%)
  Pallas kernels  12.8 us (10%)
  between operations  6.31 us (5%)
  other arithmetic  4.67 us (4%)
    ppermute x3, waiting for transfers between devices, z_ring(): fwd.append(lax.ppermute(fwd[-1], 'z', [(i, (i + 1) % n) for i in range(n)]))  17.5 us
    pallas_call x1, Pallas kernels, attention(): pl.pallas_call(attn_kernel, out_shape=jax.ShapeDtypeStruct((rows, HD), jn...  12.8 us
    ppermute x3, starting transfers between devices, z_ring(): fwd.append(lax.ppermute(fwd[-1], 'z', [(i, (i + 1) % n) for i in range(n)]))  10.5 us
    all_to_all x1, blocking collectives, per_device(): got = lax.all_to_all(packed, CL, split_axis=1, concat_axis=0, tiled=True)  10.3 us
    all_to_all x1, blocking collectives, per_device(): recv = lax.all_to_all(send, CL, split_axis=0, concat_axis=0, tiled=True)  9.55 us
    unnamed x24, local copies, waits for them, and re-layouts  8.49 us
    dot_general x3, matrix products, project(): jnp.dot(hidden_in, rows_of(own_t), preferred_element_type=jnp.float32)  5.38 us
    ppermute x1, waiting for transfers between devices, per_device(): kv_other = lax.ppermute(kv_mine, 'yhi', swap)  5.27 us
  transfers between devices with their start and end apart: 13, of which 7 were waited for; matrix products, arithmetic and copies ran while one was open for 15% of the time, Pallas kernels for 0%

profile of v7, /device:TPU:96, one launch (start us, length us, event | category | flops | bytes accessed | tf_op | source)
XLA Modules:
  0.0 127.4 jit_solution(11389346690930557748)
XLA Ops:
  0.6 3.1 %collective-permute-start = (bf16[128,1024]{1,0:T(8,128)(2,1)}, bf16[128,1024]{1,0:T(8,128)(2,1)S(1)}, u32[]{:S(2)}, u32[]{:S(2)}) collective-permute-start(bf16[128,1024]{1,0:T(8,128)(2,1)} %param.7), channel_id=1, source_target_pairs={{0,2},{2,0},{1,3},{3,1},{4,6},{6,4},{5,7},{7,5},{8,10},{10,8},{9,1... | collective-permute-start | bytes 786440 | tf_op jit(solution)/shard_map/ppermute | solution.py:152
  3.8 1.7 %fusion.23 = f32[512,128]{1,0:T(8,128)S(1)} fusion(bf16[128,1024]{1,0:T(8,128)(2,1)} %param.7, bf16[4096,512]{1,0:T(8,128)(2,1)} %param.8, s32[]{:T(128)S(6)} %select_n.90), kind=kOutput, calls=%fused_computation.29 | convolution fusion | flops 134217728 | bytes 1572868 | tf_op jit(solution)/shard_map/dot_general | solution.py:158
  5.5 1.7 %fusion.17 = f32[512,128]{1,0:T(8,128)S(1)} fusion(bf16[128,1024]{1,0:T(8,128)(2,1)} %param.7, bf16[4096,512]{1,0:T(8,128)(2,1)} %param.9, s32[]{:T(128)S(6)} %select_n.90), kind=kOutput, calls=%fused_computation.23 | convolution fusion | flops 134217728 | bytes 1572868 | tf_op jit(solution)/shard_map/dot_general | solution.py:158
  9.3 1.9 %fusion.11 = f32[512,128]{1,0:T(8,128)S(1)} fusion(bf16[128,1024]{1,0:T(8,128)(2,1)} %param.7, bf16[4096,512]{1,0:T(8,128)(2,1)} %param.10, s32[]{:T(128)S(6)} %select_n.90), kind=kOutput, calls=%fused_computation.17 | convolution fusion | flops 134217728 | bytes 1572868 | tf_op jit(solution)/shard_map/dot_general | solution.py:158
  11.4 1.9 %fusion.5 = f32[128,512]{0,1:T(8,128)S(1)} fusion(f32[512,128]{1,0:T(8,128)S(1)} %fusion.23, bf16[128,1024]{1,0:T(8,128)(2,1)S(1)} %collective-permute-done, bf16[4096,512]{1,0:T(8,128)(2,1)} %param.8, s32[]{:T(128)S(6)} %select_n.91), kind=kOutput, calls=%fused_computation.11 | convolution fusion | flops 134283264 | bytes 1835012 | tf_op jit(solution)/shard_map/dot_general | solution.py:159
  13.2 1.7 %fusion.3 = f32[128,512]{0,1:T(8,128)S(1)} fusion(f32[512,128]{1,0:T(8,128)S(1)} %fusion.17, bf16[128,1024]{1,0:T(8,128)(2,1)S(1)} %collective-permute-done, bf16[4096,512]{1,0:T(8,128)(2,1)} %param.9, s32[]{:T(128)S(6)} %select_n.91), kind=kOutput, calls=%fused_computation.7 | convolution fusion | flops 134283264 | bytes 1835012 | tf_op jit(solution)/shard_map/dot_general | solution.py:159
  15.4 1.8 %fusion.19 = f32[128,512]{0,1:T(8,128)S(1)} fusion(bf16[4096,512]{1,0:T(8,128)(2,1)} %param.8, s32[]{:T(128)S(6)} %select_n.93, bf16[256,1024]{1,0:T(8,128)(2,1)S(1)} %collective-permute-done.1), kind=kOutput, calls=%fused_computation.25 | convolution fusion | flops 134217728 | bytes 1572868 | tf_op jit(solution)/shard_map/dot_general | solution.py:161
  17.8 1.8 %multiply_reduce_fusion.1 = (f32[128]{0:T(128)S(1)}, f32[128,512]{0,1:T(8,128)S(1)}) fusion(f32[128,512]{0,1:T(8,128)S(1)} %fusion.19, f32[128,512]{0,1:T(8,128)S(1)} %fusion.5, bf16[4096,512]{1,0:T(8,128)(2,1)} %param.8, s32[]{:T(128)S(6)} %select_n.92, bf16[256,1024]{1,0:T(8,128)(2,1)S(1)} %collective-permute-done.1), kind=kOutput, calls=%fused_computation.46 | convolution fusion | flops 134479744 | bytes 2097668 | tf_op jit(solution)/shard_map/dot_general | solution.py:160
  20.1 2.2 %collective-permute-start.2 = (f32[2,128]{1,0:T(2,128)S(1)}, f32[2,128]{1,0:T(2,128)S(1)}, u32[]{:S(2)}, u32[]{:S(2)}) collective-permute-start(f32[2,128]{1,0:T(2,128)S(1)} %pad_maximum_fusion.5), channel_id=1, source_target_pairs={{0,2},{2,0},{1,3},{3,1},{4,6},{6,4},{5,7},{7,5},{8,10},{10,8},{9,1... | collective-permute-start | bytes 3080 | tf_op jit(solution)/shard_map/ppermute | solution.py:167
  22.9 2.4 %collective-permute-done.2 = f32[2,128]{1,0:T(2,128)S(1)} collective-permute-done((f32[2,128]{1,0:T(2,128)S(1)}, f32[2,128]{1,0:T(2,128)S(1)}, u32[]{:S(2)}, u32[]{:S(2)}) %collective-permute-start.2) | collective-permute-done | bytes 1056 | tf_op jit(solution)/shard_map/ppermute | solution.py:167
  27.8 10.3 %all_to_all.20 = bf16[128,4,384]{2,0,1:T(8,128)(2,1)S(1)} all-to-all(bf16[128,4,384]{2,0,1:T(8,128)(2,1)S(1)} %concatenate.37), channel_id=1, replica_groups=mesh['z'=8,'yhi'=2,'ylo'=2,'xlo'=2,'xhi'=2,'core'=2] {'ylo','xlo'}, dimensions={1} | all-to-all | bytes 786432 | tf_op jit(solution)/shard_map/all_to_all | solution.py:189
  38.2 3.1 %collective-permute-start.4 = (bf16[512,256]{1,0:T(8,128)(2,1)S(1)}, bf16[512,256]{1,0:T(8,128)(2,1)S(1)}, u32[]{:S(2)}, u32[]{:S(2)}) collective-permute-start(bf16[512,256]{1,0:T(8,128)(2,1)S(1)} %pad_maximum_fusion.2), channel_id=1, source_target_pairs={{0,16},{16,0},{1,17},{17,1},{2,18},{18,2},{3,19},{19,3},{4,20},{20... | collective-permute-start | bytes 786440 | tf_op jit(solution)/shard_map/ppermute | solution.py:198
  41.3 5.3 %collective-permute-done.4 = bf16[512,256]{1,0:T(8,128)(2,1)S(1)} collective-permute-done((bf16[512,256]{1,0:T(8,128)(2,1)S(1)}, bf16[512,256]{1,0:T(8,128)(2,1)S(1)}, u32[]{:S(2)}, u32[]{:S(2)}) %collective-permute-start.4) | collective-permute-done | bytes 262176 | tf_op jit(solution)/shard_map/ppermute | solution.py:198
  47.5 3.1 %collective-permute-start.8 = (bf16[1024,256]{1,0:T(8,128)(2,1)S(1)}, bf16[1024,256]{1,0:T(8,128)(2,1)S(1)}, u32[]{:S(2)}, u32[]{:S(2)}) collective-permute-start(bf16[1024,256]{1,0:T(8,128)(2,1)S(1)} %get-tuple-element.10), channel_id=1, source_target_pairs={{0,32},{32,64},{64,96},{96,128},{128,160},{160,192},{192,224},{224... | collective-permute-start | bytes 1572872 | tf_op jit(solution)/shard_map/ppermute | solution.py:120
  50.7 9.1 %collective-permute-done.8 = bf16[1024,256]{1,0:T(8,128)(2,1)S(1)} collective-permute-done((bf16[1024,256]{1,0:T(8,128)(2,1)S(1)}, bf16[1024,256]{1,0:T(8,128)(2,1)S(1)}, u32[]{:S(2)}, u32[]{:S(2)}) %collective-permute-start.8) | collective-permute-done | bytes 524320 | tf_op jit(solution)/shard_map/ppermute | solution.py:120
  59.7 3.7 %collective-permute-start.9 = (bf16[1024,256]{1,0:T(8,128)(2,1)S(1)}, bf16[1024,256]{1,0:T(8,128)(2,1)S(1)}, u32[]{:S(2)}, u32[]{:S(2)}) collective-permute-start(bf16[1024,256]{1,0:T(8,128)(2,1)S(1)} %collective-permute-done.8), channel_id=1, source_target_pairs={{0,32},{32,64},{64,96},{96,128},{128,160},{160,192},{192,224},{224... | collective-permute-start | bytes 1572872 | tf_op jit(solution)/shard_map/ppermute | solution.py:120
  63.4 8.4 %collective-permute-done.9 = bf16[1024,256]{1,0:T(8,128)(2,1)S(1)} collective-permute-done((bf16[1024,256]{1,0:T(8,128)(2,1)S(1)}, bf16[1024,256]{1,0:T(8,128)(2,1)S(1)}, u32[]{:S(2)}, u32[]{:S(2)}) %collective-permute-start.9) | collective-permute-done | bytes 524320 | tf_op jit(solution)/shard_map/ppermute | solution.py:120
  71.8 3.7 %collective-permute-start.10 = (bf16[1024,256]{1,0:T(8,128)(2,1)S(1)}, bf16[1024,256]{1,0:T(8,128)(2,1)S(1)}, u32[]{:S(2)}, u32[]{:S(2)}) collective-permute-start(bf16[1024,256]{1,0:T(8,128)(2,1)S(1)} %collective-permute-done.9), channel_id=1, source_target_pairs={{0,32},{32,64},{64,96},{96,128},{128,160},{160,192},{192,224},{224... | collective-permute-start | bytes 1572872 | tf_op jit(solution)/shard_map/ppermute | solution.py:120
  84.6 3.3 %collective-permute-start.11 = (bf16[512,256]{1,0:T(8,128)(2,1)S(1)}, bf16[512,256]{1,0:T(8,128)(2,1)S(1)}, u32[]{:S(2)}, u32[]{:S(2)}) collective-permute-start(bf16[512,256]{1,0:T(8,128)(2,1)S(1)} %slice.104), channel_id=1, source_target_pairs={{0,32},{32,64},{64,96},{96,128},{128,160},{160,192},{192,224},{224... | collective-permute-start | bytes 786440 | tf_op jit(solution)/shard_map/ppermute | solution.py:124
  90.6 1.3 collective-permute-done.11
  92.5 3.9 %collective-permute-done.12 = bf16[512,256]{1,0:T(8,128)(2,1)S(1)} collective-permute-done((bf16[512,256]{1,0:T(8,128)(2,1)S(1)}, bf16[512,256]{1,0:T(8,128)(2,1)S(1)}, u32[]{:S(2)}, u32[]{:S(2)}) %collective-permute-start.12) | collective-permute-done | bytes 262176 | tf_op jit(solution)/shard_map/ppermute | solution.py:125
  99.7 12.8 %shard_map.94 = bf16[512,128]{1,0:T(8,128)(2,1)} custom-call(s32[6]{0:T(128)} %stack.38.info_ref, bf16[512,128]{1,0:T(8,128)(2,1)} %pad_maximum_fusion.3.q_ref, bf16[8192,256]{1,0:T(8,128)(2,1)} %constant_dynamic-update-slice_fusion.kv_ref, s32[512,1]{1,0:T(8,128)} %copy.83.qtok_ref, s32[512,1]{1,0:T(8,128)} %copy.84.qlo_ref), custom_call_target="tpu_custom_call" | custom-call | tf_op jit(solution)/shard_map/pallas_call | solution.py:97
  113.4 1.2 constant_dynamic-slice_fusion
  115.3 9.6 %all_to_all.21 = bf16[4,128,384]{2,1,0:T(8,128)(2,1)S(1)} all-to-all(bf16[4,128,384]{2,1,0:T(8,128)(2,1)S(1)} %pad_maximum_fusion.1), channel_id=1, replica_groups=mesh['z'=8,'yhi'=2,'ylo'=2,'xlo'=2,'xhi'=2,'core'=2] {'ylo','xlo'}, dimensions={0} | all-to-all | bytes 786432 | tf_op jit(solution)/shard_map/all_to_all | solution.py:231
  (89 shorter events, 22.2 us)
Async XLA Ops:
  0.6 10.6 %copy-start.2 = (bf16[128,1024]{1,0:T(8,128)(2,1)S(1)}, bf16[128,1024]{1,0:T(8,128)(2,1)}, u32[]{:S(2)}) copy-start(bf16[128,1024]{1,0:T(8,128)(2,1)} %param.7) | copy-start | bytes 786436
  0.6 10.6 %collective-permute-start = (bf16[128,1024]{1,0:T(8,128)(2,1)}, bf16[128,1024]{1,0:T(8,128)(2,1)S(1)}, u32[]{:S(2)}, u32[]{:S(2)}) collective-permute-start(bf16[128,1024]{1,0:T(8,128)(2,1)} %param.7), channel_id=1, source_target_pairs={{0,2},{2,0},{1,3},{3,1},{4,6},{6,4},{5,7},{7,5},{8,10},{10,8},{9,1... | collective-permute-start | bytes 786440 | tf_op jit(solution)/shard_map/ppermute | solution.py:152
  9.3 5.7 %copy-start = (bf16[4096,512]{1,0:T(8,128)(2,1)S(1)}, bf16[4096,512]{1,0:T(8,128)(2,1)}, u32[]{:S(2)}) copy-start(bf16[4096,512]{1,0:T(8,128)(2,1)} %param.10) | copy-start | bytes 12582916
  11.2 6.0 %copy-start.1 = (bf16[4096,512]{1,0:T(8,128)(2,1)S(1)}, bf16[4096,512]{1,0:T(8,128)(2,1)}, u32[]{:S(2)}) copy-start(bf16[4096,512]{1,0:T(8,128)(2,1)} %param.9) | copy-start | bytes 12582916
  11.3 4.2 %collective-permute-start.1 = (bf16[256,1024]{1,0:T(8,128)(2,1)S(1)}, bf16[256,1024]{1,0:T(8,128)(2,1)S(1)}, u32[]{:S(2)}, u32[]{:S(2)}) collective-permute-start(bf16[256,1024]{1,0:T(8,128)(2,1)S(1)} %pad_maximum_fusion), channel_id=1, source_target_pairs={{0,1},{1,0},{2,3},{3,2},{4,5},{5,4},{6,7},{7,6},{8,9},{9,8},{10,11... | collective-permute-start | bytes 1572872 | tf_op jit(solution)/shard_map/ppermute | solution.py:154
  17.8 8.8 %copy-start.3 = (f32[512]{0:T(512)S(1)}, f32[512]{0:T(512)}, u32[]{:S(2)}) copy-start(f32[512]{0:T(512)} %param.12) | copy-start | bytes 6148
  17.8 8.8 %copy-start.4 = (f32[512]{0:T(512)S(1)}, f32[512]{0:T(512)}, u32[]{:S(2)}) copy-start(f32[512]{0:T(512)} %param.11) | copy-start | bytes 6148
  20.1 5.2 %collective-permute-start.2 = (f32[2,128]{1,0:T(2,128)S(1)}, f32[2,128]{1,0:T(2,128)S(1)}, u32[]{:S(2)}, u32[]{:S(2)}) collective-permute-start(f32[2,128]{1,0:T(2,128)S(1)} %pad_maximum_fusion.5), channel_id=1, source_target_pairs={{0,2},{2,0},{1,3},{3,1},{4,6},{6,4},{5,7},{7,5},{8,10},{10,8},{9,1... | collective-permute-start | bytes 3080 | tf_op jit(solution)/shard_map/ppermute | solution.py:167
  25.3 1.2 collective-permute-start.3
  38.2 8.4 %collective-permute-start.4 = (bf16[512,256]{1,0:T(8,128)(2,1)S(1)}, bf16[512,256]{1,0:T(8,128)(2,1)S(1)}, u32[]{:S(2)}, u32[]{:S(2)}) collective-permute-start(bf16[512,256]{1,0:T(8,128)(2,1)S(1)} %pad_maximum_fusion.2), channel_id=1, source_target_pairs={{0,16},{16,0},{1,17},{17,1},{2,18},{18,2},{3,19},{19,3},{4,20},{20... | collective-permute-start | bytes 786440 | tf_op jit(solution)/shard_map/ppermute | solution.py:198
  47.5 12.2 %collective-permute-start.8 = (bf16[1024,256]{1,0:T(8,128)(2,1)S(1)}, bf16[1024,256]{1,0:T(8,128)(2,1)S(1)}, u32[]{:S(2)}, u32[]{:S(2)}) collective-permute-start(bf16[1024,256]{1,0:T(8,128)(2,1)S(1)} %get-tuple-element.10), channel_id=1, source_target_pairs={{0,32},{32,64},{64,96},{96,128},{128,160},{160,192},{192,224},{224... | collective-permute-start | bytes 1572872 | tf_op jit(solution)/shard_map/ppermute | solution.py:120
  50.7 12.8 %collective-permute-start.5 = (bf16[1024,256]{1,0:T(8,128)(2,1)S(1)}, bf16[1024,256]{1,0:T(8,128)(2,1)S(1)}, u32[]{:S(2)}, u32[]{:S(2)}) collective-permute-start(bf16[1024,256]{1,0:T(8,128)(2,1)S(1)} %get-tuple-element.10), channel_id=1, source_target_pairs={{0,224},{32,0},{64,32},{96,64},{128,96},{160,128},{192,160},{224,1... | collective-permute-start | bytes 1572872 | tf_op jit(solution)/shard_map/ppermute | solution.py:121
  59.7 12.1 %collective-permute-start.9 = (bf16[1024,256]{1,0:T(8,128)(2,1)S(1)}, bf16[1024,256]{1,0:T(8,128)(2,1)S(1)}, u32[]{:S(2)}, u32[]{:S(2)}) collective-permute-start(bf16[1024,256]{1,0:T(8,128)(2,1)S(1)} %collective-permute-done.8), channel_id=1, source_target_pairs={{0,32},{32,64},{64,96},{96,128},{128,160},{160,192},{192,224},{224... | collective-permute-start | bytes 1572872 | tf_op jit(solution)/shard_map/ppermute | solution.py:120
  63.4 12.1 %collective-permute-start.6 = (bf16[1024,256]{1,0:T(8,128)(2,1)S(1)}, bf16[1024,256]{1,0:T(8,128)(2,1)S(1)}, u32[]{:S(2)}, u32[]{:S(2)}) collective-permute-start(bf16[1024,256]{1,0:T(8,128)(2,1)S(1)} %collective-permute-done.5), channel_id=1, source_target_pairs={{0,224},{32,0},{64,32},{96,64},{128,96},{160,128},{192,160},{224,1... | collective-permute-start | bytes 1572872 | tf_op jit(solution)/shard_map/ppermute | solution.py:121
  71.8 12.8 %collective-permute-start.10 = (bf16[1024,256]{1,0:T(8,128)(2,1)S(1)}, bf16[1024,256]{1,0:T(8,128)(2,1)S(1)}, u32[]{:S(2)}, u32[]{:S(2)}) collective-permute-start(bf16[1024,256]{1,0:T(8,128)(2,1)S(1)} %collective-permute-done.9), channel_id=1, source_target_pairs={{0,32},{32,64},{64,96},{96,128},{128,160},{160,192},{192,224},{224... | collective-permute-start | bytes 1572872 | tf_op jit(solution)/shard_map/ppermute | solution.py:120
  75.5 13.2 %collective-permute-start.7 = (bf16[1024,256]{1,0:T(8,128)(2,1)S(1)}, bf16[1024,256]{1,0:T(8,128)(2,1)S(1)}, u32[]{:S(2)}, u32[]{:S(2)}) collective-permute-start(bf16[1024,256]{1,0:T(8,128)(2,1)S(1)} %collective-permute-done.6), channel_id=1, source_target_pairs={{0,224},{32,0},{64,32},{96,64},{128,96},{160,128},{192,160},{224,1... | collective-permute-start | bytes 1572872 | tf_op jit(solution)/shard_map/ppermute | solution.py:121
  84.6 7.2 %collective-permute-start.11 = (bf16[512,256]{1,0:T(8,128)(2,1)S(1)}, bf16[512,256]{1,0:T(8,128)(2,1)S(1)}, u32[]{:S(2)}, u32[]{:S(2)}) collective-permute-start(bf16[512,256]{1,0:T(8,128)(2,1)S(1)} %slice.104), channel_id=1, source_target_pairs={{0,32},{32,64},{64,96},{96,128},{128,160},{160,192},{192,224},{224... | collective-permute-start | bytes 786440 | tf_op jit(solution)/shard_map/ppermute | solution.py:124
  88.8 7.7 %collective-permute-start.12 = (bf16[512,256]{1,0:T(8,128)(2,1)S(1)}, bf16[512,256]{1,0:T(8,128)(2,1)S(1)}, u32[]{:S(2)}, u32[]{:S(2)}) collective-permute-start(bf16[512,256]{1,0:T(8,128)(2,1)S(1)} %slice.105), channel_id=1, source_target_pairs={{0,224},{32,0},{64,32},{96,64},{128,96},{160,128},{192,160},{224,1... | collective-permute-start | bytes 786440 | tf_op jit(solution)/shard_map/ppermute | solution.py:125
